TPU v7x, 512 devices: a whole 4x4x16 slice. The times are simulated.
512 devices in a mesh: box: 8 (over z_lo, core), panel: 64 (over y, x, z_hi).
Axes of the slice: x: 4, y: 4, z: 16 (z_hi: 4, z_lo: 4; z = z_hi * 4 + z_lo), core: 2. Of those that a mesh axis runs over, the one named last changes fastest.
Arguments:
- exterior_rows: float32 [8, 2048, 2, 128], P('box'), may hold values from -6 to 6
- exterior_block: float32 [8, 6144, 2, 128], P('box', 'panel'), may hold values from -6 to 6
- shared_block: float32 [8, 2048, 2, 2048], P('box', 'panel'), may hold values from -0.9 to 0.9
- crossing_block: float32 [8, 6144, 2, 2048], P('box', 'panel'), may hold values from -0.125 to 0.125
Outputs:
- merged_map: float32 [8, 2, 6144, 2, 128], P('box', None, 'panel')
All inputs are finite; a program needn't handle non-finite values.
Results may differ from a plain program's by a relative error of at most 0.0001.
Values sent between devices are 32-bit elements; how exact they have to be, the bound alone decides.
No kernel may reach another device: no remote copies, remote signals or barrier semaphores. Data moves between devices by JAX's collectives and lax.ppermute only.
A program may use at most 64 MiB of HBM per device.

v0:
```python
import jax
import jax.numpy as jnp
from jax import lax
from jax.sharding import PartitionSpec as P

ITERS = 3


def swapped(shard, axis, bit):
    return lax.ppermute(shard, axis, [(i, i ^ 1 << bit) for i in range(lax.axis_size(axis))])


def complex_product(left_factor, operand):
    highest = lax.Precision.HIGHEST
    real_part = jnp.dot(
        left_factor[:, 0], operand[:, 0], precision=highest, preferred_element_type=jnp.float32
    ) - jnp.dot(
        left_factor[:, 1], operand[:, 1], precision=highest, preferred_element_type=jnp.float32
    )
    imag_part = jnp.dot(
        left_factor[:, 0], operand[:, 1], precision=highest, preferred_element_type=jnp.float32
    ) + jnp.dot(
        left_factor[:, 1], operand[:, 0], precision=highest, preferred_element_type=jnp.float32
    )
    return jnp.stack([real_part, imag_part], axis=1)


def slice_product(matrix, gathered_piece):
    return complex_product(matrix, gathered_piece)


def local(exterior_rows, exterior_block, shared_block, crossing_block):
    start_rows = exterior_rows[0]
    own_exterior = exterior_block[0]
    own_shared = shared_block[0]
    own_crossing = crossing_block[0]
    width_panel = own_shared.shape[0]
    panel_index = lax.axis_index("panel")
    own_rows = lax.dynamic_slice_in_dim(start_rows, panel_index * width_panel, width_panel, 0)
    other_form, other_crossing = swapped((own_shared, own_crossing), "box", 0)

    def through_own(gathered_piece):
        return slice_product(own_shared, gathered_piece)

    def own_step(image_now):
        return own_rows + through_own(lax.all_gather(image_now, "panel", axis=0, tiled=True))

    image_panel = complex_product(other_form, start_rows)
    rows_panel = own_step(image_panel)
    for iteration in range(1, ITERS):
        image_panel = slice_product(
            other_form, lax.all_gather(rows_panel, "panel", axis=0, tiled=True)
        )
        rows_panel = own_step(image_panel)
    gathered_piece = lax.all_gather(rows_panel, "panel", axis=0, tiled=True)
    image_final = slice_product(other_form, gathered_piece)
    other_terms = slice_product(other_crossing, gathered_piece)
    own_terms = slice_product(
        own_crossing, lax.all_gather(image_final, "panel", axis=0, tiled=True)
    )
    merged = jnp.stack([own_exterior + own_terms, -other_terms], axis=0)
    return merged[None]


def solution(mesh):
    return jax.shard_map(
        local,
        mesh=mesh,
        in_specs=(
            P("box", None, None, None),
            P("box", "panel", None, None),
            P("box", "panel", None, None),
            P("box", "panel", None, None),
        ),
        out_specs=P("box", None, "panel", None, None),
        check_vma=False,
    )
```

profile of v0, /device:TPU:6, one launch (start us, length us, event | category | flops | bytes accessed | tf_op | source)
XLA Modules:
  0.0 853.3 jit_solution(4631152785487353609)
XLA Ops:
  8.5 4.0 fusion.108
  17.6 119.1 %all-gather.8.cloned.1.call-done = f32[2048,2,128]{2,0,1:T(8,128)} async-done(((f32[32,2,128]{2,0,1:T(8,128)}), f32[2048,2,128]{2,0,1:T(8,128)}) %all-gather.8.cloned.1.call-update) | async-done | bytes 2097168 | tf_op jit(solution)/shard_map/all_gather | solution.py:46
  136.8 2.1 fusion.19
  138.9 2.0 fusion.18
  143.1 110.5 %all-gather.10.cloned.1.call-done = f32[2048,2,128]{2,0,1:T(8,128)} async-done(((f32[32,2,128]{2,0,1:T(8,128)}), f32[2048,2,128]{2,0,1:T(8,128)}) %all-gather.10.cloned.1.call-update) | async-done | bytes 2097168 | tf_op jit(solution)/shard_map/all_gather | solution.py:52
  253.6 2.1 fusion.20
  255.7 2.0 fusion.21
  260.1 110.3 %all-gather.12.cloned.1.call-done = f32[2048,2,128]{2,0,1:T(8,128)} async-done(((f32[32,2,128]{2,0,1:T(8,128)}), f32[2048,2,128]{2,0,1:T(8,128)}) %all-gather.12.cloned.1.call-update) | async-done | bytes 2097168 | tf_op jit(solution)/shard_map/all_gather | solution.py:46
  370.5 2.1 fusion.23
  372.6 2.0 fusion.22
  376.8 110.5 %all-gather.14.cloned.1.call-done = f32[2048,2,128]{2,0,1:T(8,128)} async-done(((f32[32,2,128]{2,0,1:T(8,128)}), f32[2048,2,128]{2,0,1:T(8,128)}) %all-gather.14.cloned.1.call-update) | async-done | bytes 2097168 | tf_op jit(solution)/shard_map/all_gather | solution.py:52
  487.3 2.1 fusion.24
  489.4 2.0 fusion.25
  493.7 110.5 %all-gather.16.cloned.1.call-done = f32[2048,2,128]{2,0,1:T(8,128)} async-done(((f32[32,2,128]{2,0,1:T(8,128)}), f32[2048,2,128]{2,0,1:T(8,128)}) %all-gather.16.cloned.1.call-update) | async-done | bytes 2097168 | tf_op jit(solution)/shard_map/all_gather | solution.py:46
  604.2 2.1 fusion.27
  606.3 2.0 fusion.26
  610.5 110.5 %all-gather.18.cloned.1.call-done = f32[2048,2,128]{2,0,1:T(8,128)} async-done(((f32[32,2,128]{2,0,1:T(8,128)}), f32[2048,2,128]{2,0,1:T(8,128)}) %all-gather.18.cloned.1.call-update) | async-done | bytes 2097168 | tf_op jit(solution)/shard_map/all_gather | solution.py:55
  721.0 2.1 fusion.31
  723.1 2.0 fusion.33
  727.3 2.1 collective-permute-start.1
  729.4 4.5 fusion.109
  740.2 97.6 %all-gather.20.cloned.1.call-done = f32[2048,2,128]{2,0,1:T(8,128)} async-done(((f32[32,2,128]{2,0,1:T(8,128)}), f32[2048,2,128]{2,0,1:T(8,128)}) %all-gather.20.cloned.1.call-update) | async-done | bytes 2097168 | tf_op jit(solution)/shard_map/all_gather | solution.py:59
  837.8 2.6 fusion.29
  840.4 2.4 fusion.28
  (74 shorter events, 29.9 us)
Async XLA Ops:
  6.5 130.2 %all-gather.8.cloned.1.call-start = ((), (), s32[]{:S(2)}) async-start(), calls=%async_computation | async-start | bytes 2129920 | tf_op jit(solution)/shard_map/all_gather | solution.py:46
  6.5 6.0 collective-permute-start
  13.6 3.6 copy-start.8
  16.4 237.2 %all-gather.10.cloned.1.call-start = ((), (), s32[]{:S(2)}) async-start(), calls=%async_computation.1 | async-start | bytes 2129920 | tf_op jit(solution)/shard_map/all_gather | solution.py:52
  136.8 4.1 copy-start.2
  143.1 227.4 %all-gather.12.cloned.1.call-start = ((), (), s32[]{:S(2)}) async-start(), calls=%async_computation.2 | async-start | bytes 2129920 | tf_op jit(solution)/shard_map/all_gather | solution.py:46
  253.6 4.1 copy-start.4
  259.9 227.4 %all-gather.14.cloned.1.call-start = ((), (), s32[]{:S(2)}) async-start(), calls=%async_computation.3 | async-start | bytes 2129920 | tf_op jit(solution)/shard_map/all_gather | solution.py:52
  370.5 4.1 copy-start.5
  376.8 227.4 %all-gather.16.cloned.1.call-start = ((), (), s32[]{:S(2)}) async-start(), calls=%async_computation.4 | async-start | bytes 2129920 | tf_op jit(solution)/shard_map/all_gather | solution.py:46
  487.3 4.1 copy-start.6
  493.6 227.4 %all-gather.18.cloned.1.call-start = ((), (), s32[]{:S(2)}) async-start(), calls=%async_computation.5 | async-start | bytes 2129920 | tf_op jit(solution)/shard_map/all_gather | solution.py:55
  604.2 4.1 copy-start.3
  610.5 227.4 %all-gather.20.cloned.1.call-start = ((), (), s32[]{:S(2)}) async-start(), calls=%async_computation.6 | async-start | bytes 2129920 | tf_op jit(solution)/shard_map/all_gather | solution.py:59
  721.0 4.1 copy-start
  727.3 6.6 collective-permute-start.1
  740.2 102.7 %copy-start.7 = (f32[96,1,2048]{2,1,0:T(1,128)S(1)}, f32[96,1,2048]{2,1,0:T(1,128)}, u32[]{:S(2)}) copy-start(f32[96,1,2048]{2,1,0:T(1,128)} %get-tuple-element.7) | copy-start | bytes 2359300
  837.8 5.0 copy-start.1
  842.8 2.4 copy-start.9
Sparse Core Ops, SparseCore 0:
  16.5 120.1 all-gather.7
  143.2 110.4 all-gather.9
  260.0 110.4 all-gather.11
  376.9 110.4 all-gather.13
  493.7 110.4 all-gather.15
  610.6 110.4 all-gather.17
  727.4 110.4 all-gather.19
where the time goes:
time: 862 us; the launch traced here: 853 us
  waiting for transfers between devices  769 us (89%)
  matrix products  48.9 us (6%)
  between operations  14.1 us (2%)
  local copies, waits for them, and re-layouts  12.2 us (1%)
    all_gather x3, waiting for transfers between devices, own_step(): lax.all_gather(image_now, 'panel', axis=0, tiled=True)  340 us
    all_gather x2, waiting for transfers between devices, local(): lax.all_gather(rows_panel, 'panel', axis=0, tiled=True)  221 us
    all_gather x1, waiting for transfers between devices, local(): gathered_piece = lax.all_gather(rows_panel, 'panel', axis=0, tiled=True)  111 us
    all_gather x1, waiting for transfers between devices, local(): lax.all_gather(image_final, 'panel', axis=0, tiled=True)  97.6 us
  transfers between devices with their start and end apart: 9, of which 7 were waited for; matrix products, arithmetic and copies ran while one was open for 2% of the time, Pallas kernels for 0%

commit v1 on v0

--- a/solution.py
+++ b/solution.py
@@ -25,6 +25,28 @@
     return jnp.stack([real_part, imag_part], axis=1)
 
 
+def ring_stage(piece, stride):
+    count = lax.axis_size("panel")
+    digit = (lax.axis_index("panel") // stride) % 4
+    pieces = [piece]
+    for shift in (1, 2, 3):
+        pairs = []
+        for source in range(count):
+            own = (source // stride) % 4
+            pairs.append((source, source + ((own + shift) % 4 - own) * stride))
+        pieces.append(lax.ppermute(piece, "panel", pairs))
+    stacked = jnp.stack(pieces, 0)
+    order = (digit - jnp.arange(4)) % 4
+    out = jnp.take(stacked, order, axis=0)
+    return out.reshape((4 * piece.shape[0],) + piece.shape[1:])
+
+
+def panel_gather(piece):
+    for stride in (1, 4, 16):
+        piece = ring_stage(piece, stride)
+    return piece
+
+
 def slice_product(matrix, gathered_piece):
     return complex_product(matrix, gathered_piece)
 
@@ -43,20 +65,20 @@
         return slice_product(own_shared, gathered_piece)
 
     def own_step(image_now):
-        return own_rows + through_own(lax.all_gather(image_now, "panel", axis=0, tiled=True))
+        return own_rows + through_own(panel_gather(image_now))
 
     image_panel = complex_product(other_form, start_rows)
     rows_panel = own_step(image_panel)
     for iteration in range(1, ITERS):
         image_panel = slice_product(
-            other_form, lax.all_gather(rows_panel, "panel", axis=0, tiled=True)
+            other_form, panel_gather(rows_panel)
         )
         rows_panel = own_step(image_panel)
-    gathered_piece = lax.all_gather(rows_panel, "panel", axis=0, tiled=True)
+    gathered_piece = panel_gather(rows_panel)
     image_final = slice_product(other_form, gathered_piece)
     other_terms = slice_product(other_crossing, gathered_piece)
     own_terms = slice_product(
-        own_crossing, lax.all_gather(image_final, "panel", axis=0, tiled=True)
+        own_crossing, panel_gather(image_final)
     )
     merged = jnp.stack([own_exterior + own_terms, -other_terms], axis=0)
     return merged[None]

time: 862 us -> 551 us (0.64)
  the two profiles are of different devices: /device:TPU:6 before, /device:TPU:33 now
where the time goes in v1:
time: 551 us; the launch traced here: 541 us
  starting transfers between devices  241 us (44%)
  waiting for transfers between devices  210 us (38%)
  local copies, waits for them, and re-layouts  39.8 us (7%)
  matrix products  31.9 us (6%)
  other arithmetic  16.6 us (3%)
    ppermute x63, starting transfers between devices, ring_stage(): pieces.append(lax.ppermute(piece, 'panel', pairs))  234 us
    ppermute x63, waiting for transfers between devices, ring_stage(): pieces.append(lax.ppermute(piece, 'panel', pairs))  210 us
    gather x21, local copies, waits for them, and re-layouts, ring_stage(): out = jnp.take(stacked, order, axis=0)  22.8 us
    select_n x24, other arithmetic, ring_stage(): out = jnp.take(stacked, order, axis=0)  15.1 us
  transfers between devices with their start and end apart: 65, of which 44 were waited for; matrix products, arithmetic and copies ran while one was open for 5% of the time, Pallas kernels for 0%

profile of v1, /device:TPU:33, one launch (start us, length us, event | category | flops | bytes accessed | tf_op | source)
XLA Modules:
  0.0 541.0 jit_solution(3892711112204247810)
XLA Ops:
  10.1 11.6 %collective-permute-start.3 = (f32[32,2,128]{2,0,1:T(8,128)S(1)}, f32[32,2,128]{2,0,1:T(8,128)S(1)}, u32[]{:S(2)}, u32[]{:S(2)}) collective-permute-start(f32[32,2,128]{2,0,1:T(8,128)S(1)} %get-tuple-element.25), channel_id=1, source_target_pairs={{0,3},{1,0},{2,1},{3,2},{4,7},{5,4},{6,5},{7,6},{8,11},{9,8},{10,9... | collective-permute-start | bytes 98312 | tf_op jit(solution)/shard_map/ppermute | solution.py:37
  21.7 4.9 collective-permute-start.2
  26.6 7.3 %collective-permute-start.1 = (f32[32,2,128]{2,0,1:T(8,128)S(1)}, f32[32,2,128]{2,0,1:T(8,128)S(1)}, u32[]{:S(2)}, u32[]{:S(2)}) collective-permute-start(f32[32,2,128]{2,0,1:T(8,128)S(1)} %get-tuple-element.25), channel_id=1, source_target_pairs={{0,1},{1,2},{2,3},{3,0},{4,5},{5,6},{6,7},{7,4},{8,9},{9,10},{10,1... | collective-permute-start | bytes 98312 | tf_op jit(solution)/shard_map/ppermute | solution.py:37
  73.1 14.1 %collective-permute-done.7 = f32[512,2,128]{2,0,1:T(8,128)S(1)} collective-permute-done((f32[512,2,128]{2,0,1:T(8,128)S(1)}, f32[512,2,128]{2,0,1:T(8,128)S(1)}, u32[]{:S(2)}, u32[]{:S(2)}) %collective-permute-start.7) | collective-permute-done | bytes 524320 | tf_op jit(solution)/shard_map/ppermute | solution.py:37
  97.3 10.9 %collective-permute-start.11 = (f32[32,2,128]{2,0,1:T(8,128)S(1)}, f32[32,2,128]{2,0,1:T(8,128)S(1)}, u32[]{:S(2)}, u32[]{:S(2)}) collective-permute-start(f32[32,2,128]{2,0,1:T(8,128)S(1)} %maximum_add_fusion.2), channel_id=1, source_target_pairs={{0,2},{1,3},{2,0},{3,1},{4,6},{5,7},{6,4},{7,5},{8,10},{9,11},{10,... | collective-permute-start | bytes 98312 | tf_op jit(solution)/shard_map/ppermute | solution.py:37
  110.8 6.3 %collective-permute-done.10 = f32[32,2,128]{2,0,1:T(8,128)S(1)} collective-permute-done((f32[32,2,128]{2,0,1:T(8,128)S(1)}, f32[32,2,128]{2,0,1:T(8,128)S(1)}, u32[]{:S(2)}, u32[]{:S(2)}) %collective-permute-start.10) | collective-permute-done | bytes 32800 | tf_op jit(solution)/shard_map/ppermute | solution.py:37
  139.4 5.7 %collective-permute-done.18 = f32[512,2,128]{2,0,1:T(8,128)S(1)} collective-permute-done((f32[512,2,128]{2,0,1:T(8,128)S(1)}, f32[512,2,128]{2,0,1:T(8,128)S(1)}, u32[]{:S(2)}, u32[]{:S(2)}) %collective-permute-start.18) | collective-permute-done | bytes 524320 | tf_op jit(solution)/shard_map/ppermute | solution.py:37
  148.1 14.3 %collective-permute-done.16 = f32[512,2,128]{2,0,1:T(8,128)S(1)} collective-permute-done((f32[512,2,128]{2,0,1:T(8,128)S(1)}, f32[512,2,128]{2,0,1:T(8,128)S(1)}, u32[]{:S(2)}, u32[]{:S(2)}) %collective-permute-start.16) | collective-permute-done | bytes 524320 | tf_op jit(solution)/shard_map/ppermute | solution.py:37
  172.0 6.6 %collective-permute-start.20 = (f32[32,2,128]{2,0,1:T(8,128)S(1)}, f32[32,2,128]{2,0,1:T(8,128)S(1)}, u32[]{:S(2)}, u32[]{:S(2)}) collective-permute-start(f32[32,2,128]{2,0,1:T(8,128)S(1)} %get-tuple-element.23), channel_id=1, source_target_pairs={{0,2},{1,3},{2,0},{3,1},{4,6},{5,7},{6,4},{7,5},{8,10},{9,11},{10,... | collective-permute-start | bytes 98312 | tf_op jit(solution)/shard_map/ppermute | solution.py:37
  178.6 4.8 collective-permute-start.19
  199.0 5.5 %collective-permute-done.22 = f32[128,2,128]{2,0,1:T(8,128)S(1)} collective-permute-done((f32[128,2,128]{2,0,1:T(8,128)S(1)}, f32[128,2,128]{2,0,1:T(8,128)S(1)}, u32[]{:S(2)}, u32[]{:S(2)}) %collective-permute-start.22) | collective-permute-done | bytes 131104 | tf_op jit(solution)/shard_map/ppermute | solution.py:37
  212.5 6.7 %collective-permute-done.27 = f32[512,2,128]{2,0,1:T(8,128)S(1)} collective-permute-done((f32[512,2,128]{2,0,1:T(8,128)S(1)}, f32[512,2,128]{2,0,1:T(8,128)S(1)}, u32[]{:S(2)}, u32[]{:S(2)}) %collective-permute-start.27) | collective-permute-done | bytes 524320 | tf_op jit(solution)/shard_map/ppermute | solution.py:37
  222.7 13.0 %collective-permute-done.25 = f32[512,2,128]{2,0,1:T(8,128)S(1)} collective-permute-done((f32[512,2,128]{2,0,1:T(8,128)S(1)}, f32[512,2,128]{2,0,1:T(8,128)S(1)}, u32[]{:S(2)}, u32[]{:S(2)}) %collective-permute-start.25) | collective-permute-done | bytes 524320 | tf_op jit(solution)/shard_map/ppermute | solution.py:37
  289.6 15.4 %collective-permute-done.34 = f32[512,2,128]{2,0,1:T(8,128)S(1)} collective-permute-done((f32[512,2,128]{2,0,1:T(8,128)S(1)}, f32[512,2,128]{2,0,1:T(8,128)S(1)}, u32[]{:S(2)}, u32[]{:S(2)}) %collective-permute-start.34) | collective-permute-done | bytes 524320 | tf_op jit(solution)/shard_map/ppermute | solution.py:37
  312.1 8.4 %collective-permute-start.39 = (f32[32,2,128]{2,0,1:T(8,128)S(1)}, f32[32,2,128]{2,0,1:T(8,128)S(1)}, u32[]{:S(2)}, u32[]{:S(2)}) collective-permute-start(f32[32,2,128]{2,0,1:T(8,128)S(1)} %get-tuple-element.21), channel_id=1, source_target_pairs={{0,3},{1,0},{2,1},{3,2},{4,7},{5,4},{6,5},{7,6},{8,11},{9,8},{10,9... | collective-permute-start | bytes 98312 | tf_op jit(solution)/shard_map/ppermute | solution.py:37
  320.5 6.0 %collective-permute-start.38 = (f32[32,2,128]{2,0,1:T(8,128)S(1)}, f32[32,2,128]{2,0,1:T(8,128)S(1)}, u32[]{:S(2)}, u32[]{:S(2)}) collective-permute-start(f32[32,2,128]{2,0,1:T(8,128)S(1)} %get-tuple-element.21), channel_id=1, source_target_pairs={{0,2},{1,3},{2,0},{3,1},{4,6},{5,7},{6,4},{7,5},{8,10},{9,11},{10,... | collective-permute-start | bytes 98312 | tf_op jit(solution)/shard_map/ppermute | solution.py:37
  326.5 5.5 %collective-permute-start.37 = (f32[32,2,128]{2,0,1:T(8,128)S(1)}, f32[32,2,128]{2,0,1:T(8,128)S(1)}, u32[]{:S(2)}, u32[]{:S(2)}) collective-permute-start(f32[32,2,128]{2,0,1:T(8,128)S(1)} %get-tuple-element.21), channel_id=1, source_target_pairs={{0,1},{1,2},{2,3},{3,0},{4,5},{5,6},{6,7},{7,4},{8,9},{9,10},{10,1... | collective-permute-start | bytes 98312 | tf_op jit(solution)/shard_map/ppermute | solution.py:37
  366.7 14.4 %collective-permute-done.43 = f32[512,2,128]{2,0,1:T(8,128)S(1)} collective-permute-done((f32[512,2,128]{2,0,1:T(8,128)S(1)}, f32[512,2,128]{2,0,1:T(8,128)S(1)}, u32[]{:S(2)}, u32[]{:S(2)}) %collective-permute-start.43) | collective-permute-done | bytes 524320 | tf_op jit(solution)/shard_map/ppermute | solution.py:37
  391.9 7.9 %collective-permute-start.47 = (f32[32,2,128]{2,0,1:T(8,128)S(1)}, f32[32,2,128]{2,0,1:T(8,128)S(1)}, u32[]{:S(2)}, u32[]{:S(2)}) collective-permute-start(f32[32,2,128]{2,0,1:T(8,128)S(1)} %maximum_add_fusion.6), channel_id=1, source_target_pairs={{0,2},{1,3},{2,0},{3,1},{4,6},{5,7},{6,4},{7,5},{8,10},{9,11},{10,... | collective-permute-start | bytes 98312 | tf_op jit(solution)/shard_map/ppermute | solution.py:37
  399.8 5.2 collective-permute-start.46
  438.8 15.1 %collective-permute-done.52 = f32[512,2,128]{2,0,1:T(8,128)S(1)} collective-permute-done((f32[512,2,128]{2,0,1:T(8,128)S(1)}, f32[512,2,128]{2,0,1:T(8,128)S(1)}, u32[]{:S(2)}, u32[]{:S(2)}) %collective-permute-start.52) | collective-permute-done | bytes 524320 | tf_op jit(solution)/shard_map/ppermute | solution.py:37
  461.0 5.1 collective-permute-start.57
  466.2 8.1 %collective-permute-start.56 = (f32[32,2,128]{2,0,1:T(8,128)S(1)}, f32[32,2,128]{2,0,1:T(8,128)S(1)}, u32[]{:S(2)}, u32[]{:S(2)}) collective-permute-start(f32[32,2,128]{2,0,1:T(8,128)S(1)} %get-tuple-element.19), channel_id=1, source_target_pairs={{0,2},{1,3},{2,0},{3,1},{4,6},{5,7},{6,4},{7,5},{8,10},{9,11},{10,... | collective-permute-start | bytes 98312 | tf_op jit(solution)/shard_map/ppermute | solution.py:37
  516.9 13.8 %collective-permute-done.61 = f32[512,2,128]{2,0,1:T(8,128)S(1)} collective-permute-done((f32[512,2,128]{2,0,1:T(8,128)S(1)}, f32[512,2,128]{2,0,1:T(8,128)S(1)}, u32[]{:S(2)}, u32[]{:S(2)}) %collective-permute-start.61) | collective-permute-done | bytes 524320 | tf_op jit(solution)/shard_map/ppermute | solution.py:37
  (273 shorter events, 322.5 us)
Async XLA Ops:
  10.1 23.8 %collective-permute-start.3 = (f32[32,2,128]{2,0,1:T(8,128)S(1)}, f32[32,2,128]{2,0,1:T(8,128)S(1)}, u32[]{:S(2)}, u32[]{:S(2)}) collective-permute-start(f32[32,2,128]{2,0,1:T(8,128)S(1)} %get-tuple-element.25), channel_id=1, source_target_pairs={{0,3},{1,0},{2,1},{3,2},{4,7},{5,4},{6,5},{7,6},{8,11},{9,8},{10,9... | collective-permute-start | bytes 98312 | tf_op jit(solution)/shard_map/ppermute | solution.py:37
  54.0 14.7 %collective-permute-start.9 = (f32[512,2,128]{2,0,1:T(8,128)S(1)}, f32[512,2,128]{2,0,1:T(8,128)S(1)}, u32[]{:S(2)}, u32[]{:S(2)}) collective-permute-start(f32[512,2,128]{2,0,1:T(8,128)S(1)} %bitcast.380), channel_id=1, source_target_pairs={{0,48},{1,49},{2,50},{3,51},{4,52},{5,53},{6,54},{7,55},{8,56},{9,... | collective-permute-start | bytes 1572872 | tf_op jit(solution)/shard_map/ppermute | solution.py:37
  58.7 14.4 %collective-permute-start.8 = (f32[512,2,128]{2,0,1:T(8,128)S(1)}, f32[512,2,128]{2,0,1:T(8,128)S(1)}, u32[]{:S(2)}, u32[]{:S(2)}) collective-permute-start(f32[512,2,128]{2,0,1:T(8,128)S(1)} %bitcast.381), channel_id=1, source_target_pairs={{0,32},{1,33},{2,34},{3,35},{4,36},{5,37},{6,38},{7,39},{8,40},{9,... | collective-permute-start | bytes 1572872 | tf_op jit(solution)/shard_map/ppermute | solution.py:37
  61.0 26.2 %collective-permute-start.7 = (f32[512,2,128]{2,0,1:T(8,128)S(1)}, f32[512,2,128]{2,0,1:T(8,128)S(1)}, u32[]{:S(2)}, u32[]{:S(2)}) collective-permute-start(f32[512,2,128]{2,0,1:T(8,128)S(1)} %bitcast.382), channel_id=1, source_target_pairs={{0,16},{1,17},{2,18},{3,19},{4,20},{5,21},{6,22},{7,23},{8,24},{9,... | collective-permute-start | bytes 1572872 | tf_op jit(solution)/shard_map/ppermute | solution.py:37
  94.3 16.5 %collective-permute-start.12 = (f32[32,2,128]{2,0,1:T(8,128)S(1)}, f32[32,2,128]{2,0,1:T(8,128)S(1)}, u32[]{:S(2)}, u32[]{:S(2)}) collective-permute-start(f32[32,2,128]{2,0,1:T(8,128)S(1)} %maximum_add_fusion.2), channel_id=1, source_target_pairs={{0,3},{1,0},{2,1},{3,2},{4,7},{5,4},{6,5},{7,6},{8,11},{9,8},{10,9... | collective-permute-start | bytes 98312 | tf_op jit(solution)/shard_map/ppermute | solution.py:37
  133.9 14.2 %collective-permute-start.17 = (f32[512,2,128]{2,0,1:T(8,128)S(1)}, f32[512,2,128]{2,0,1:T(8,128)S(1)}, u32[]{:S(2)}, u32[]{:S(2)}) collective-permute-start(f32[512,2,128]{2,0,1:T(8,128)S(1)} %bitcast.389), channel_id=1, source_target_pairs={{0,32},{1,33},{2,34},{3,35},{4,36},{5,37},{6,38},{7,39},{8,40},{9,... | collective-permute-start | bytes 1572872 | tf_op jit(solution)/shard_map/ppermute | solution.py:37
  136.2 26.2 %collective-permute-start.16 = (f32[512,2,128]{2,0,1:T(8,128)S(1)}, f32[512,2,128]{2,0,1:T(8,128)S(1)}, u32[]{:S(2)}, u32[]{:S(2)}) collective-permute-start(f32[512,2,128]{2,0,1:T(8,128)S(1)} %bitcast.390), channel_id=1, source_target_pairs={{0,16},{1,17},{2,18},{3,19},{4,20},{5,21},{6,22},{7,23},{8,24},{9,... | collective-permute-start | bytes 1572872 | tf_op jit(solution)/shard_map/ppermute | solution.py:37
  169.5 13.9 %collective-permute-start.21 = (f32[32,2,128]{2,0,1:T(8,128)S(1)}, f32[32,2,128]{2,0,1:T(8,128)S(1)}, u32[]{:S(2)}, u32[]{:S(2)}) collective-permute-start(f32[32,2,128]{2,0,1:T(8,128)S(1)} %get-tuple-element.23), channel_id=1, source_target_pairs={{0,3},{1,0},{2,1},{3,2},{4,7},{5,4},{6,5},{7,6},{8,11},{9,8},{10,9... | collective-permute-start | bytes 98312 | tf_op jit(solution)/shard_map/ppermute | solution.py:37
  205.3 13.9 %collective-permute-start.27 = (f32[512,2,128]{2,0,1:T(8,128)S(1)}, f32[512,2,128]{2,0,1:T(8,128)S(1)}, u32[]{:S(2)}, u32[]{:S(2)}) collective-permute-start(f32[512,2,128]{2,0,1:T(8,128)S(1)} %bitcast.392), channel_id=1, source_target_pairs={{0,48},{1,49},{2,50},{3,51},{4,52},{5,53},{6,54},{7,55},{8,56},{9,... | collective-permute-start | bytes 1572872 | tf_op jit(solution)/shard_map/ppermute | solution.py:37
  207.2 15.5 %collective-permute-start.26 = (f32[512,2,128]{2,0,1:T(8,128)S(1)}, f32[512,2,128]{2,0,1:T(8,128)S(1)}, u32[]{:S(2)}, u32[]{:S(2)}) collective-permute-start(f32[512,2,128]{2,0,1:T(8,128)S(1)} %bitcast.393), channel_id=1, source_target_pairs={{0,32},{1,33},{2,34},{3,35},{4,36},{5,37},{6,38},{7,39},{8,40},{9,... | collective-permute-start | bytes 1572872 | tf_op jit(solution)/shard_map/ppermute | solution.py:37
  209.6 26.1 %collective-permute-start.25 = (f32[512,2,128]{2,0,1:T(8,128)S(1)}, f32[512,2,128]{2,0,1:T(8,128)S(1)}, u32[]{:S(2)}, u32[]{:S(2)}) collective-permute-start(f32[512,2,128]{2,0,1:T(8,128)S(1)} %bitcast.394), channel_id=1, source_target_pairs={{0,16},{1,17},{2,18},{3,19},{4,20},{5,21},{6,22},{7,23},{8,24},{9,... | collective-permute-start | bytes 1572872 | tf_op jit(solution)/shard_map/ppermute | solution.py:37
  242.8 13.8 %collective-permute-start.30 = (f32[32,2,128]{2,0,1:T(8,128)S(1)}, f32[32,2,128]{2,0,1:T(8,128)S(1)}, u32[]{:S(2)}, u32[]{:S(2)}) collective-permute-start(f32[32,2,128]{2,0,1:T(8,128)S(1)} %maximum_add_fusion.4), channel_id=1, source_target_pairs={{0,3},{1,0},{2,1},{3,2},{4,7},{5,4},{6,5},{7,6},{8,11},{9,8},{10,9... | collective-permute-start | bytes 98312 | tf_op jit(solution)/shard_map/ppermute | solution.py:37
  280.9 24.0 %collective-permute-start.34 = (f32[512,2,128]{2,0,1:T(8,128)S(1)}, f32[512,2,128]{2,0,1:T(8,128)S(1)}, u32[]{:S(2)}, u32[]{:S(2)}) collective-permute-start(f32[512,2,128]{2,0,1:T(8,128)S(1)} %bitcast.398), channel_id=1, source_target_pairs={{0,16},{1,17},{2,18},{3,19},{4,20},{5,21},{6,22},{7,23},{8,24},{9,... | collective-permute-start | bytes 1572872 | tf_op jit(solution)/shard_map/ppermute | solution.py:37
  312.1 20.0 %collective-permute-start.39 = (f32[32,2,128]{2,0,1:T(8,128)S(1)}, f32[32,2,128]{2,0,1:T(8,128)S(1)}, u32[]{:S(2)}, u32[]{:S(2)}) collective-permute-start(f32[32,2,128]{2,0,1:T(8,128)S(1)} %get-tuple-element.21), channel_id=1, source_target_pairs={{0,3},{1,0},{2,1},{3,2},{4,7},{5,4},{6,5},{7,6},{8,11},{9,8},{10,9... | collective-permute-start | bytes 98312 | tf_op jit(solution)/shard_map/ppermute | solution.py:37
  350.6 13.7 %collective-permute-start.45 = (f32[512,2,128]{2,0,1:T(8,128)S(1)}, f32[512,2,128]{2,0,1:T(8,128)S(1)}, u32[]{:S(2)}, u32[]{:S(2)}) collective-permute-start(f32[512,2,128]{2,0,1:T(8,128)S(1)} %bitcast.384), channel_id=1, source_target_pairs={{0,48},{1,49},{2,50},{3,51},{4,52},{5,53},{6,54},{7,55},{8,56},{9,... | collective-permute-start | bytes 1572872 | tf_op jit(solution)/shard_map/ppermute | solution.py:37
  352.6 14.1 %collective-permute-start.44 = (f32[512,2,128]{2,0,1:T(8,128)S(1)}, f32[512,2,128]{2,0,1:T(8,128)S(1)}, u32[]{:S(2)}, u32[]{:S(2)}) collective-permute-start(f32[512,2,128]{2,0,1:T(8,128)S(1)} %bitcast.385), channel_id=1, source_target_pairs={{0,32},{1,33},{2,34},{3,35},{4,36},{5,37},{6,38},{7,39},{8,40},{9,... | collective-permute-start | bytes 1572872 | tf_op jit(solution)/shard_map/ppermute | solution.py:37
  354.9 26.1 %collective-permute-start.43 = (f32[512,2,128]{2,0,1:T(8,128)S(1)}, f32[512,2,128]{2,0,1:T(8,128)S(1)}, u32[]{:S(2)}, u32[]{:S(2)}) collective-permute-start(f32[512,2,128]{2,0,1:T(8,128)S(1)} %bitcast.386), channel_id=1, source_target_pairs={{0,16},{1,17},{2,18},{3,19},{4,20},{5,21},{6,22},{7,23},{8,24},{9,... | collective-permute-start | bytes 1572872 | tf_op jit(solution)/shard_map/ppermute | solution.py:37
  357.9 73.2 %collective-permute-start.64 = (f32[96,2,2048]{2,1,0:T(2,128)}, f32[96,2,2048]{2,1,0:T(2,128)}, u32[]{:S(2)}, u32[]{:S(2)}) collective-permute-start(f32[96,2,2048]{2,1,0:T(2,128)} %bitcast.152), channel_id=1, source_target_pairs={{0,64},{64,0},{128,192},{192,128},{256,320},{320,256},{384,448},{4... | collective-permute-start | bytes 4718600 | tf_op jit(solution)/shard_map/ppermute | solution.py:10
  388.2 16.8 %collective-permute-start.48 = (f32[32,2,128]{2,0,1:T(8,128)S(1)}, f32[32,2,128]{2,0,1:T(8,128)S(1)}, u32[]{:S(2)}, u32[]{:S(2)}) collective-permute-start(f32[32,2,128]{2,0,1:T(8,128)S(1)} %maximum_add_fusion.6), channel_id=1, source_target_pairs={{0,3},{1,0},{2,1},{3,2},{4,7},{5,4},{6,5},{7,6},{8,11},{9,8},{10,9... | collective-permute-start | bytes 98312 | tf_op jit(solution)/shard_map/ppermute | solution.py:37
  427.6 26.2 %collective-permute-start.52 = (f32[512,2,128]{2,0,1:T(8,128)S(1)}, f32[512,2,128]{2,0,1:T(8,128)S(1)}, u32[]{:S(2)}, u32[]{:S(2)}) collective-permute-start(f32[512,2,128]{2,0,1:T(8,128)S(1)} %bitcast.378), channel_id=1, source_target_pairs={{0,16},{1,17},{2,18},{3,19},{4,20},{5,21},{6,22},{7,23},{8,24},{9,... | collective-permute-start | bytes 1572872 | tf_op jit(solution)/shard_map/ppermute | solution.py:37
  461.0 16.7 %collective-permute-start.57 = (f32[32,2,128]{2,0,1:T(8,128)S(1)}, f32[32,2,128]{2,0,1:T(8,128)S(1)}, u32[]{:S(2)}, u32[]{:S(2)}) collective-permute-start(f32[32,2,128]{2,0,1:T(8,128)S(1)} %get-tuple-element.19), channel_id=1, source_target_pairs={{0,3},{1,0},{2,1},{3,2},{4,7},{5,4},{6,5},{7,6},{8,11},{9,8},{10,9... | collective-permute-start | bytes 98312 | tf_op jit(solution)/shard_map/ppermute | solution.py:37
  500.3 13.6 %collective-permute-start.63 = (f32[512,2,128]{2,0,1:T(8,128)S(1)}, f32[512,2,128]{2,0,1:T(8,128)S(1)}, u32[]{:S(2)}, u32[]{:S(2)}) collective-permute-start(f32[512,2,128]{2,0,1:T(8,128)S(1)} %bitcast.372), channel_id=1, source_target_pairs={{0,48},{1,49},{2,50},{3,51},{4,52},{5,53},{6,54},{7,55},{8,56},{9,... | collective-permute-start | bytes 1572872 | tf_op jit(solution)/shard_map/ppermute | solution.py:37
  502.3 14.6 %collective-permute-start.62 = (f32[512,2,128]{2,0,1:T(8,128)S(1)}, f32[512,2,128]{2,0,1:T(8,128)S(1)}, u32[]{:S(2)}, u32[]{:S(2)}) collective-permute-start(f32[512,2,128]{2,0,1:T(8,128)S(1)} %bitcast.373), channel_id=1, source_target_pairs={{0,32},{1,33},{2,34},{3,35},{4,36},{5,37},{6,38},{7,39},{8,40},{9,... | collective-permute-start | bytes 1572872 | tf_op jit(solution)/shard_map/ppermute | solution.py:37
  504.9 25.8 %collective-permute-start.61 = (f32[512,2,128]{2,0,1:T(8,128)S(1)}, f32[512,2,128]{2,0,1:T(8,128)S(1)}, u32[]{:S(2)}, u32[]{:S(2)}) collective-permute-start(f32[512,2,128]{2,0,1:T(8,128)S(1)} %bitcast.374), channel_id=1, source_target_pairs={{0,16},{1,17},{2,18},{3,19},{4,20},{5,21},{6,22},{7,23},{8,24},{9,... | collective-permute-start | bytes 1572872 | tf_op jit(solution)/shard_map/ppermute | solution.py:37
  (50 other events, 1302.7 us)

commit v2 on v0

--- a/solution.py
+++ b/solution.py
@@ -25,6 +25,44 @@
     return jnp.stack([real_part, imag_part], axis=1)
 
 
+def shifted_along(piece, stride, shift):
+    pairs = []
+    for source in range(lax.axis_size("panel")):
+        own = (source // stride) % 4
+        pairs.append((source, source + ((own + shift) % 4 - own) * stride))
+    return lax.ppermute(piece, "panel", pairs)
+
+
+def direct_stage(blocks, stride):
+    return jnp.stack(
+        [blocks, shifted_along(blocks, stride, 3), shifted_along(blocks, stride, 2),
+         shifted_along(blocks, stride, 1)], 0)
+
+
+def relay_stage(blocks, stride):
+    from_below = shifted_along(blocks, stride, 1)
+    from_above = shifted_along(blocks, stride, 3)
+    half = blocks.shape[0] // 2
+    opposite = jnp.concatenate(
+        [shifted_along(from_below[:half], stride, 1), shifted_along(from_above[half:], stride, 3)], 0)
+    return jnp.stack([blocks, from_above, opposite, from_below], 0)
+
+
+def panel_gather(piece):
+    blocks = direct_stage(piece[None], 1)
+    blocks = relay_stage(blocks, 4)
+    blocks = relay_stage(blocks, 16)
+    blocks = blocks.reshape((64,) + piece.shape)
+    me = lax.axis_index("panel")
+    target = jnp.arange(64)
+    slot = jnp.zeros((64,), jnp.int32)
+    for stride in (16, 4, 1):
+        offset = (target // stride % 4 - me // stride % 4) % 4
+        slot = slot + offset * stride
+    out = jnp.take(blocks, slot, axis=0)
+    return out.reshape((64 * piece.shape[0],) + piece.shape[1:])
+
+
 def slice_product(matrix, gathered_piece):
     return complex_product(matrix, gathered_piece)
 
@@ -43,20 +81,20 @@
         return slice_product(own_shared, gathered_piece)
 
     def own_step(image_now):
-        return own_rows + through_own(lax.all_gather(image_now, "panel", axis=0, tiled=True))
+        return own_rows + through_own(panel_gather(image_now))
 
     image_panel = complex_product(other_form, start_rows)
     rows_panel = own_step(image_panel)
     for iteration in range(1, ITERS):
         image_panel = slice_product(
-            other_form, lax.all_gather(rows_panel, "panel", axis=0, tiled=True)
+            other_form, panel_gather(rows_panel)
         )
         rows_panel = own_step(image_panel)
-    gathered_piece = lax.all_gather(rows_panel, "panel", axis=0, tiled=True)
+    gathered_piece = panel_gather(rows_panel)
     image_final = slice_product(other_form, gathered_piece)
     other_terms = slice_product(other_crossing, gathered_piece)
     own_terms = slice_product(
-        own_crossing, lax.all_gather(image_final, "panel", axis=0, tiled=True)
+        own_crossing, panel_gather(image_final)
     )
     merged = jnp.stack([own_exterior + own_terms, -other_terms], axis=0)
     return merged[None]

time: 862 us -> 551 us (0.64)
  waiting for transfers between devices: 769 us -> 137 us
  starting transfers between devices: 4.47 us -> 322 us
  local copies, waits for them, and re-layouts: 12.2 us -> 30.3 us
  matrix products: 48.9 us -> 31 us
  other arithmetic: 4.38 us -> 18 us
  between operations: 14.1 us -> 1.86 us
    all_gather x7 -> x0, waiting for transfers between devices: 769 us -> none  [the longest x3 340 us: own_step(): lax.all_gather(image_now, 'panel', axis=0, tiled=True)]
    ppermute x0 -> x77, starting transfers between devices: none -> 318 us  [shifted_along(): return lax.ppermute(piece, 'panel', pairs)]
    ppermute x0 -> x77, waiting for transfers between devices: none -> 137 us  [shifted_along(): return lax.ppermute(piece, 'panel', pairs)]
    gather x0 -> x7, local copies, waits for them, and re-layouts: none -> 14 us  [panel_gather(): out = jnp.take(blocks, slot, axis=0)]
    select_n x0 -> x7, other arithmetic: none -> 12.6 us  [panel_gather(): out = jnp.take(blocks, slot, axis=0)]
  transfers between devices with their start and end apart: 9 -> 79, of which waited for: 7 -> 51; matrix products, arithmetic and copies ran while one was open for 2% -> 5% of each run, Pallas kernels for 0% -> 0%
where the time goes in v2:
time: 551 us; the launch traced here: 540 us
  starting transfers between devices  322 us (58%)
  waiting for transfers between devices  137 us (25%)
  matrix products  31 us (6%)
  local copies, waits for them, and re-layouts  30.3 us (5%)
  other arithmetic  18 us (3%)
    ppermute x77, starting transfers between devices, shifted_along(): return lax.ppermute(piece, 'panel', pairs)  318 us
    ppermute x77, waiting for transfers between devices, shifted_along(): return lax.ppermute(piece, 'panel', pairs)  137 us
    gather x7, local copies, waits for them, and re-layouts, panel_gather(): out = jnp.take(blocks, slot, axis=0)  14 us
    select_n x7, other arithmetic, panel_gather(): out = jnp.take(blocks, slot, axis=0)  12.6 us
  transfers between devices with their start and end apart: 79, of which 51 were waited for; matrix products, arithmetic and copies ran while one was open for 5% of the time, Pallas kernels for 0%

profile of v2, /device:TPU:6, one launch (start us, length us, event | category | flops | bytes accessed | tf_op | source)
XLA Modules:
  0.0 540.2 jit_solution(10750399801220685093)
XLA Ops:
  9.3 9.1 %collective-permute-start.3 = (f32[1,32,2,128]{3,1,2,0:T(8,128)S(1)}, f32[1,32,2,128]{3,1,2,0:T(8,128)S(1)}, u32[]{:S(2)}, u32[]{:S(2)}) collective-permute-start(f32[1,32,2,128]{3,1,2,0:T(8,128)S(1)} %get-tuple-element.67), channel_id=1, source_target_pairs={{0,1},{1,2},{2,3},{3,0},{4,5},{5,6},{6,7},{7,4},{8,9},{9,10},{10,1... | collective-permute-start | bytes 98312 | tf_op jit(solution)/shard_map/ppermute | solution.py:33
  18.4 10.9 %collective-permute-start.2 = (f32[1,32,2,128]{3,1,2,0:T(8,128)S(1)}, f32[1,32,2,128]{3,1,2,0:T(8,128)S(1)}, u32[]{:S(2)}, u32[]{:S(2)}) collective-permute-start(f32[1,32,2,128]{3,1,2,0:T(8,128)S(1)} %get-tuple-element.67), channel_id=1, source_target_pairs={{0,2},{1,3},{2,0},{3,1},{4,6},{5,7},{6,4},{7,5},{8,10},{9,11},{10,... | collective-permute-start | bytes 98312 | tf_op jit(solution)/shard_map/ppermute | solution.py:33
  29.3 5.5 %collective-permute-start.1 = (f32[1,32,2,128]{3,1,2,0:T(8,128)S(1)}, f32[1,32,2,128]{3,1,2,0:T(8,128)S(1)}, u32[]{:S(2)}, u32[]{:S(2)}) collective-permute-start(f32[1,32,2,128]{3,1,2,0:T(8,128)S(1)} %get-tuple-element.67), channel_id=1, source_target_pairs={{0,3},{1,0},{2,1},{3,2},{4,7},{5,4},{6,5},{7,6},{8,11},{9,8},{10,9... | collective-permute-start | bytes 98312 | tf_op jit(solution)/shard_map/ppermute | solution.py:33
  70.4 5.5 %collective-permute-start.11 = (f32[2,4,1,32,2,128]{5,3,4,1,0,2:T(8,128)S(1)}, f32[2,4,1,32,2,128]{5,3,4,1,0,2:T(8,128)S(1)}, u32[]{:S(2)}, u32[]{:S(2)}) collective-permute-start(f32[2,4,1,32,2,128]{5,3,4,1,0,2:T(8,128)S(1)} %slice.277), channel_id=1, source_target_pairs={{0,48},{1,49},{2,50},{3,51},{4,52},{5,53},{6,54},{7,55},{8,56},{9,... | collective-permute-start | bytes 786440 | tf_op jit(solution)/shard_map/ppermute | solution.py:33
  79.8 5.7 %collective-permute-done.10 = f32[2,4,1,32,2,128]{5,3,4,1,0,2:T(8,128)S(1)} collective-permute-done((f32[2,4,1,32,2,128]{5,3,4,1,0,2:T(8,128)S(1)}, f32[2,4,1,32,2,128]{5,3,4,1,0,2:T(8,128)S(1)}, u32[]{:S(2)}, u32[]{:S(2)}) %collective-permute-start.10) | collective-permute-done | bytes 262176 | tf_op jit(solution)/shard_map/ppermute | solution.py:33
  97.6 9.3 %collective-permute-start.13 = (f32[1,32,2,128]{3,1,2,0:T(8,128)S(1)}, f32[1,32,2,128]{3,1,2,0:T(8,128)S(1)}, u32[]{:S(2)}, u32[]{:S(2)}) collective-permute-start(f32[1,32,2,128]{3,1,2,0:T(8,128)S(1)} %maximum_add_fusion.2), channel_id=1, source_target_pairs={{0,2},{1,3},{2,0},{3,1},{4,6},{5,7},{6,4},{7,5},{8,10},{9,11},{10,... | collective-permute-start | bytes 98312 | tf_op jit(solution)/shard_map/ppermute | solution.py:33
  106.9 6.2 %collective-permute-start.12 = (f32[1,32,2,128]{3,1,2,0:T(8,128)S(1)}, f32[1,32,2,128]{3,1,2,0:T(8,128)S(1)}, u32[]{:S(2)}, u32[]{:S(2)}) collective-permute-start(f32[1,32,2,128]{3,1,2,0:T(8,128)S(1)} %maximum_add_fusion.2), channel_id=1, source_target_pairs={{0,3},{1,0},{2,1},{3,2},{4,7},{5,4},{6,5},{7,6},{8,11},{9,8},{10,9... | collective-permute-start | bytes 98312 | tf_op jit(solution)/shard_map/ppermute | solution.py:33
  139.8 6.8 %collective-permute-done.19 = f32[4,4,1,32,2,128]{5,3,4,1,0,2:T(8,128)S(1)} collective-permute-done((f32[4,4,1,32,2,128]{5,3,4,1,0,2:T(8,128)S(1)}, f32[4,4,1,32,2,128]{5,3,4,1,0,2:T(8,128)S(1)}, u32[]{:S(2)}, u32[]{:S(2)}) %collective-permute-start.19) | collective-permute-done | bytes 524320 | tf_op jit(solution)/shard_map/ppermute | solution.py:33
  154.9 5.6 %collective-permute-done.21 = f32[2,4,1,32,2,128]{5,3,4,1,0,2:T(8,128)S(1)} collective-permute-done((f32[2,4,1,32,2,128]{5,3,4,1,0,2:T(8,128)S(1)}, f32[2,4,1,32,2,128]{5,3,4,1,0,2:T(8,128)S(1)}, u32[]{:S(2)}, u32[]{:S(2)}) %collective-permute-start.21) | collective-permute-done | bytes 262176 | tf_op jit(solution)/shard_map/ppermute | solution.py:33
  172.3 7.0 %collective-permute-start.24 = (f32[1,32,2,128]{3,1,2,0:T(8,128)S(1)}, f32[1,32,2,128]{3,1,2,0:T(8,128)S(1)}, u32[]{:S(2)}, u32[]{:S(2)}) collective-permute-start(f32[1,32,2,128]{3,1,2,0:T(8,128)S(1)} %get-tuple-element.65), channel_id=1, source_target_pairs={{0,2},{1,3},{2,0},{3,1},{4,6},{5,7},{6,4},{7,5},{8,10},{9,11},{10,... | collective-permute-start | bytes 98312 | tf_op jit(solution)/shard_map/ppermute | solution.py:33
  213.6 5.2 collective-permute-done.30
  243.3 6.7 %collective-permute-start.35 = (f32[1,32,2,128]{3,1,2,0:T(8,128)S(1)}, f32[1,32,2,128]{3,1,2,0:T(8,128)S(1)}, u32[]{:S(2)}, u32[]{:S(2)}) collective-permute-start(f32[1,32,2,128]{3,1,2,0:T(8,128)S(1)} %maximum_add_fusion.4), channel_id=1, source_target_pairs={{0,2},{1,3},{2,0},{3,1},{4,6},{5,7},{6,4},{7,5},{8,10},{9,11},{10,... | collective-permute-start | bytes 98312 | tf_op jit(solution)/shard_map/ppermute | solution.py:33
  283.3 5.2 collective-permute-done.41
  308.5 6.2 %collective-permute-start.47 = (f32[1,32,2,128]{3,1,2,0:T(8,128)S(1)}, f32[1,32,2,128]{3,1,2,0:T(8,128)S(1)}, u32[]{:S(2)}, u32[]{:S(2)}) collective-permute-start(f32[1,32,2,128]{3,1,2,0:T(8,128)S(1)} %get-tuple-element.63), channel_id=1, source_target_pairs={{0,1},{1,2},{2,3},{3,0},{4,5},{5,6},{6,7},{7,4},{8,9},{9,10},{10,1... | collective-permute-start | bytes 98312 | tf_op jit(solution)/shard_map/ppermute | solution.py:33
  314.7 5.9 %collective-permute-start.46 = (f32[1,32,2,128]{3,1,2,0:T(8,128)S(1)}, f32[1,32,2,128]{3,1,2,0:T(8,128)S(1)}, u32[]{:S(2)}, u32[]{:S(2)}) collective-permute-start(f32[1,32,2,128]{3,1,2,0:T(8,128)S(1)} %get-tuple-element.63), channel_id=1, source_target_pairs={{0,2},{1,3},{2,0},{3,1},{4,6},{5,7},{6,4},{7,5},{8,10},{9,11},{10,... | collective-permute-start | bytes 98312 | tf_op jit(solution)/shard_map/ppermute | solution.py:33
  320.6 5.4 collective-permute-start.45
  353.8 5.2 collective-permute-done.52
  383.9 7.7 %collective-permute-start.57 = (f32[1,32,2,128]{3,1,2,0:T(8,128)S(1)}, f32[1,32,2,128]{3,1,2,0:T(8,128)S(1)}, u32[]{:S(2)}, u32[]{:S(2)}) collective-permute-start(f32[1,32,2,128]{3,1,2,0:T(8,128)S(1)} %maximum_add_fusion.6), channel_id=1, source_target_pairs={{0,2},{1,3},{2,0},{3,1},{4,6},{5,7},{6,4},{7,5},{8,10},{9,11},{10,... | collective-permute-start | bytes 98312 | tf_op jit(solution)/shard_map/ppermute | solution.py:33
  391.7 6.1 %collective-permute-start.56 = (f32[1,32,2,128]{3,1,2,0:T(8,128)S(1)}, f32[1,32,2,128]{3,1,2,0:T(8,128)S(1)}, u32[]{:S(2)}, u32[]{:S(2)}) collective-permute-start(f32[1,32,2,128]{3,1,2,0:T(8,128)S(1)} %maximum_add_fusion.6), channel_id=1, source_target_pairs={{0,3},{1,0},{2,1},{3,2},{4,7},{5,4},{6,5},{7,6},{8,11},{9,8},{10,9... | collective-permute-start | bytes 98312 | tf_op jit(solution)/shard_map/ppermute | solution.py:33
  454.4 9.2 %collective-permute-start.68 = (f32[1,32,2,128]{3,1,2,0:T(8,128)S(1)}, f32[1,32,2,128]{3,1,2,0:T(8,128)S(1)}, u32[]{:S(2)}, u32[]{:S(2)}) collective-permute-start(f32[1,32,2,128]{3,1,2,0:T(8,128)S(1)} %get-tuple-element.61), channel_id=1, source_target_pairs={{0,2},{1,3},{2,0},{3,1},{4,6},{5,7},{6,4},{7,5},{8,10},{9,11},{10,... | collective-permute-start | bytes 98312 | tf_op jit(solution)/shard_map/ppermute | solution.py:33
  473.5 5.5 %collective-permute-start.71 = (f32[4,1,32,2,128]{4,2,3,1,0:T(8,128)S(1)}, f32[4,1,32,2,128]{4,2,3,1,0:T(8,128)S(1)}, u32[]{:S(2)}, u32[]{:S(2)}) collective-permute-start(f32[4,1,32,2,128]{4,2,3,1,0:T(8,128)S(1)} %get-tuple-element.41), channel_id=1, source_target_pairs={{0,4},{1,5},{2,6},{3,7},{4,8},{5,9},{6,10},{7,11},{8,12},{9,13},{1... | collective-permute-start | bytes 393224 | tf_op jit(solution)/shard_map/ppermute | solution.py:33
  509.0 5.6 %collective-permute-done.74 = f32[4,4,1,32,2,128]{5,3,4,1,0,2:T(8,128)S(1)} collective-permute-done((f32[4,4,1,32,2,128]{5,3,4,1,0,2:T(8,128)S(1)}, f32[4,4,1,32,2,128]{5,3,4,1,0,2:T(8,128)S(1)}, u32[]{:S(2)}, u32[]{:S(2)}) %collective-permute-start.74) | collective-permute-done | bytes 524320 | tf_op jit(solution)/shard_map/ppermute | solution.py:33
  514.6 5.8 %collective-permute-start.77 = (f32[2,4,1,32,2,128]{5,3,4,1,0,2:T(8,128)S(1)}, f32[2,4,1,32,2,128]{5,3,4,1,0,2:T(8,128)S(1)}, u32[]{:S(2)}, u32[]{:S(2)}) collective-permute-start(f32[2,4,1,32,2,128]{5,3,4,1,0,2:T(8,128)S(1)} %slice.315), channel_id=1, source_target_pairs={{0,48},{1,49},{2,50},{3,51},{4,52},{5,53},{6,54},{7,55},{8,56},{9,... | collective-permute-start | bytes 786440 | tf_op jit(solution)/shard_map/ppermute | solution.py:33
  524.1 5.8 %collective-permute-done.76 = f32[2,4,1,32,2,128]{5,3,4,1,0,2:T(8,128)S(1)} collective-permute-done((f32[2,4,1,32,2,128]{5,3,4,1,0,2:T(8,128)S(1)}, f32[2,4,1,32,2,128]{5,3,4,1,0,2:T(8,128)S(1)}, u32[]{:S(2)}, u32[]{:S(2)}) %collective-permute-start.76) | collective-permute-done | bytes 262176 | tf_op jit(solution)/shard_map/ppermute | solution.py:33
  (286 shorter events, 381.3 us)
Async XLA Ops:
  9.3 25.5 %collective-permute-start.3 = (f32[1,32,2,128]{3,1,2,0:T(8,128)S(1)}, f32[1,32,2,128]{3,1,2,0:T(8,128)S(1)}, u32[]{:S(2)}, u32[]{:S(2)}) collective-permute-start(f32[1,32,2,128]{3,1,2,0:T(8,128)S(1)} %get-tuple-element.67), channel_id=1, source_target_pairs={{0,1},{1,2},{2,3},{3,0},{4,5},{5,6},{6,7},{7,4},{8,9},{9,10},{10,1... | collective-permute-start | bytes 98312 | tf_op jit(solution)/shard_map/ppermute | solution.py:33
  18.4 16.4 %collective-permute-start.2 = (f32[1,32,2,128]{3,1,2,0:T(8,128)S(1)}, f32[1,32,2,128]{3,1,2,0:T(8,128)S(1)}, u32[]{:S(2)}, u32[]{:S(2)}) collective-permute-start(f32[1,32,2,128]{3,1,2,0:T(8,128)S(1)} %get-tuple-element.67), channel_id=1, source_target_pairs={{0,2},{1,3},{2,0},{3,1},{4,6},{5,7},{6,4},{7,5},{8,10},{9,11},{10,... | collective-permute-start | bytes 98312 | tf_op jit(solution)/shard_map/ppermute | solution.py:33
  63.1 12.8 %collective-permute-start.9 = (f32[4,4,1,32,2,128]{5,3,4,1,2,0:T(8,128)S(1)}, f32[4,4,1,32,2,128]{5,3,4,1,2,0:T(8,128)S(1)}, u32[]{:S(2)}, u32[]{:S(2)}) collective-permute-start(f32[4,4,1,32,2,128]{5,3,4,1,2,0:T(8,128)S(1)} %get-tuple-element.36), channel_id=1, source_target_pairs={{0,16},{1,17},{2,18},{3,19},{4,20},{5,21},{6,22},{7,23},{8,24},{9,... | collective-permute-start | bytes 1572872 | tf_op jit(solution)/shard_map/ppermute | solution.py:33
  94.2 18.9 %collective-permute-start.14 = (f32[1,32,2,128]{3,1,2,0:T(8,128)S(1)}, f32[1,32,2,128]{3,1,2,0:T(8,128)S(1)}, u32[]{:S(2)}, u32[]{:S(2)}) collective-permute-start(f32[1,32,2,128]{3,1,2,0:T(8,128)S(1)} %maximum_add_fusion.2), channel_id=1, source_target_pairs={{0,1},{1,2},{2,3},{3,0},{4,5},{5,6},{6,7},{7,4},{8,9},{9,10},{10,1... | collective-permute-start | bytes 98312 | tf_op jit(solution)/shard_map/ppermute | solution.py:33
  97.6 15.5 %collective-permute-start.13 = (f32[1,32,2,128]{3,1,2,0:T(8,128)S(1)}, f32[1,32,2,128]{3,1,2,0:T(8,128)S(1)}, u32[]{:S(2)}, u32[]{:S(2)}) collective-permute-start(f32[1,32,2,128]{3,1,2,0:T(8,128)S(1)} %maximum_add_fusion.2), channel_id=1, source_target_pairs={{0,2},{1,3},{2,0},{3,1},{4,6},{5,7},{6,4},{7,5},{8,10},{9,11},{10,... | collective-permute-start | bytes 98312 | tf_op jit(solution)/shard_map/ppermute | solution.py:33
  134.0 12.7 %collective-permute-start.19 = (f32[4,4,1,32,2,128]{5,3,4,1,0,2:T(8,128)S(1)}, f32[4,4,1,32,2,128]{5,3,4,1,0,2:T(8,128)S(1)}, u32[]{:S(2)}, u32[]{:S(2)}) collective-permute-start(f32[4,4,1,32,2,128]{5,3,4,1,0,2:T(8,128)S(1)} %get-tuple-element.30), channel_id=1, source_target_pairs={{0,48},{1,49},{2,50},{3,51},{4,52},{5,53},{6,54},{7,55},{8,56},{9,... | collective-permute-start | bytes 1572872 | tf_op jit(solution)/shard_map/ppermute | solution.py:33
  135.9 15.1 %collective-permute-start.20 = (f32[4,4,1,32,2,128]{5,3,4,1,2,0:T(8,128)S(1)}, f32[4,4,1,32,2,128]{5,3,4,1,2,0:T(8,128)S(1)}, u32[]{:S(2)}, u32[]{:S(2)}) collective-permute-start(f32[4,4,1,32,2,128]{5,3,4,1,2,0:T(8,128)S(1)} %get-tuple-element.31), channel_id=1, source_target_pairs={{0,16},{1,17},{2,18},{3,19},{4,20},{5,21},{6,22},{7,23},{8,24},{9,... | collective-permute-start | bytes 1572872 | tf_op jit(solution)/shard_map/ppermute | solution.py:33
  167.8 16.4 %collective-permute-start.25 = (f32[1,32,2,128]{3,1,2,0:T(8,128)S(1)}, f32[1,32,2,128]{3,1,2,0:T(8,128)S(1)}, u32[]{:S(2)}, u32[]{:S(2)}) collective-permute-start(f32[1,32,2,128]{3,1,2,0:T(8,128)S(1)} %get-tuple-element.65), channel_id=1, source_target_pairs={{0,1},{1,2},{2,3},{3,0},{4,5},{5,6},{6,7},{7,4},{8,9},{9,10},{10,1... | collective-permute-start | bytes 98312 | tf_op jit(solution)/shard_map/ppermute | solution.py:33
  172.3 14.5 %collective-permute-start.24 = (f32[1,32,2,128]{3,1,2,0:T(8,128)S(1)}, f32[1,32,2,128]{3,1,2,0:T(8,128)S(1)}, u32[]{:S(2)}, u32[]{:S(2)}) collective-permute-start(f32[1,32,2,128]{3,1,2,0:T(8,128)S(1)} %get-tuple-element.65), channel_id=1, source_target_pairs={{0,2},{1,3},{2,0},{3,1},{4,6},{5,7},{6,4},{7,5},{8,10},{9,11},{10,... | collective-permute-start | bytes 98312 | tf_op jit(solution)/shard_map/ppermute | solution.py:33
  209.7 12.3 %collective-permute-start.31 = (f32[4,4,1,32,2,128]{5,3,4,1,2,0:T(8,128)S(1)}, f32[4,4,1,32,2,128]{5,3,4,1,2,0:T(8,128)S(1)}, u32[]{:S(2)}, u32[]{:S(2)}) collective-permute-start(f32[4,4,1,32,2,128]{5,3,4,1,2,0:T(8,128)S(1)} %get-tuple-element.28), channel_id=1, source_target_pairs={{0,16},{1,17},{2,18},{3,19},{4,20},{5,21},{6,22},{7,23},{8,24},{9,... | collective-permute-start | bytes 1572872 | tf_op jit(solution)/shard_map/ppermute | solution.py:33
  238.9 16.1 %collective-permute-start.36 = (f32[1,32,2,128]{3,1,2,0:T(8,128)S(1)}, f32[1,32,2,128]{3,1,2,0:T(8,128)S(1)}, u32[]{:S(2)}, u32[]{:S(2)}) collective-permute-start(f32[1,32,2,128]{3,1,2,0:T(8,128)S(1)} %maximum_add_fusion.4), channel_id=1, source_target_pairs={{0,1},{1,2},{2,3},{3,0},{4,5},{5,6},{6,7},{7,4},{8,9},{9,10},{10,1... | collective-permute-start | bytes 98312 | tf_op jit(solution)/shard_map/ppermute | solution.py:33
  243.3 14.9 %collective-permute-start.35 = (f32[1,32,2,128]{3,1,2,0:T(8,128)S(1)}, f32[1,32,2,128]{3,1,2,0:T(8,128)S(1)}, u32[]{:S(2)}, u32[]{:S(2)}) collective-permute-start(f32[1,32,2,128]{3,1,2,0:T(8,128)S(1)} %maximum_add_fusion.4), channel_id=1, source_target_pairs={{0,2},{1,3},{2,0},{3,1},{4,6},{5,7},{6,4},{7,5},{8,10},{9,11},{10,... | collective-permute-start | bytes 98312 | tf_op jit(solution)/shard_map/ppermute | solution.py:33
  279.3 12.3 %collective-permute-start.42 = (f32[4,4,1,32,2,128]{5,3,4,1,2,0:T(8,128)S(1)}, f32[4,4,1,32,2,128]{5,3,4,1,2,0:T(8,128)S(1)}, u32[]{:S(2)}, u32[]{:S(2)}) collective-permute-start(f32[4,4,1,32,2,128]{5,3,4,1,2,0:T(8,128)S(1)} %get-tuple-element.25), channel_id=1, source_target_pairs={{0,16},{1,17},{2,18},{3,19},{4,20},{5,21},{6,22},{7,23},{8,24},{9,... | collective-permute-start | bytes 1572872 | tf_op jit(solution)/shard_map/ppermute | solution.py:33
  308.5 17.5 %collective-permute-start.47 = (f32[1,32,2,128]{3,1,2,0:T(8,128)S(1)}, f32[1,32,2,128]{3,1,2,0:T(8,128)S(1)}, u32[]{:S(2)}, u32[]{:S(2)}) collective-permute-start(f32[1,32,2,128]{3,1,2,0:T(8,128)S(1)} %get-tuple-element.63), channel_id=1, source_target_pairs={{0,1},{1,2},{2,3},{3,0},{4,5},{5,6},{6,7},{7,4},{8,9},{9,10},{10,1... | collective-permute-start | bytes 98312 | tf_op jit(solution)/shard_map/ppermute | solution.py:33
  314.7 14.5 %collective-permute-start.46 = (f32[1,32,2,128]{3,1,2,0:T(8,128)S(1)}, f32[1,32,2,128]{3,1,2,0:T(8,128)S(1)}, u32[]{:S(2)}, u32[]{:S(2)}) collective-permute-start(f32[1,32,2,128]{3,1,2,0:T(8,128)S(1)} %get-tuple-element.63), channel_id=1, source_target_pairs={{0,2},{1,3},{2,0},{3,1},{4,6},{5,7},{6,4},{7,5},{8,10},{9,11},{10,... | collective-permute-start | bytes 98312 | tf_op jit(solution)/shard_map/ppermute | solution.py:33
  379.0 18.8 %collective-permute-start.58 = (f32[1,32,2,128]{3,1,2,0:T(8,128)S(1)}, f32[1,32,2,128]{3,1,2,0:T(8,128)S(1)}, u32[]{:S(2)}, u32[]{:S(2)}) collective-permute-start(f32[1,32,2,128]{3,1,2,0:T(8,128)S(1)} %maximum_add_fusion.6), channel_id=1, source_target_pairs={{0,1},{1,2},{2,3},{3,0},{4,5},{5,6},{6,7},{7,4},{8,9},{9,10},{10,1... | collective-permute-start | bytes 98312 | tf_op jit(solution)/shard_map/ppermute | solution.py:33
  383.9 14.5 %collective-permute-start.57 = (f32[1,32,2,128]{3,1,2,0:T(8,128)S(1)}, f32[1,32,2,128]{3,1,2,0:T(8,128)S(1)}, u32[]{:S(2)}, u32[]{:S(2)}) collective-permute-start(f32[1,32,2,128]{3,1,2,0:T(8,128)S(1)} %maximum_add_fusion.6), channel_id=1, source_target_pairs={{0,2},{1,3},{2,0},{3,1},{4,6},{5,7},{6,4},{7,5},{8,10},{9,11},{10,... | collective-permute-start | bytes 98312 | tf_op jit(solution)/shard_map/ppermute | solution.py:33
  420.9 12.3 %collective-permute-start.64 = (f32[4,4,1,32,2,128]{5,3,4,1,2,0:T(8,128)S(1)}, f32[4,4,1,32,2,128]{5,3,4,1,2,0:T(8,128)S(1)}, u32[]{:S(2)}, u32[]{:S(2)}) collective-permute-start(f32[4,4,1,32,2,128]{5,3,4,1,2,0:T(8,128)S(1)} %get-tuple-element.19), channel_id=1, source_target_pairs={{0,16},{1,17},{2,18},{3,19},{4,20},{5,21},{6,22},{7,23},{8,24},{9,... | collective-permute-start | bytes 1572872 | tf_op jit(solution)/shard_map/ppermute | solution.py:33
  436.0 58.5 %collective-permute-start.78 = (f32[96,2,2048]{2,1,0:T(2,128)}, f32[96,2,2048]{2,1,0:T(2,128)}, u32[]{:S(2)}, u32[]{:S(2)}) collective-permute-start(f32[96,2,2048]{2,1,0:T(2,128)} %bitcast.177), channel_id=1, source_target_pairs={{0,64},{64,0},{128,192},{192,128},{256,320},{320,256},{384,448},{4... | collective-permute-start | bytes 4718600 | tf_op jit(solution)/shard_map/ppermute | solution.py:10
  450.1 16.6 %collective-permute-start.69 = (f32[1,32,2,128]{3,1,2,0:T(8,128)S(1)}, f32[1,32,2,128]{3,1,2,0:T(8,128)S(1)}, u32[]{:S(2)}, u32[]{:S(2)}) collective-permute-start(f32[1,32,2,128]{3,1,2,0:T(8,128)S(1)} %get-tuple-element.61), channel_id=1, source_target_pairs={{0,1},{1,2},{2,3},{3,0},{4,5},{5,6},{6,7},{7,4},{8,9},{9,10},{10,1... | collective-permute-start | bytes 98312 | tf_op jit(solution)/shard_map/ppermute | solution.py:33
  454.4 14.5 %collective-permute-start.68 = (f32[1,32,2,128]{3,1,2,0:T(8,128)S(1)}, f32[1,32,2,128]{3,1,2,0:T(8,128)S(1)}, u32[]{:S(2)}, u32[]{:S(2)}) collective-permute-start(f32[1,32,2,128]{3,1,2,0:T(8,128)S(1)} %get-tuple-element.61), channel_id=1, source_target_pairs={{0,2},{1,3},{2,0},{3,1},{4,6},{5,7},{6,4},{7,5},{8,10},{9,11},{10,... | collective-permute-start | bytes 98312 | tf_op jit(solution)/shard_map/ppermute | solution.py:33
  473.5 15.8 %collective-permute-start.71 = (f32[4,1,32,2,128]{4,2,3,1,0:T(8,128)S(1)}, f32[4,1,32,2,128]{4,2,3,1,0:T(8,128)S(1)}, u32[]{:S(2)}, u32[]{:S(2)}) collective-permute-start(f32[4,1,32,2,128]{4,2,3,1,0:T(8,128)S(1)} %get-tuple-element.41), channel_id=1, source_target_pairs={{0,4},{1,5},{2,6},{3,7},{4,8},{5,9},{6,10},{7,11},{8,12},{9,13},{1... | collective-permute-start | bytes 393224 | tf_op jit(solution)/shard_map/ppermute | solution.py:33
  498.2 22.2 %collective-permute-start.75 = (f32[4,4,1,32,2,128]{5,3,4,1,2,0:T(8,128)S(1)}, f32[4,4,1,32,2,128]{5,3,4,1,2,0:T(8,128)S(1)}, u32[]{:S(2)}, u32[]{:S(2)}) collective-permute-start(f32[4,4,1,32,2,128]{5,3,4,1,2,0:T(8,128)S(1)} %get-tuple-element.16), channel_id=1, source_target_pairs={{0,16},{1,17},{2,18},{3,19},{4,20},{5,21},{6,22},{7,23},{8,24},{9,... | collective-permute-start | bytes 1572872 | tf_op jit(solution)/shard_map/ppermute | solution.py:33
  500.2 14.4 %collective-permute-start.74 = (f32[4,4,1,32,2,128]{5,3,4,1,0,2:T(8,128)S(1)}, f32[4,4,1,32,2,128]{5,3,4,1,0,2:T(8,128)S(1)}, u32[]{:S(2)}, u32[]{:S(2)}) collective-permute-start(f32[4,4,1,32,2,128]{5,3,4,1,0,2:T(8,128)S(1)} %get-tuple-element.15), channel_id=1, source_target_pairs={{0,48},{1,49},{2,50},{3,51},{4,52},{5,53},{6,54},{7,55},{8,56},{9,... | collective-permute-start | bytes 1572872 | tf_op jit(solution)/shard_map/ppermute | solution.py:33
  (60 other events, 568.6 us)

commit v3 on v2

--- a/solution.py
+++ b/solution.py
@@ -50,7 +50,7 @@
 
 def panel_gather(piece):
     blocks = direct_stage(piece[None], 1)
-    blocks = relay_stage(blocks, 4)
+    blocks = direct_stage(blocks, 4)
     blocks = relay_stage(blocks, 16)
     blocks = blocks.reshape((64,) + piece.shape)
     me = lax.axis_index("panel")

time: 551 us -> 521 us (0.946)
  starting transfers between devices: 322 us -> 282 us
  waiting for transfers between devices: 137 us -> 147 us
    ppermute x77 -> x70, starting transfers between devices: 318 us -> 278 us  [shifted_along(): return lax.ppermute(piece, 'panel', pairs)]
    ppermute x77 -> x70, waiting for transfers between devices: 137 us -> 147 us  [shifted_along(): return lax.ppermute(piece, 'panel', pairs)]
  transfers between devices with their start and end apart: 79 -> 72, of which waited for: 51 -> 44; matrix products, arithmetic and copies ran while one was open for 5% -> 5% of each run, Pallas kernels for 0% -> 0%
where the time goes in v3:
time: 521 us; the launch traced here: 510 us
  starting transfers between devices  282 us (54%)
  waiting for transfers between devices  147 us (28%)
  matrix products  31 us (6%)
  local copies, waits for them, and re-layouts  30.1 us (6%)
  other arithmetic  17.9 us (3%)
    ppermute x70, starting transfers between devices, shifted_along(): return lax.ppermute(piece, 'panel', pairs)  278 us
    ppermute x70, waiting for transfers between devices, shifted_along(): return lax.ppermute(piece, 'panel', pairs)  147 us
    gather x7, local copies, waits for them, and re-layouts, panel_gather(): out = jnp.take(blocks, slot, axis=0)  13.9 us
    select_n x7, other arithmetic, panel_gather(): out = jnp.take(blocks, slot, axis=0)  12.6 us
  transfers between devices with their start and end apart: 72, of which 44 were waited for; matrix products, arithmetic and copies ran while one was open for 5% of the time, Pallas kernels for 0%

profile of v3, /device:TPU:6, one launch (start us, length us, event | category | flops | bytes accessed | tf_op | source)
XLA Modules:
  0.0 510.4 jit_solution(12170032947839644270)
XLA Ops:
  9.3 9.1 %collective-permute-start.3 = (f32[1,32,2,128]{3,1,2,0:T(8,128)S(1)}, f32[1,32,2,128]{3,1,2,0:T(8,128)S(1)}, u32[]{:S(2)}, u32[]{:S(2)}) collective-permute-start(f32[1,32,2,128]{3,1,2,0:T(8,128)S(1)} %get-tuple-element.67), channel_id=1, source_target_pairs={{0,1},{1,2},{2,3},{3,0},{4,5},{5,6},{6,7},{7,4},{8,9},{9,10},{10,1... | collective-permute-start | bytes 98312 | tf_op jit(solution)/shard_map/ppermute | solution.py:33
  18.4 10.9 %collective-permute-start.2 = (f32[1,32,2,128]{3,1,2,0:T(8,128)S(1)}, f32[1,32,2,128]{3,1,2,0:T(8,128)S(1)}, u32[]{:S(2)}, u32[]{:S(2)}) collective-permute-start(f32[1,32,2,128]{3,1,2,0:T(8,128)S(1)} %get-tuple-element.67), channel_id=1, source_target_pairs={{0,2},{1,3},{2,0},{3,1},{4,6},{5,7},{6,4},{7,5},{8,10},{9,11},{10,... | collective-permute-start | bytes 98312 | tf_op jit(solution)/shard_map/ppermute | solution.py:33
  29.3 5.5 %collective-permute-start.1 = (f32[1,32,2,128]{3,1,2,0:T(8,128)S(1)}, f32[1,32,2,128]{3,1,2,0:T(8,128)S(1)}, u32[]{:S(2)}, u32[]{:S(2)}) collective-permute-start(f32[1,32,2,128]{3,1,2,0:T(8,128)S(1)} %get-tuple-element.67), channel_id=1, source_target_pairs={{0,3},{1,0},{2,1},{3,2},{4,7},{5,4},{6,5},{7,6},{8,11},{9,8},{10,9... | collective-permute-start | bytes 98312 | tf_op jit(solution)/shard_map/ppermute | solution.py:33
  63.3 6.4 %collective-permute-done.7 = f32[4,4,1,32,2,128]{5,3,4,1,0,2:T(8,128)S(1)} collective-permute-done((f32[4,4,1,32,2,128]{5,3,4,1,0,2:T(8,128)}, f32[4,4,1,32,2,128]{5,3,4,1,0,2:T(8,128)S(1)}, u32[]{:S(2)}, u32[]{:S(2)}) %collective-permute-start.7) | collective-permute-done | bytes 524320 | tf_op jit(solution)/shard_map/ppermute | solution.py:33
  69.7 5.5 %collective-permute-start.10 = (f32[2,4,1,32,2,128]{5,3,4,1,0,2:T(8,128)S(1)}, f32[2,4,1,32,2,128]{5,3,4,1,0,2:T(8,128)S(1)}, u32[]{:S(2)}, u32[]{:S(2)}) collective-permute-start(f32[2,4,1,32,2,128]{5,3,4,1,0,2:T(8,128)S(1)} %slice.219), channel_id=1, source_target_pairs={{0,48},{1,49},{2,50},{3,51},{4,52},{5,53},{6,54},{7,55},{8,56},{9,... | collective-permute-start | bytes 786440 | tf_op jit(solution)/shard_map/ppermute | solution.py:33
  79.1 5.7 %collective-permute-done.9 = f32[2,4,1,32,2,128]{5,3,4,1,0,2:T(8,128)S(1)} collective-permute-done((f32[2,4,1,32,2,128]{5,3,4,1,0,2:T(8,128)S(1)}, f32[2,4,1,32,2,128]{5,3,4,1,0,2:T(8,128)S(1)}, u32[]{:S(2)}, u32[]{:S(2)}) %collective-permute-start.9) | collective-permute-done | bytes 262176 | tf_op jit(solution)/shard_map/ppermute | solution.py:33
  96.7 9.3 %collective-permute-start.12 = (f32[1,32,2,128]{3,1,2,0:T(8,128)S(1)}, f32[1,32,2,128]{3,1,2,0:T(8,128)S(1)}, u32[]{:S(2)}, u32[]{:S(2)}) collective-permute-start(f32[1,32,2,128]{3,1,2,0:T(8,128)S(1)} %maximum_add_fusion.2), channel_id=1, source_target_pairs={{0,2},{1,3},{2,0},{3,1},{4,6},{5,7},{6,4},{7,5},{8,10},{9,11},{10,... | collective-permute-start | bytes 98312 | tf_op jit(solution)/shard_map/ppermute | solution.py:33
  135.2 8.0 %collective-permute-done.17 = f32[4,4,1,32,2,128]{5,3,4,1,0,2:T(8,128)S(1)} collective-permute-done((f32[4,4,1,32,2,128]{5,3,4,1,0,2:T(8,128)S(1)}, f32[4,4,1,32,2,128]{5,3,4,1,0,2:T(8,128)S(1)}, u32[]{:S(2)}, u32[]{:S(2)}) %collective-permute-start.17) | collective-permute-done | bytes 524320 | tf_op jit(solution)/shard_map/ppermute | solution.py:33
  168.0 7.6 %collective-permute-start.22 = (f32[1,32,2,128]{3,1,2,0:T(8,128)S(1)}, f32[1,32,2,128]{3,1,2,0:T(8,128)S(1)}, u32[]{:S(2)}, u32[]{:S(2)}) collective-permute-start(f32[1,32,2,128]{3,1,2,0:T(8,128)S(1)} %get-tuple-element.65), channel_id=1, source_target_pairs={{0,2},{1,3},{2,0},{3,1},{4,6},{5,7},{6,4},{7,5},{8,10},{9,11},{10,... | collective-permute-start | bytes 98312 | tf_op jit(solution)/shard_map/ppermute | solution.py:33
  205.7 5.2 %collective-permute-done.27 = f32[4,4,1,32,2,128]{5,3,4,1,0,2:T(8,128)S(1)} collective-permute-done((f32[4,4,1,32,2,128]{5,3,4,1,0,2:T(8,128)S(1)}, f32[4,4,1,32,2,128]{5,3,4,1,0,2:T(8,128)S(1)}, u32[]{:S(2)}, u32[]{:S(2)}) %collective-permute-start.27) | collective-permute-done | bytes 524320 | tf_op jit(solution)/shard_map/ppermute | solution.py:33
  235.6 6.2 %collective-permute-start.32 = (f32[1,32,2,128]{3,1,2,0:T(8,128)S(1)}, f32[1,32,2,128]{3,1,2,0:T(8,128)S(1)}, u32[]{:S(2)}, u32[]{:S(2)}) collective-permute-start(f32[1,32,2,128]{3,1,2,0:T(8,128)S(1)} %maximum_add_fusion.4), channel_id=1, source_target_pairs={{0,2},{1,3},{2,0},{3,1},{4,6},{5,7},{6,4},{7,5},{8,10},{9,11},{10,... | collective-permute-start | bytes 98312 | tf_op jit(solution)/shard_map/ppermute | solution.py:33
  241.8 5.5 %collective-permute-start.31 = (f32[1,32,2,128]{3,1,2,0:T(8,128)S(1)}, f32[1,32,2,128]{3,1,2,0:T(8,128)S(1)}, u32[]{:S(2)}, u32[]{:S(2)}) collective-permute-start(f32[1,32,2,128]{3,1,2,0:T(8,128)S(1)} %maximum_add_fusion.4), channel_id=1, source_target_pairs={{0,3},{1,0},{2,1},{3,2},{4,7},{5,4},{6,5},{7,6},{8,11},{9,8},{10,9... | collective-permute-start | bytes 98312 | tf_op jit(solution)/shard_map/ppermute | solution.py:33
  271.5 5.2 %collective-permute-done.37 = f32[4,4,1,32,2,128]{5,3,4,1,0,2:T(8,128)S(1)} collective-permute-done((f32[4,4,1,32,2,128]{5,3,4,1,0,2:T(8,128)S(1)}, f32[4,4,1,32,2,128]{5,3,4,1,0,2:T(8,128)S(1)}, u32[]{:S(2)}, u32[]{:S(2)}) %collective-permute-start.37) | collective-permute-done | bytes 524320 | tf_op jit(solution)/shard_map/ppermute | solution.py:33
  296.7 7.1 %collective-permute-start.43 = (f32[1,32,2,128]{3,1,2,0:T(8,128)S(1)}, f32[1,32,2,128]{3,1,2,0:T(8,128)S(1)}, u32[]{:S(2)}, u32[]{:S(2)}) collective-permute-start(f32[1,32,2,128]{3,1,2,0:T(8,128)S(1)} %get-tuple-element.63), channel_id=1, source_target_pairs={{0,1},{1,2},{2,3},{3,0},{4,5},{5,6},{6,7},{7,4},{8,9},{9,10},{10,1... | collective-permute-start | bytes 98312 | tf_op jit(solution)/shard_map/ppermute | solution.py:33
  303.8 5.9 %collective-permute-start.42 = (f32[1,32,2,128]{3,1,2,0:T(8,128)S(1)}, f32[1,32,2,128]{3,1,2,0:T(8,128)S(1)}, u32[]{:S(2)}, u32[]{:S(2)}) collective-permute-start(f32[1,32,2,128]{3,1,2,0:T(8,128)S(1)} %get-tuple-element.63), channel_id=1, source_target_pairs={{0,2},{1,3},{2,0},{3,1},{4,6},{5,7},{6,4},{7,5},{8,10},{9,11},{10,... | collective-permute-start | bytes 98312 | tf_op jit(solution)/shard_map/ppermute | solution.py:33
  339.7 5.2 %collective-permute-done.47 = f32[4,4,1,32,2,128]{5,3,4,1,0,2:T(8,128)S(1)} collective-permute-done((f32[4,4,1,32,2,128]{5,3,4,1,0,2:T(8,128)S(1)}, f32[4,4,1,32,2,128]{5,3,4,1,0,2:T(8,128)S(1)}, u32[]{:S(2)}, u32[]{:S(2)}) %collective-permute-start.47) | collective-permute-done | bytes 524320 | tf_op jit(solution)/shard_map/ppermute | solution.py:33
  368.9 8.2 %collective-permute-start.52 = (f32[1,32,2,128]{3,1,2,0:T(8,128)S(1)}, f32[1,32,2,128]{3,1,2,0:T(8,128)S(1)}, u32[]{:S(2)}, u32[]{:S(2)}) collective-permute-start(f32[1,32,2,128]{3,1,2,0:T(8,128)S(1)} %maximum_add_fusion.6), channel_id=1, source_target_pairs={{0,2},{1,3},{2,0},{3,1},{4,6},{5,7},{6,4},{7,5},{8,10},{9,11},{10,... | collective-permute-start | bytes 98312 | tf_op jit(solution)/shard_map/ppermute | solution.py:33
  377.1 6.2 %collective-permute-start.51 = (f32[1,32,2,128]{3,1,2,0:T(8,128)S(1)}, f32[1,32,2,128]{3,1,2,0:T(8,128)S(1)}, u32[]{:S(2)}, u32[]{:S(2)}) collective-permute-start(f32[1,32,2,128]{3,1,2,0:T(8,128)S(1)} %maximum_add_fusion.6), channel_id=1, source_target_pairs={{0,3},{1,0},{2,1},{3,2},{4,7},{5,4},{6,5},{7,6},{8,11},{9,8},{10,9... | collective-permute-start | bytes 98312 | tf_op jit(solution)/shard_map/ppermute | solution.py:33
  406.5 5.2 %collective-permute-done.57 = f32[4,4,1,32,2,128]{5,3,4,1,0,2:T(8,128)S(1)} collective-permute-done((f32[4,4,1,32,2,128]{5,3,4,1,0,2:T(8,128)S(1)}, f32[4,4,1,32,2,128]{5,3,4,1,0,2:T(8,128)S(1)}, u32[]{:S(2)}, u32[]{:S(2)}) %collective-permute-start.57) | collective-permute-done | bytes 524320 | tf_op jit(solution)/shard_map/ppermute | solution.py:33
  431.7 5.4 %collective-permute-start.63 = (f32[1,32,2,128]{3,1,2,0:T(8,128)S(1)}, f32[1,32,2,128]{3,1,2,0:T(8,128)S(1)}, u32[]{:S(2)}, u32[]{:S(2)}) collective-permute-start(f32[1,32,2,128]{3,1,2,0:T(8,128)S(1)} %get-tuple-element.61), channel_id=1, source_target_pairs={{0,1},{1,2},{2,3},{3,0},{4,5},{5,6},{6,7},{7,4},{8,9},{9,10},{10,1... | collective-permute-start | bytes 98312 | tf_op jit(solution)/shard_map/ppermute | solution.py:33
  437.1 8.3 %collective-permute-start.62 = (f32[1,32,2,128]{3,1,2,0:T(8,128)S(1)}, f32[1,32,2,128]{3,1,2,0:T(8,128)S(1)}, u32[]{:S(2)}, u32[]{:S(2)}) collective-permute-start(f32[1,32,2,128]{3,1,2,0:T(8,128)S(1)} %get-tuple-element.61), channel_id=1, source_target_pairs={{0,2},{1,3},{2,0},{3,1},{4,6},{5,7},{6,4},{7,5},{8,10},{9,11},{10,... | collective-permute-start | bytes 98312 | tf_op jit(solution)/shard_map/ppermute | solution.py:33
  471.6 5.1 %collective-permute-start.67 = (f32[4,4,1,32,2,128]{5,3,4,1,0,2:T(8,128)S(1)}, f32[4,4,1,32,2,128]{5,3,4,1,0,2:T(8,128)S(1)}, u32[]{:S(2)}, u32[]{:S(2)}) collective-permute-start(f32[4,4,1,32,2,128]{5,3,4,1,0,2:T(8,128)S(1)} %get-tuple-element.15), channel_id=1, source_target_pairs={{0,48},{1,49},{2,50},{3,51},{4,52},{5,53},{6,54},{7,55},{8,56},{9,... | collective-permute-start | bytes 1572872 | tf_op jit(solution)/shard_map/ppermute | solution.py:33
  485.1 5.6 %collective-permute-start.70 = (f32[2,4,1,32,2,128]{5,3,4,1,0,2:T(8,128)S(1)}, f32[2,4,1,32,2,128]{5,3,4,1,0,2:T(8,128)S(1)}, u32[]{:S(2)}, u32[]{:S(2)}) collective-permute-start(f32[2,4,1,32,2,128]{5,3,4,1,0,2:T(8,128)S(1)} %slice.245), channel_id=1, source_target_pairs={{0,48},{1,49},{2,50},{3,51},{4,52},{5,53},{6,54},{7,55},{8,56},{9,... | collective-permute-start | bytes 786440 | tf_op jit(solution)/shard_map/ppermute | solution.py:33
  494.6 5.6 %collective-permute-done.69 = f32[2,4,1,32,2,128]{5,3,4,1,0,2:T(8,128)S(1)} collective-permute-done((f32[2,4,1,32,2,128]{5,3,4,1,0,2:T(8,128)S(1)}, f32[2,4,1,32,2,128]{5,3,4,1,0,2:T(8,128)S(1)}, u32[]{:S(2)}, u32[]{:S(2)}) %collective-permute-start.69) | collective-permute-done | bytes 262176 | tf_op jit(solution)/shard_map/ppermute | solution.py:33
  (251 shorter events, 350.7 us)
Async XLA Ops:
  9.3 25.5 %collective-permute-start.3 = (f32[1,32,2,128]{3,1,2,0:T(8,128)S(1)}, f32[1,32,2,128]{3,1,2,0:T(8,128)S(1)}, u32[]{:S(2)}, u32[]{:S(2)}) collective-permute-start(f32[1,32,2,128]{3,1,2,0:T(8,128)S(1)} %get-tuple-element.67), channel_id=1, source_target_pairs={{0,1},{1,2},{2,3},{3,0},{4,5},{5,6},{6,7},{7,4},{8,9},{9,10},{10,1... | collective-permute-start | bytes 98312 | tf_op jit(solution)/shard_map/ppermute | solution.py:33
  18.4 16.4 %collective-permute-start.2 = (f32[1,32,2,128]{3,1,2,0:T(8,128)S(1)}, f32[1,32,2,128]{3,1,2,0:T(8,128)S(1)}, u32[]{:S(2)}, u32[]{:S(2)}) collective-permute-start(f32[1,32,2,128]{3,1,2,0:T(8,128)S(1)} %get-tuple-element.67), channel_id=1, source_target_pairs={{0,2},{1,3},{2,0},{3,1},{4,6},{5,7},{6,4},{7,5},{8,10},{9,11},{10,... | collective-permute-start | bytes 98312 | tf_op jit(solution)/shard_map/ppermute | solution.py:33
  55.9 13.7 %collective-permute-start.7 = (f32[4,4,1,32,2,128]{5,3,4,1,0,2:T(8,128)}, f32[4,4,1,32,2,128]{5,3,4,1,0,2:T(8,128)S(1)}, u32[]{:S(2)}, u32[]{:S(2)}) collective-permute-start(f32[4,4,1,32,2,128]{5,3,4,1,0,2:T(8,128)} %get-tuple-element.35), channel_id=1, source_target_pairs={{0,48},{1,49},{2,50},{3,51},{4,52},{5,53},{6,54},{7,55},{8,56},{9,... | collective-permute-start | bytes 1572872 | tf_op jit(solution)/shard_map/ppermute | solution.py:33
  60.9 14.4 %collective-permute-start.8 = (f32[4,4,1,32,2,128]{5,3,4,1,2,0:T(8,128)S(1)}, f32[4,4,1,32,2,128]{5,3,4,1,2,0:T(8,128)S(1)}, u32[]{:S(2)}, u32[]{:S(2)}) collective-permute-start(f32[4,4,1,32,2,128]{5,3,4,1,2,0:T(8,128)S(1)} %get-tuple-element.36), channel_id=1, source_target_pairs={{0,16},{1,17},{2,18},{3,19},{4,20},{5,21},{6,22},{7,23},{8,24},{9,... | collective-permute-start | bytes 1572872 | tf_op jit(solution)/shard_map/ppermute | solution.py:33
  93.4 16.8 %collective-permute-start.13 = (f32[1,32,2,128]{3,1,2,0:T(8,128)S(1)}, f32[1,32,2,128]{3,1,2,0:T(8,128)S(1)}, u32[]{:S(2)}, u32[]{:S(2)}) collective-permute-start(f32[1,32,2,128]{3,1,2,0:T(8,128)S(1)} %maximum_add_fusion.2), channel_id=1, source_target_pairs={{0,1},{1,2},{2,3},{3,0},{4,5},{5,6},{6,7},{7,4},{8,9},{9,10},{10,1... | collective-permute-start | bytes 98312 | tf_op jit(solution)/shard_map/ppermute | solution.py:33
  96.7 14.7 %collective-permute-start.12 = (f32[1,32,2,128]{3,1,2,0:T(8,128)S(1)}, f32[1,32,2,128]{3,1,2,0:T(8,128)S(1)}, u32[]{:S(2)}, u32[]{:S(2)}) collective-permute-start(f32[1,32,2,128]{3,1,2,0:T(8,128)S(1)} %maximum_add_fusion.2), channel_id=1, source_target_pairs={{0,2},{1,3},{2,0},{3,1},{4,6},{5,7},{6,4},{7,5},{8,10},{9,11},{10,... | collective-permute-start | bytes 98312 | tf_op jit(solution)/shard_map/ppermute | solution.py:33
  129.3 13.9 %collective-permute-start.17 = (f32[4,4,1,32,2,128]{5,3,4,1,0,2:T(8,128)S(1)}, f32[4,4,1,32,2,128]{5,3,4,1,0,2:T(8,128)S(1)}, u32[]{:S(2)}, u32[]{:S(2)}) collective-permute-start(f32[4,4,1,32,2,128]{5,3,4,1,0,2:T(8,128)S(1)} %get-tuple-element.30), channel_id=1, source_target_pairs={{0,48},{1,49},{2,50},{3,51},{4,52},{5,53},{6,54},{7,55},{8,56},{9,... | collective-permute-start | bytes 1572872 | tf_op jit(solution)/shard_map/ppermute | solution.py:33
  131.2 15.1 %collective-permute-start.18 = (f32[4,4,1,32,2,128]{5,3,4,1,2,0:T(8,128)S(1)}, f32[4,4,1,32,2,128]{5,3,4,1,2,0:T(8,128)S(1)}, u32[]{:S(2)}, u32[]{:S(2)}) collective-permute-start(f32[4,4,1,32,2,128]{5,3,4,1,2,0:T(8,128)S(1)} %get-tuple-element.31), channel_id=1, source_target_pairs={{0,16},{1,17},{2,18},{3,19},{4,20},{5,21},{6,22},{7,23},{8,24},{9,... | collective-permute-start | bytes 1572872 | tf_op jit(solution)/shard_map/ppermute | solution.py:33
  163.2 15.8 %collective-permute-start.23 = (f32[1,32,2,128]{3,1,2,0:T(8,128)S(1)}, f32[1,32,2,128]{3,1,2,0:T(8,128)S(1)}, u32[]{:S(2)}, u32[]{:S(2)}) collective-permute-start(f32[1,32,2,128]{3,1,2,0:T(8,128)S(1)} %get-tuple-element.65), channel_id=1, source_target_pairs={{0,1},{1,2},{2,3},{3,0},{4,5},{5,6},{6,7},{7,4},{8,9},{9,10},{10,1... | collective-permute-start | bytes 98312 | tf_op jit(solution)/shard_map/ppermute | solution.py:33
  168.0 14.6 %collective-permute-start.22 = (f32[1,32,2,128]{3,1,2,0:T(8,128)S(1)}, f32[1,32,2,128]{3,1,2,0:T(8,128)S(1)}, u32[]{:S(2)}, u32[]{:S(2)}) collective-permute-start(f32[1,32,2,128]{3,1,2,0:T(8,128)S(1)} %get-tuple-element.65), channel_id=1, source_target_pairs={{0,2},{1,3},{2,0},{3,1},{4,6},{5,7},{6,4},{7,5},{8,10},{9,11},{10,... | collective-permute-start | bytes 98312 | tf_op jit(solution)/shard_map/ppermute | solution.py:33
  201.8 12.3 %collective-permute-start.28 = (f32[4,4,1,32,2,128]{5,3,4,1,2,0:T(8,128)S(1)}, f32[4,4,1,32,2,128]{5,3,4,1,2,0:T(8,128)S(1)}, u32[]{:S(2)}, u32[]{:S(2)}) collective-permute-start(f32[4,4,1,32,2,128]{5,3,4,1,2,0:T(8,128)S(1)} %get-tuple-element.28), channel_id=1, source_target_pairs={{0,16},{1,17},{2,18},{3,19},{4,20},{5,21},{6,22},{7,23},{8,24},{9,... | collective-permute-start | bytes 1572872 | tf_op jit(solution)/shard_map/ppermute | solution.py:33
  230.9 16.4 %collective-permute-start.33 = (f32[1,32,2,128]{3,1,2,0:T(8,128)S(1)}, f32[1,32,2,128]{3,1,2,0:T(8,128)S(1)}, u32[]{:S(2)}, u32[]{:S(2)}) collective-permute-start(f32[1,32,2,128]{3,1,2,0:T(8,128)S(1)} %maximum_add_fusion.4), channel_id=1, source_target_pairs={{0,1},{1,2},{2,3},{3,0},{4,5},{5,6},{6,7},{7,4},{8,9},{9,10},{10,1... | collective-permute-start | bytes 98312 | tf_op jit(solution)/shard_map/ppermute | solution.py:33
  235.6 14.5 %collective-permute-start.32 = (f32[1,32,2,128]{3,1,2,0:T(8,128)S(1)}, f32[1,32,2,128]{3,1,2,0:T(8,128)S(1)}, u32[]{:S(2)}, u32[]{:S(2)}) collective-permute-start(f32[1,32,2,128]{3,1,2,0:T(8,128)S(1)} %maximum_add_fusion.4), channel_id=1, source_target_pairs={{0,2},{1,3},{2,0},{3,1},{4,6},{5,7},{6,4},{7,5},{8,10},{9,11},{10,... | collective-permute-start | bytes 98312 | tf_op jit(solution)/shard_map/ppermute | solution.py:33
  267.6 12.3 %collective-permute-start.38 = (f32[4,4,1,32,2,128]{5,3,4,1,2,0:T(8,128)S(1)}, f32[4,4,1,32,2,128]{5,3,4,1,2,0:T(8,128)S(1)}, u32[]{:S(2)}, u32[]{:S(2)}) collective-permute-start(f32[4,4,1,32,2,128]{5,3,4,1,2,0:T(8,128)S(1)} %get-tuple-element.25), channel_id=1, source_target_pairs={{0,16},{1,17},{2,18},{3,19},{4,20},{5,21},{6,22},{7,23},{8,24},{9,... | collective-permute-start | bytes 1572872 | tf_op jit(solution)/shard_map/ppermute | solution.py:33
  296.7 18.0 %collective-permute-start.43 = (f32[1,32,2,128]{3,1,2,0:T(8,128)S(1)}, f32[1,32,2,128]{3,1,2,0:T(8,128)S(1)}, u32[]{:S(2)}, u32[]{:S(2)}) collective-permute-start(f32[1,32,2,128]{3,1,2,0:T(8,128)S(1)} %get-tuple-element.63), channel_id=1, source_target_pairs={{0,1},{1,2},{2,3},{3,0},{4,5},{5,6},{6,7},{7,4},{8,9},{9,10},{10,1... | collective-permute-start | bytes 98312 | tf_op jit(solution)/shard_map/ppermute | solution.py:33
  303.8 15.2 %collective-permute-start.42 = (f32[1,32,2,128]{3,1,2,0:T(8,128)S(1)}, f32[1,32,2,128]{3,1,2,0:T(8,128)S(1)}, u32[]{:S(2)}, u32[]{:S(2)}) collective-permute-start(f32[1,32,2,128]{3,1,2,0:T(8,128)S(1)} %get-tuple-element.63), channel_id=1, source_target_pairs={{0,2},{1,3},{2,0},{3,1},{4,6},{5,7},{6,4},{7,5},{8,10},{9,11},{10,... | collective-permute-start | bytes 98312 | tf_op jit(solution)/shard_map/ppermute | solution.py:33
  364.9 18.5 %collective-permute-start.53 = (f32[1,32,2,128]{3,1,2,0:T(8,128)S(1)}, f32[1,32,2,128]{3,1,2,0:T(8,128)S(1)}, u32[]{:S(2)}, u32[]{:S(2)}) collective-permute-start(f32[1,32,2,128]{3,1,2,0:T(8,128)S(1)} %maximum_add_fusion.6), channel_id=1, source_target_pairs={{0,1},{1,2},{2,3},{3,0},{4,5},{5,6},{6,7},{7,4},{8,9},{9,10},{10,1... | collective-permute-start | bytes 98312 | tf_op jit(solution)/shard_map/ppermute | solution.py:33
  368.9 14.6 %collective-permute-start.52 = (f32[1,32,2,128]{3,1,2,0:T(8,128)S(1)}, f32[1,32,2,128]{3,1,2,0:T(8,128)S(1)}, u32[]{:S(2)}, u32[]{:S(2)}) collective-permute-start(f32[1,32,2,128]{3,1,2,0:T(8,128)S(1)} %maximum_add_fusion.6), channel_id=1, source_target_pairs={{0,2},{1,3},{2,0},{3,1},{4,6},{5,7},{6,4},{7,5},{8,10},{9,11},{10,... | collective-permute-start | bytes 98312 | tf_op jit(solution)/shard_map/ppermute | solution.py:33
  417.6 48.3 %collective-permute-start.71 = (f32[96,2,2048]{2,1,0:T(2,128)}, f32[96,2,2048]{2,1,0:T(2,128)}, u32[]{:S(2)}, u32[]{:S(2)}) collective-permute-start(f32[96,2,2048]{2,1,0:T(2,128)} %bitcast.177), channel_id=1, source_target_pairs={{0,64},{64,0},{128,192},{192,128},{256,320},{320,256},{384,448},{4... | collective-permute-start | bytes 4718600 | tf_op jit(solution)/shard_map/ppermute | solution.py:10
  431.7 21.4 %collective-permute-start.63 = (f32[1,32,2,128]{3,1,2,0:T(8,128)S(1)}, f32[1,32,2,128]{3,1,2,0:T(8,128)S(1)}, u32[]{:S(2)}, u32[]{:S(2)}) collective-permute-start(f32[1,32,2,128]{3,1,2,0:T(8,128)S(1)} %get-tuple-element.61), channel_id=1, source_target_pairs={{0,1},{1,2},{2,3},{3,0},{4,5},{5,6},{6,7},{7,4},{8,9},{9,10},{10,1... | collective-permute-start | bytes 98312 | tf_op jit(solution)/shard_map/ppermute | solution.py:33
  437.1 16.0 %collective-permute-start.62 = (f32[1,32,2,128]{3,1,2,0:T(8,128)S(1)}, f32[1,32,2,128]{3,1,2,0:T(8,128)S(1)}, u32[]{:S(2)}, u32[]{:S(2)}) collective-permute-start(f32[1,32,2,128]{3,1,2,0:T(8,128)S(1)} %get-tuple-element.61), channel_id=1, source_target_pairs={{0,2},{1,3},{2,0},{3,1},{4,6},{5,7},{6,4},{7,5},{8,10},{9,11},{10,... | collective-permute-start | bytes 98312 | tf_op jit(solution)/shard_map/ppermute | solution.py:33
  455.6 13.9 %collective-permute-start.65 = (f32[4,1,32,2,128]{4,2,3,0,1:T(8,128)S(1)}, f32[4,1,32,2,128]{4,2,3,0,1:T(8,128)S(1)}, u32[]{:S(2)}, u32[]{:S(2)}) collective-permute-start(f32[4,1,32,2,128]{4,2,3,0,1:T(8,128)S(1)} %get-tuple-element.40), channel_id=1, source_target_pairs={{0,8},{1,9},{2,10},{3,11},{4,12},{5,13},{6,14},{7,15},{8,0},{9,1},... | collective-permute-start | bytes 393224 | tf_op jit(solution)/shard_map/ppermute | solution.py:33
  469.7 21.0 %collective-permute-start.68 = (f32[4,4,1,32,2,128]{5,3,4,1,2,0:T(8,128)S(1)}, f32[4,4,1,32,2,128]{5,3,4,1,2,0:T(8,128)S(1)}, u32[]{:S(2)}, u32[]{:S(2)}) collective-permute-start(f32[4,4,1,32,2,128]{5,3,4,1,2,0:T(8,128)S(1)} %get-tuple-element.16), channel_id=1, source_target_pairs={{0,16},{1,17},{2,18},{3,19},{4,20},{5,21},{6,22},{7,23},{8,24},{9,... | collective-permute-start | bytes 1572872 | tf_op jit(solution)/shard_map/ppermute | solution.py:33
  471.6 13.5 %collective-permute-start.67 = (f32[4,4,1,32,2,128]{5,3,4,1,0,2:T(8,128)S(1)}, f32[4,4,1,32,2,128]{5,3,4,1,0,2:T(8,128)S(1)}, u32[]{:S(2)}, u32[]{:S(2)}) collective-permute-start(f32[4,4,1,32,2,128]{5,3,4,1,0,2:T(8,128)S(1)} %get-tuple-element.15), channel_id=1, source_target_pairs={{0,48},{1,49},{2,50},{3,51},{4,52},{5,53},{6,54},{7,55},{8,56},{9,... | collective-permute-start | bytes 1572872 | tf_op jit(solution)/shard_map/ppermute | solution.py:33
  (53 other events, 526.6 us)

commit v4 on v3

--- a/solution.py
+++ b/solution.py
@@ -59,7 +59,7 @@
     for stride in (16, 4, 1):
         offset = (target // stride % 4 - me // stride % 4) % 4
         slot = slot + offset * stride
-    out = jnp.take(blocks, slot, axis=0)
+    out = jnp.take(blocks, slot, axis=0, mode="clip")
     return out.reshape((64 * piece.shape[0],) + piece.shape[1:])
 
 
@@ -75,7 +75,8 @@
     width_panel = own_shared.shape[0]
     panel_index = lax.axis_index("panel")
     own_rows = lax.dynamic_slice_in_dim(start_rows, panel_index * width_panel, width_panel, 0)
-    other_form, other_crossing = swapped((own_shared, own_crossing), "box", 0)
+    other_form = swapped(own_shared, "box", 0)
+    other_crossing = swapped(own_crossing, "box", 0)
 
     def through_own(gathered_piece):
         return slice_product(own_shared, gathered_piece)

time: 521 us -> 519 us (level)
  other arithmetic: 17.9 us -> 5.35 us
  local copies, waits for them, and re-layouts: 30.1 us -> 41.1 us
    select_n x7 -> x0, other arithmetic: 12.6 us -> none  [panel_gather(): out = jnp.take(blocks, slot, axis=0)]
    gather x7 -> x14, local copies, waits for them, and re-layouts: 13.9 us -> 26.3 us  [panel_gather(): out = jnp.take(blocks, slot, axis=0, mode='clip')]
where the time goes in v4:
time: 519 us; the launch traced here: 509 us
  starting transfers between devices  282 us (54%)
  waiting for transfers between devices  147 us (28%)
  local copies, waits for them, and re-layouts  41.1 us (8%)
  matrix products  31 us (6%)
  other arithmetic  5.35 us (1%)
    ppermute x70, starting transfers between devices, shifted_along(): return lax.ppermute(piece, 'panel', pairs)  278 us
    ppermute x70, waiting for transfers between devices, shifted_along(): return lax.ppermute(piece, 'panel', pairs)  147 us
    gather x14, local copies, waits for them, and re-layouts, panel_gather(): out = jnp.take(blocks, slot, axis=0, mode='clip')  26.3 us
  transfers between devices with their start and end apart: 72, of which 44 were waited for; matrix products, arithmetic and copies ran while one was open for 5% of the time, Pallas kernels for 0%

profile of v4, /device:TPU:6, one launch (start us, length us, event | category | flops | bytes accessed | tf_op | source)
XLA Modules:
  0.0 508.9 jit_solution(8247796976646855675)
XLA Ops:
  9.3 9.1 %collective-permute-start.3 = (f32[1,32,2,128]{3,1,2,0:T(8,128)S(1)}, f32[1,32,2,128]{3,1,2,0:T(8,128)S(1)}, u32[]{:S(2)}, u32[]{:S(2)}) collective-permute-start(f32[1,32,2,128]{3,1,2,0:T(8,128)S(1)} %get-tuple-element.64), channel_id=1, source_target_pairs={{0,1},{1,2},{2,3},{3,0},{4,5},{5,6},{6,7},{7,4},{8,9},{9,10},{10,1... | collective-permute-start | bytes 98312 | tf_op jit(solution)/shard_map/ppermute | solution.py:33
  18.4 10.9 %collective-permute-start.2 = (f32[1,32,2,128]{3,1,2,0:T(8,128)S(1)}, f32[1,32,2,128]{3,1,2,0:T(8,128)S(1)}, u32[]{:S(2)}, u32[]{:S(2)}) collective-permute-start(f32[1,32,2,128]{3,1,2,0:T(8,128)S(1)} %get-tuple-element.64), channel_id=1, source_target_pairs={{0,2},{1,3},{2,0},{3,1},{4,6},{5,7},{6,4},{7,5},{8,10},{9,11},{10,... | collective-permute-start | bytes 98312 | tf_op jit(solution)/shard_map/ppermute | solution.py:33
  29.3 5.5 %collective-permute-start.1 = (f32[1,32,2,128]{3,1,2,0:T(8,128)S(1)}, f32[1,32,2,128]{3,1,2,0:T(8,128)S(1)}, u32[]{:S(2)}, u32[]{:S(2)}) collective-permute-start(f32[1,32,2,128]{3,1,2,0:T(8,128)S(1)} %get-tuple-element.64), channel_id=1, source_target_pairs={{0,3},{1,0},{2,1},{3,2},{4,7},{5,4},{6,5},{7,6},{8,11},{9,8},{10,9... | collective-permute-start | bytes 98312 | tf_op jit(solution)/shard_map/ppermute | solution.py:33
  63.3 6.4 %collective-permute-done.7 = f32[4,4,1,32,2,128]{5,3,4,1,0,2:T(8,128)S(1)} collective-permute-done((f32[4,4,1,32,2,128]{5,3,4,1,0,2:T(8,128)}, f32[4,4,1,32,2,128]{5,3,4,1,0,2:T(8,128)S(1)}, u32[]{:S(2)}, u32[]{:S(2)}) %collective-permute-start.7) | collective-permute-done | bytes 524320 | tf_op jit(solution)/shard_map/ppermute | solution.py:33
  69.7 5.5 %collective-permute-start.10 = (f32[2,4,1,32,2,128]{5,3,4,1,0,2:T(8,128)S(1)}, f32[2,4,1,32,2,128]{5,3,4,1,0,2:T(8,128)S(1)}, u32[]{:S(2)}, u32[]{:S(2)}) collective-permute-start(f32[2,4,1,32,2,128]{5,3,4,1,0,2:T(8,128)S(1)} %slice.219), channel_id=1, source_target_pairs={{0,48},{1,49},{2,50},{3,51},{4,52},{5,53},{6,54},{7,55},{8,56},{9,... | collective-permute-start | bytes 786440 | tf_op jit(solution)/shard_map/ppermute | solution.py:33
  79.1 5.7 %collective-permute-done.9 = f32[2,4,1,32,2,128]{5,3,4,1,0,2:T(8,128)S(1)} collective-permute-done((f32[2,4,1,32,2,128]{5,3,4,1,0,2:T(8,128)S(1)}, f32[2,4,1,32,2,128]{5,3,4,1,0,2:T(8,128)S(1)}, u32[]{:S(2)}, u32[]{:S(2)}) %collective-permute-start.9) | collective-permute-done | bytes 262176 | tf_op jit(solution)/shard_map/ppermute | solution.py:33
  96.5 9.3 %collective-permute-start.12 = (f32[1,32,2,128]{3,1,2,0:T(8,128)S(1)}, f32[1,32,2,128]{3,1,2,0:T(8,128)S(1)}, u32[]{:S(2)}, u32[]{:S(2)}) collective-permute-start(f32[1,32,2,128]{3,1,2,0:T(8,128)S(1)} %maximum_add_fusion.2), channel_id=1, source_target_pairs={{0,2},{1,3},{2,0},{3,1},{4,6},{5,7},{6,4},{7,5},{8,10},{9,11},{10,... | collective-permute-start | bytes 98312 | tf_op jit(solution)/shard_map/ppermute | solution.py:33
  134.9 8.0 %collective-permute-done.17 = f32[4,4,1,32,2,128]{5,3,4,1,0,2:T(8,128)S(1)} collective-permute-done((f32[4,4,1,32,2,128]{5,3,4,1,0,2:T(8,128)S(1)}, f32[4,4,1,32,2,128]{5,3,4,1,0,2:T(8,128)S(1)}, u32[]{:S(2)}, u32[]{:S(2)}) %collective-permute-start.17) | collective-permute-done | bytes 524320 | tf_op jit(solution)/shard_map/ppermute | solution.py:33
  167.5 7.6 %collective-permute-start.22 = (f32[1,32,2,128]{3,1,2,0:T(8,128)S(1)}, f32[1,32,2,128]{3,1,2,0:T(8,128)S(1)}, u32[]{:S(2)}, u32[]{:S(2)}) collective-permute-start(f32[1,32,2,128]{3,1,2,0:T(8,128)S(1)} %get-tuple-element.62), channel_id=1, source_target_pairs={{0,2},{1,3},{2,0},{3,1},{4,6},{5,7},{6,4},{7,5},{8,10},{9,11},{10,... | collective-permute-start | bytes 98312 | tf_op jit(solution)/shard_map/ppermute | solution.py:33
  205.2 5.2 %collective-permute-done.27 = f32[4,4,1,32,2,128]{5,3,4,1,0,2:T(8,128)S(1)} collective-permute-done((f32[4,4,1,32,2,128]{5,3,4,1,0,2:T(8,128)S(1)}, f32[4,4,1,32,2,128]{5,3,4,1,0,2:T(8,128)S(1)}, u32[]{:S(2)}, u32[]{:S(2)}) %collective-permute-start.27) | collective-permute-done | bytes 524320 | tf_op jit(solution)/shard_map/ppermute | solution.py:33
  235.0 6.2 %collective-permute-start.32 = (f32[1,32,2,128]{3,1,2,0:T(8,128)S(1)}, f32[1,32,2,128]{3,1,2,0:T(8,128)S(1)}, u32[]{:S(2)}, u32[]{:S(2)}) collective-permute-start(f32[1,32,2,128]{3,1,2,0:T(8,128)S(1)} %maximum_add_fusion.4), channel_id=1, source_target_pairs={{0,2},{1,3},{2,0},{3,1},{4,6},{5,7},{6,4},{7,5},{8,10},{9,11},{10,... | collective-permute-start | bytes 98312 | tf_op jit(solution)/shard_map/ppermute | solution.py:33
  241.2 5.5 %collective-permute-start.31 = (f32[1,32,2,128]{3,1,2,0:T(8,128)S(1)}, f32[1,32,2,128]{3,1,2,0:T(8,128)S(1)}, u32[]{:S(2)}, u32[]{:S(2)}) collective-permute-start(f32[1,32,2,128]{3,1,2,0:T(8,128)S(1)} %maximum_add_fusion.4), channel_id=1, source_target_pairs={{0,3},{1,0},{2,1},{3,2},{4,7},{5,4},{6,5},{7,6},{8,11},{9,8},{10,9... | collective-permute-start | bytes 98312 | tf_op jit(solution)/shard_map/ppermute | solution.py:33
  270.8 5.2 %collective-permute-done.37 = f32[4,4,1,32,2,128]{5,3,4,1,0,2:T(8,128)S(1)} collective-permute-done((f32[4,4,1,32,2,128]{5,3,4,1,0,2:T(8,128)S(1)}, f32[4,4,1,32,2,128]{5,3,4,1,0,2:T(8,128)S(1)}, u32[]{:S(2)}, u32[]{:S(2)}) %collective-permute-start.37) | collective-permute-done | bytes 524320 | tf_op jit(solution)/shard_map/ppermute | solution.py:33
  295.8 7.1 %collective-permute-start.43 = (f32[1,32,2,128]{3,1,2,0:T(8,128)S(1)}, f32[1,32,2,128]{3,1,2,0:T(8,128)S(1)}, u32[]{:S(2)}, u32[]{:S(2)}) collective-permute-start(f32[1,32,2,128]{3,1,2,0:T(8,128)S(1)} %get-tuple-element.60), channel_id=1, source_target_pairs={{0,1},{1,2},{2,3},{3,0},{4,5},{5,6},{6,7},{7,4},{8,9},{9,10},{10,1... | collective-permute-start | bytes 98312 | tf_op jit(solution)/shard_map/ppermute | solution.py:33
  302.9 5.9 %collective-permute-start.42 = (f32[1,32,2,128]{3,1,2,0:T(8,128)S(1)}, f32[1,32,2,128]{3,1,2,0:T(8,128)S(1)}, u32[]{:S(2)}, u32[]{:S(2)}) collective-permute-start(f32[1,32,2,128]{3,1,2,0:T(8,128)S(1)} %get-tuple-element.60), channel_id=1, source_target_pairs={{0,2},{1,3},{2,0},{3,1},{4,6},{5,7},{6,4},{7,5},{8,10},{9,11},{10,... | collective-permute-start | bytes 98312 | tf_op jit(solution)/shard_map/ppermute | solution.py:33
  338.8 5.2 %collective-permute-done.47 = f32[4,4,1,32,2,128]{5,3,4,1,0,2:T(8,128)S(1)} collective-permute-done((f32[4,4,1,32,2,128]{5,3,4,1,0,2:T(8,128)S(1)}, f32[4,4,1,32,2,128]{5,3,4,1,0,2:T(8,128)S(1)}, u32[]{:S(2)}, u32[]{:S(2)}) %collective-permute-start.47) | collective-permute-done | bytes 524320 | tf_op jit(solution)/shard_map/ppermute | solution.py:33
  367.8 8.2 %collective-permute-start.52 = (f32[1,32,2,128]{3,1,2,0:T(8,128)S(1)}, f32[1,32,2,128]{3,1,2,0:T(8,128)S(1)}, u32[]{:S(2)}, u32[]{:S(2)}) collective-permute-start(f32[1,32,2,128]{3,1,2,0:T(8,128)S(1)} %maximum_add_fusion.6), channel_id=1, source_target_pairs={{0,2},{1,3},{2,0},{3,1},{4,6},{5,7},{6,4},{7,5},{8,10},{9,11},{10,... | collective-permute-start | bytes 98312 | tf_op jit(solution)/shard_map/ppermute | solution.py:33
  376.0 6.2 %collective-permute-start.51 = (f32[1,32,2,128]{3,1,2,0:T(8,128)S(1)}, f32[1,32,2,128]{3,1,2,0:T(8,128)S(1)}, u32[]{:S(2)}, u32[]{:S(2)}) collective-permute-start(f32[1,32,2,128]{3,1,2,0:T(8,128)S(1)} %maximum_add_fusion.6), channel_id=1, source_target_pairs={{0,3},{1,0},{2,1},{3,2},{4,7},{5,4},{6,5},{7,6},{8,11},{9,8},{10,9... | collective-permute-start | bytes 98312 | tf_op jit(solution)/shard_map/ppermute | solution.py:33
  405.4 5.2 %collective-permute-done.57 = f32[4,4,1,32,2,128]{5,3,4,1,0,2:T(8,128)S(1)} collective-permute-done((f32[4,4,1,32,2,128]{5,3,4,1,0,2:T(8,128)S(1)}, f32[4,4,1,32,2,128]{5,3,4,1,0,2:T(8,128)S(1)}, u32[]{:S(2)}, u32[]{:S(2)}) %collective-permute-start.57) | collective-permute-done | bytes 524320 | tf_op jit(solution)/shard_map/ppermute | solution.py:33
  430.4 5.4 %collective-permute-start.63 = (f32[1,32,2,128]{3,1,2,0:T(8,128)S(1)}, f32[1,32,2,128]{3,1,2,0:T(8,128)S(1)}, u32[]{:S(2)}, u32[]{:S(2)}) collective-permute-start(f32[1,32,2,128]{3,1,2,0:T(8,128)S(1)} %get-tuple-element.58), channel_id=1, source_target_pairs={{0,1},{1,2},{2,3},{3,0},{4,5},{5,6},{6,7},{7,4},{8,9},{9,10},{10,1... | collective-permute-start | bytes 98312 | tf_op jit(solution)/shard_map/ppermute | solution.py:33
  435.8 8.3 %collective-permute-start.62 = (f32[1,32,2,128]{3,1,2,0:T(8,128)S(1)}, f32[1,32,2,128]{3,1,2,0:T(8,128)S(1)}, u32[]{:S(2)}, u32[]{:S(2)}) collective-permute-start(f32[1,32,2,128]{3,1,2,0:T(8,128)S(1)} %get-tuple-element.58), channel_id=1, source_target_pairs={{0,2},{1,3},{2,0},{3,1},{4,6},{5,7},{6,4},{7,5},{8,10},{9,11},{10,... | collective-permute-start | bytes 98312 | tf_op jit(solution)/shard_map/ppermute | solution.py:33
  470.3 5.1 %collective-permute-start.67 = (f32[4,4,1,32,2,128]{5,3,4,1,0,2:T(8,128)S(1)}, f32[4,4,1,32,2,128]{5,3,4,1,0,2:T(8,128)S(1)}, u32[]{:S(2)}, u32[]{:S(2)}) collective-permute-start(f32[4,4,1,32,2,128]{5,3,4,1,0,2:T(8,128)S(1)} %get-tuple-element.12), channel_id=1, source_target_pairs={{0,48},{1,49},{2,50},{3,51},{4,52},{5,53},{6,54},{7,55},{8,56},{9,... | collective-permute-start | bytes 1572872 | tf_op jit(solution)/shard_map/ppermute | solution.py:33
  483.8 5.6 %collective-permute-start.70 = (f32[2,4,1,32,2,128]{5,3,4,1,0,2:T(8,128)S(1)}, f32[2,4,1,32,2,128]{5,3,4,1,0,2:T(8,128)S(1)}, u32[]{:S(2)}, u32[]{:S(2)}) collective-permute-start(f32[2,4,1,32,2,128]{5,3,4,1,0,2:T(8,128)S(1)} %slice.245), channel_id=1, source_target_pairs={{0,48},{1,49},{2,50},{3,51},{4,52},{5,53},{6,54},{7,55},{8,56},{9,... | collective-permute-start | bytes 786440 | tf_op jit(solution)/shard_map/ppermute | solution.py:33
  493.2 5.6 %collective-permute-done.69 = f32[2,4,1,32,2,128]{5,3,4,1,0,2:T(8,128)S(1)} collective-permute-done((f32[2,4,1,32,2,128]{5,3,4,1,0,2:T(8,128)S(1)}, f32[2,4,1,32,2,128]{5,3,4,1,0,2:T(8,128)S(1)}, u32[]{:S(2)}, u32[]{:S(2)}) %collective-permute-start.69) | collective-permute-done | bytes 262176 | tf_op jit(solution)/shard_map/ppermute | solution.py:33
  (244 shorter events, 349.2 us)
Async XLA Ops:
  9.3 25.5 %collective-permute-start.3 = (f32[1,32,2,128]{3,1,2,0:T(8,128)S(1)}, f32[1,32,2,128]{3,1,2,0:T(8,128)S(1)}, u32[]{:S(2)}, u32[]{:S(2)}) collective-permute-start(f32[1,32,2,128]{3,1,2,0:T(8,128)S(1)} %get-tuple-element.64), channel_id=1, source_target_pairs={{0,1},{1,2},{2,3},{3,0},{4,5},{5,6},{6,7},{7,4},{8,9},{9,10},{10,1... | collective-permute-start | bytes 98312 | tf_op jit(solution)/shard_map/ppermute | solution.py:33
  18.4 16.4 %collective-permute-start.2 = (f32[1,32,2,128]{3,1,2,0:T(8,128)S(1)}, f32[1,32,2,128]{3,1,2,0:T(8,128)S(1)}, u32[]{:S(2)}, u32[]{:S(2)}) collective-permute-start(f32[1,32,2,128]{3,1,2,0:T(8,128)S(1)} %get-tuple-element.64), channel_id=1, source_target_pairs={{0,2},{1,3},{2,0},{3,1},{4,6},{5,7},{6,4},{7,5},{8,10},{9,11},{10,... | collective-permute-start | bytes 98312 | tf_op jit(solution)/shard_map/ppermute | solution.py:33
  55.9 13.7 %collective-permute-start.7 = (f32[4,4,1,32,2,128]{5,3,4,1,0,2:T(8,128)}, f32[4,4,1,32,2,128]{5,3,4,1,0,2:T(8,128)S(1)}, u32[]{:S(2)}, u32[]{:S(2)}) collective-permute-start(f32[4,4,1,32,2,128]{5,3,4,1,0,2:T(8,128)} %get-tuple-element.32), channel_id=1, source_target_pairs={{0,48},{1,49},{2,50},{3,51},{4,52},{5,53},{6,54},{7,55},{8,56},{9,... | collective-permute-start | bytes 1572872 | tf_op jit(solution)/shard_map/ppermute | solution.py:33
  60.9 14.4 %collective-permute-start.8 = (f32[4,4,1,32,2,128]{5,3,4,1,2,0:T(8,128)S(1)}, f32[4,4,1,32,2,128]{5,3,4,1,2,0:T(8,128)S(1)}, u32[]{:S(2)}, u32[]{:S(2)}) collective-permute-start(f32[4,4,1,32,2,128]{5,3,4,1,2,0:T(8,128)S(1)} %get-tuple-element.33), channel_id=1, source_target_pairs={{0,16},{1,17},{2,18},{3,19},{4,20},{5,21},{6,22},{7,23},{8,24},{9,... | collective-permute-start | bytes 1572872 | tf_op jit(solution)/shard_map/ppermute | solution.py:33
  93.2 16.8 %collective-permute-start.13 = (f32[1,32,2,128]{3,1,2,0:T(8,128)S(1)}, f32[1,32,2,128]{3,1,2,0:T(8,128)S(1)}, u32[]{:S(2)}, u32[]{:S(2)}) collective-permute-start(f32[1,32,2,128]{3,1,2,0:T(8,128)S(1)} %maximum_add_fusion.2), channel_id=1, source_target_pairs={{0,1},{1,2},{2,3},{3,0},{4,5},{5,6},{6,7},{7,4},{8,9},{9,10},{10,1... | collective-permute-start | bytes 98312 | tf_op jit(solution)/shard_map/ppermute | solution.py:33
  96.5 14.7 %collective-permute-start.12 = (f32[1,32,2,128]{3,1,2,0:T(8,128)S(1)}, f32[1,32,2,128]{3,1,2,0:T(8,128)S(1)}, u32[]{:S(2)}, u32[]{:S(2)}) collective-permute-start(f32[1,32,2,128]{3,1,2,0:T(8,128)S(1)} %maximum_add_fusion.2), channel_id=1, source_target_pairs={{0,2},{1,3},{2,0},{3,1},{4,6},{5,7},{6,4},{7,5},{8,10},{9,11},{10,... | collective-permute-start | bytes 98312 | tf_op jit(solution)/shard_map/ppermute | solution.py:33
  129.1 13.9 %collective-permute-start.17 = (f32[4,4,1,32,2,128]{5,3,4,1,0,2:T(8,128)S(1)}, f32[4,4,1,32,2,128]{5,3,4,1,0,2:T(8,128)S(1)}, u32[]{:S(2)}, u32[]{:S(2)}) collective-permute-start(f32[4,4,1,32,2,128]{5,3,4,1,0,2:T(8,128)S(1)} %get-tuple-element.27), channel_id=1, source_target_pairs={{0,48},{1,49},{2,50},{3,51},{4,52},{5,53},{6,54},{7,55},{8,56},{9,... | collective-permute-start | bytes 1572872 | tf_op jit(solution)/shard_map/ppermute | solution.py:33
  131.0 15.1 %collective-permute-start.18 = (f32[4,4,1,32,2,128]{5,3,4,1,2,0:T(8,128)S(1)}, f32[4,4,1,32,2,128]{5,3,4,1,2,0:T(8,128)S(1)}, u32[]{:S(2)}, u32[]{:S(2)}) collective-permute-start(f32[4,4,1,32,2,128]{5,3,4,1,2,0:T(8,128)S(1)} %get-tuple-element.28), channel_id=1, source_target_pairs={{0,16},{1,17},{2,18},{3,19},{4,20},{5,21},{6,22},{7,23},{8,24},{9,... | collective-permute-start | bytes 1572872 | tf_op jit(solution)/shard_map/ppermute | solution.py:33
  162.7 15.8 %collective-permute-start.23 = (f32[1,32,2,128]{3,1,2,0:T(8,128)S(1)}, f32[1,32,2,128]{3,1,2,0:T(8,128)S(1)}, u32[]{:S(2)}, u32[]{:S(2)}) collective-permute-start(f32[1,32,2,128]{3,1,2,0:T(8,128)S(1)} %get-tuple-element.62), channel_id=1, source_target_pairs={{0,1},{1,2},{2,3},{3,0},{4,5},{5,6},{6,7},{7,4},{8,9},{9,10},{10,1... | collective-permute-start | bytes 98312 | tf_op jit(solution)/shard_map/ppermute | solution.py:33
  167.5 14.6 %collective-permute-start.22 = (f32[1,32,2,128]{3,1,2,0:T(8,128)S(1)}, f32[1,32,2,128]{3,1,2,0:T(8,128)S(1)}, u32[]{:S(2)}, u32[]{:S(2)}) collective-permute-start(f32[1,32,2,128]{3,1,2,0:T(8,128)S(1)} %get-tuple-element.62), channel_id=1, source_target_pairs={{0,2},{1,3},{2,0},{3,1},{4,6},{5,7},{6,4},{7,5},{8,10},{9,11},{10,... | collective-permute-start | bytes 98312 | tf_op jit(solution)/shard_map/ppermute | solution.py:33
  201.3 12.3 %collective-permute-start.28 = (f32[4,4,1,32,2,128]{5,3,4,1,2,0:T(8,128)S(1)}, f32[4,4,1,32,2,128]{5,3,4,1,2,0:T(8,128)S(1)}, u32[]{:S(2)}, u32[]{:S(2)}) collective-permute-start(f32[4,4,1,32,2,128]{5,3,4,1,2,0:T(8,128)S(1)} %get-tuple-element.25), channel_id=1, source_target_pairs={{0,16},{1,17},{2,18},{3,19},{4,20},{5,21},{6,22},{7,23},{8,24},{9,... | collective-permute-start | bytes 1572872 | tf_op jit(solution)/shard_map/ppermute | solution.py:33
  230.2 16.4 %collective-permute-start.33 = (f32[1,32,2,128]{3,1,2,0:T(8,128)S(1)}, f32[1,32,2,128]{3,1,2,0:T(8,128)S(1)}, u32[]{:S(2)}, u32[]{:S(2)}) collective-permute-start(f32[1,32,2,128]{3,1,2,0:T(8,128)S(1)} %maximum_add_fusion.4), channel_id=1, source_target_pairs={{0,1},{1,2},{2,3},{3,0},{4,5},{5,6},{6,7},{7,4},{8,9},{9,10},{10,1... | collective-permute-start | bytes 98312 | tf_op jit(solution)/shard_map/ppermute | solution.py:33
  235.0 14.5 %collective-permute-start.32 = (f32[1,32,2,128]{3,1,2,0:T(8,128)S(1)}, f32[1,32,2,128]{3,1,2,0:T(8,128)S(1)}, u32[]{:S(2)}, u32[]{:S(2)}) collective-permute-start(f32[1,32,2,128]{3,1,2,0:T(8,128)S(1)} %maximum_add_fusion.4), channel_id=1, source_target_pairs={{0,2},{1,3},{2,0},{3,1},{4,6},{5,7},{6,4},{7,5},{8,10},{9,11},{10,... | collective-permute-start | bytes 98312 | tf_op jit(solution)/shard_map/ppermute | solution.py:33
  266.9 12.3 %collective-permute-start.38 = (f32[4,4,1,32,2,128]{5,3,4,1,2,0:T(8,128)S(1)}, f32[4,4,1,32,2,128]{5,3,4,1,2,0:T(8,128)S(1)}, u32[]{:S(2)}, u32[]{:S(2)}) collective-permute-start(f32[4,4,1,32,2,128]{5,3,4,1,2,0:T(8,128)S(1)} %get-tuple-element.22), channel_id=1, source_target_pairs={{0,16},{1,17},{2,18},{3,19},{4,20},{5,21},{6,22},{7,23},{8,24},{9,... | collective-permute-start | bytes 1572872 | tf_op jit(solution)/shard_map/ppermute | solution.py:33
  295.8 18.0 %collective-permute-start.43 = (f32[1,32,2,128]{3,1,2,0:T(8,128)S(1)}, f32[1,32,2,128]{3,1,2,0:T(8,128)S(1)}, u32[]{:S(2)}, u32[]{:S(2)}) collective-permute-start(f32[1,32,2,128]{3,1,2,0:T(8,128)S(1)} %get-tuple-element.60), channel_id=1, source_target_pairs={{0,1},{1,2},{2,3},{3,0},{4,5},{5,6},{6,7},{7,4},{8,9},{9,10},{10,1... | collective-permute-start | bytes 98312 | tf_op jit(solution)/shard_map/ppermute | solution.py:33
  302.9 15.2 %collective-permute-start.42 = (f32[1,32,2,128]{3,1,2,0:T(8,128)S(1)}, f32[1,32,2,128]{3,1,2,0:T(8,128)S(1)}, u32[]{:S(2)}, u32[]{:S(2)}) collective-permute-start(f32[1,32,2,128]{3,1,2,0:T(8,128)S(1)} %get-tuple-element.60), channel_id=1, source_target_pairs={{0,2},{1,3},{2,0},{3,1},{4,6},{5,7},{6,4},{7,5},{8,10},{9,11},{10,... | collective-permute-start | bytes 98312 | tf_op jit(solution)/shard_map/ppermute | solution.py:33
  363.8 18.5 %collective-permute-start.53 = (f32[1,32,2,128]{3,1,2,0:T(8,128)S(1)}, f32[1,32,2,128]{3,1,2,0:T(8,128)S(1)}, u32[]{:S(2)}, u32[]{:S(2)}) collective-permute-start(f32[1,32,2,128]{3,1,2,0:T(8,128)S(1)} %maximum_add_fusion.6), channel_id=1, source_target_pairs={{0,1},{1,2},{2,3},{3,0},{4,5},{5,6},{6,7},{7,4},{8,9},{9,10},{10,1... | collective-permute-start | bytes 98312 | tf_op jit(solution)/shard_map/ppermute | solution.py:33
  367.8 14.6 %collective-permute-start.52 = (f32[1,32,2,128]{3,1,2,0:T(8,128)S(1)}, f32[1,32,2,128]{3,1,2,0:T(8,128)S(1)}, u32[]{:S(2)}, u32[]{:S(2)}) collective-permute-start(f32[1,32,2,128]{3,1,2,0:T(8,128)S(1)} %maximum_add_fusion.6), channel_id=1, source_target_pairs={{0,2},{1,3},{2,0},{3,1},{4,6},{5,7},{6,4},{7,5},{8,10},{9,11},{10,... | collective-permute-start | bytes 98312 | tf_op jit(solution)/shard_map/ppermute | solution.py:33
  416.5 48.1 %collective-permute-start.71 = (f32[96,2,2048]{2,1,0:T(2,128)}, f32[96,2,2048]{2,1,0:T(2,128)}, u32[]{:S(2)}, u32[]{:S(2)}) collective-permute-start(f32[96,2,2048]{2,1,0:T(2,128)} %bitcast.178), channel_id=1, source_target_pairs={{0,64},{64,0},{128,192},{192,128},{256,320},{320,256},{384,448},{4... | collective-permute-start | bytes 4718600 | tf_op jit(solution)/shard_map/ppermute | solution.py:10
  430.4 21.4 %collective-permute-start.63 = (f32[1,32,2,128]{3,1,2,0:T(8,128)S(1)}, f32[1,32,2,128]{3,1,2,0:T(8,128)S(1)}, u32[]{:S(2)}, u32[]{:S(2)}) collective-permute-start(f32[1,32,2,128]{3,1,2,0:T(8,128)S(1)} %get-tuple-element.58), channel_id=1, source_target_pairs={{0,1},{1,2},{2,3},{3,0},{4,5},{5,6},{6,7},{7,4},{8,9},{9,10},{10,1... | collective-permute-start | bytes 98312 | tf_op jit(solution)/shard_map/ppermute | solution.py:33
  435.8 16.0 %collective-permute-start.62 = (f32[1,32,2,128]{3,1,2,0:T(8,128)S(1)}, f32[1,32,2,128]{3,1,2,0:T(8,128)S(1)}, u32[]{:S(2)}, u32[]{:S(2)}) collective-permute-start(f32[1,32,2,128]{3,1,2,0:T(8,128)S(1)} %get-tuple-element.58), channel_id=1, source_target_pairs={{0,2},{1,3},{2,0},{3,1},{4,6},{5,7},{6,4},{7,5},{8,10},{9,11},{10,... | collective-permute-start | bytes 98312 | tf_op jit(solution)/shard_map/ppermute | solution.py:33
  454.3 13.9 %collective-permute-start.65 = (f32[4,1,32,2,128]{4,2,3,0,1:T(8,128)S(1)}, f32[4,1,32,2,128]{4,2,3,0,1:T(8,128)S(1)}, u32[]{:S(2)}, u32[]{:S(2)}) collective-permute-start(f32[4,1,32,2,128]{4,2,3,0,1:T(8,128)S(1)} %get-tuple-element.37), channel_id=1, source_target_pairs={{0,8},{1,9},{2,10},{3,11},{4,12},{5,13},{6,14},{7,15},{8,0},{9,1},... | collective-permute-start | bytes 393224 | tf_op jit(solution)/shard_map/ppermute | solution.py:33
  468.3 21.0 %collective-permute-start.68 = (f32[4,4,1,32,2,128]{5,3,4,1,2,0:T(8,128)S(1)}, f32[4,4,1,32,2,128]{5,3,4,1,2,0:T(8,128)S(1)}, u32[]{:S(2)}, u32[]{:S(2)}) collective-permute-start(f32[4,4,1,32,2,128]{5,3,4,1,2,0:T(8,128)S(1)} %get-tuple-element.13), channel_id=1, source_target_pairs={{0,16},{1,17},{2,18},{3,19},{4,20},{5,21},{6,22},{7,23},{8,24},{9,... | collective-permute-start | bytes 1572872 | tf_op jit(solution)/shard_map/ppermute | solution.py:33
  470.3 13.5 %collective-permute-start.67 = (f32[4,4,1,32,2,128]{5,3,4,1,0,2:T(8,128)S(1)}, f32[4,4,1,32,2,128]{5,3,4,1,0,2:T(8,128)S(1)}, u32[]{:S(2)}, u32[]{:S(2)}) collective-permute-start(f32[4,4,1,32,2,128]{5,3,4,1,0,2:T(8,128)S(1)} %get-tuple-element.12), channel_id=1, source_target_pairs={{0,48},{1,49},{2,50},{3,51},{4,52},{5,53},{6,54},{7,55},{8,56},{9,... | collective-permute-start | bytes 1572872 | tf_op jit(solution)/shard_map/ppermute | solution.py:33
  (53 other events, 526.6 us)

commit v5 on v4

--- a/solution.py
+++ b/solution.py
@@ -39,17 +39,19 @@
          shifted_along(blocks, stride, 1)], 0)
 
 
-def relay_stage(blocks, stride):
+def relay_stage(blocks, stride, axis=0):
     from_below = shifted_along(blocks, stride, 1)
     from_above = shifted_along(blocks, stride, 3)
-    half = blocks.shape[0] // 2
+    half = blocks.shape[axis] // 2
     opposite = jnp.concatenate(
-        [shifted_along(from_below[:half], stride, 1), shifted_along(from_above[half:], stride, 3)], 0)
+        [shifted_along(lax.slice_in_dim(from_below, 0, half, axis=axis), stride, 1),
+         shifted_along(lax.slice_in_dim(from_above, half, blocks.shape[axis], axis=axis), stride, 3)],
+        axis)
     return jnp.stack([blocks, from_above, opposite, from_below], 0)
 
 
 def panel_gather(piece):
-    blocks = direct_stage(piece[None], 1)
+    blocks = relay_stage(piece[None], 1, axis=1)
     blocks = direct_stage(blocks, 4)
     blocks = relay_stage(blocks, 16)
     blocks = blocks.reshape((64,) + piece.shape)

time: 519 us -> 539 us (1.039)
  the two profiles are of different devices: /device:TPU:6 before, /device:TPU:32 now
where the time goes in v5:
time: 539 us; the launch traced here: 528 us
  starting transfers between devices  299 us (55%)
  waiting for transfers between devices  150 us (28%)
  local copies, waits for them, and re-layouts  41.3 us (8%)
  matrix products  31 us (6%)
  other arithmetic  5.42 us (1%)
    ppermute x77, starting transfers between devices, shifted_along(): return lax.ppermute(piece, 'panel', pairs)  295 us
    ppermute x77, waiting for transfers between devices, shifted_along(): return lax.ppermute(piece, 'panel', pairs)  150 us
    gather x14, local copies, waits for them, and re-layouts, panel_gather(): out = jnp.take(blocks, slot, axis=0, mode='clip')  26.5 us
  transfers between devices with their start and end apart: 79, of which 44 were waited for; matrix products, arithmetic and copies ran while one was open for 5% of the time, Pallas kernels for 0%

profile of v5, /device:TPU:32, one launch (start us, length us, event | category | flops | bytes accessed | tf_op | source)
XLA Modules:
  0.0 528.3 jit_solution(11879478491831907724)
XLA Ops:
  9.3 11.8 %collective-permute-start.1 = (f32[1,32,2,128]{3,1,2,0:T(8,128)S(1)}, f32[1,32,2,128]{3,1,2,0:T(8,128)S(1)}, u32[]{:S(2)}, u32[]{:S(2)}) collective-permute-start(f32[1,32,2,128]{3,1,2,0:T(8,128)S(1)} %get-tuple-element.64), channel_id=1, source_target_pairs={{0,3},{1,0},{2,1},{3,2},{4,7},{5,4},{6,5},{7,6},{8,11},{9,8},{10,9... | collective-permute-start | bytes 98312 | tf_op jit(solution)/shard_map/ppermute | solution.py:33
  24.3 8.3 %collective-permute-start.4 = (f32[1,16,2,128]{3,1,2,0:T(8,128)S(1)}, f32[1,16,2,128]{3,1,2,0:T(8,128)S(1)}, u32[]{:S(2)}, u32[]{:S(2)}) collective-permute-start(f32[1,16,2,128]{3,1,2,0:T(8,128)S(1)} %slice.275), channel_id=1, source_target_pairs={{0,3},{1,0},{2,1},{3,2},{4,7},{5,4},{6,5},{7,6},{8,11},{9,8},{10,9... | collective-permute-start | bytes 49160 | tf_op jit(solution)/shard_map/ppermute | solution.py:33
  34.5 7.6 %collective-permute-done.3 = f32[1,16,2,128]{3,1,2,0:T(8,128)S(1)} collective-permute-done((f32[1,16,2,128]{3,1,2,0:T(8,128)S(1)}, f32[1,16,2,128]{3,1,2,0:T(8,128)S(1)}, u32[]{:S(2)}, u32[]{:S(2)}) %collective-permute-start.3) | collective-permute-done | bytes 16416 | tf_op jit(solution)/shard_map/ppermute | solution.py:33
  65.4 6.0 %collective-permute-done.8 = f32[4,4,1,32,2,128]{5,3,4,1,0,2:T(8,128)S(1)} collective-permute-done((f32[4,4,1,32,2,128]{5,3,4,1,0,2:T(8,128)}, f32[4,4,1,32,2,128]{5,3,4,1,0,2:T(8,128)S(1)}, u32[]{:S(2)}, u32[]{:S(2)}) %collective-permute-start.8) | collective-permute-done | bytes 524320 | tf_op jit(solution)/shard_map/ppermute | solution.py:33
  71.4 5.5 %collective-permute-start.11 = (f32[2,4,1,32,2,128]{5,3,4,1,0,2:T(8,128)S(1)}, f32[2,4,1,32,2,128]{5,3,4,1,0,2:T(8,128)S(1)}, u32[]{:S(2)}, u32[]{:S(2)}) collective-permute-start(f32[2,4,1,32,2,128]{5,3,4,1,0,2:T(8,128)S(1)} %slice.277), channel_id=1, source_target_pairs={{0,48},{1,49},{2,50},{3,51},{4,52},{5,53},{6,54},{7,55},{8,56},{9,... | collective-permute-start | bytes 786440 | tf_op jit(solution)/shard_map/ppermute | solution.py:33
  80.7 5.7 %collective-permute-done.10 = f32[2,4,1,32,2,128]{5,3,4,1,0,2:T(8,128)S(1)} collective-permute-done((f32[2,4,1,32,2,128]{5,3,4,1,0,2:T(8,128)S(1)}, f32[2,4,1,32,2,128]{5,3,4,1,0,2:T(8,128)S(1)}, u32[]{:S(2)}, u32[]{:S(2)}) %collective-permute-start.10) | collective-permute-done | bytes 262176 | tf_op jit(solution)/shard_map/ppermute | solution.py:33
  94.9 5.4 %collective-permute-start.12 = (f32[1,32,2,128]{3,1,2,0:T(8,128)S(1)}, f32[1,32,2,128]{3,1,2,0:T(8,128)S(1)}, u32[]{:S(2)}, u32[]{:S(2)}) collective-permute-start(f32[1,32,2,128]{3,1,2,0:T(8,128)S(1)} %maximum_add_fusion.2), channel_id=1, source_target_pairs={{0,3},{1,0},{2,1},{3,2},{4,7},{5,4},{6,5},{7,6},{8,11},{9,8},{10,9... | collective-permute-start | bytes 98312 | tf_op jit(solution)/shard_map/ppermute | solution.py:33
  104.7 5.4 %collective-permute-start.15 = (f32[1,16,2,128]{3,1,2,0:T(8,128)S(1)}, f32[1,16,2,128]{3,1,2,0:T(8,128)S(1)}, u32[]{:S(2)}, u32[]{:S(2)}) collective-permute-start(f32[1,16,2,128]{3,1,2,0:T(8,128)S(1)} %slice.283), channel_id=1, source_target_pairs={{0,3},{1,0},{2,1},{3,2},{4,7},{5,4},{6,5},{7,6},{8,11},{9,8},{10,9... | collective-permute-start | bytes 49160 | tf_op jit(solution)/shard_map/ppermute | solution.py:33
  114.7 6.2 %collective-permute-done.14 = f32[1,16,2,128]{3,1,2,0:T(8,128)S(1)} collective-permute-done((f32[1,16,2,128]{3,1,2,0:T(8,128)S(1)}, f32[1,16,2,128]{3,1,2,0:T(8,128)S(1)}, u32[]{:S(2)}, u32[]{:S(2)}) %collective-permute-start.14) | collective-permute-done | bytes 16416 | tf_op jit(solution)/shard_map/ppermute | solution.py:33
  140.5 7.5 %collective-permute-done.19 = f32[4,4,1,32,2,128]{5,3,4,1,0,2:T(8,128)S(1)} collective-permute-done((f32[4,4,1,32,2,128]{5,3,4,1,0,2:T(8,128)S(1)}, f32[4,4,1,32,2,128]{5,3,4,1,0,2:T(8,128)S(1)}, u32[]{:S(2)}, u32[]{:S(2)}) %collective-permute-start.19) | collective-permute-done | bytes 524320 | tf_op jit(solution)/shard_map/ppermute | solution.py:33
  170.7 7.3 %collective-permute-start.24 = (f32[1,32,2,128]{3,1,2,0:T(8,128)S(1)}, f32[1,32,2,128]{3,1,2,0:T(8,128)S(1)}, u32[]{:S(2)}, u32[]{:S(2)}) collective-permute-start(f32[1,32,2,128]{3,1,2,0:T(8,128)S(1)} %get-tuple-element.62), channel_id=1, source_target_pairs={{0,1},{1,2},{2,3},{3,0},{4,5},{5,6},{6,7},{7,4},{8,9},{9,10},{10,1... | collective-permute-start | bytes 98312 | tf_op jit(solution)/shard_map/ppermute | solution.py:33
  180.7 7.1 %collective-permute-start.25 = (f32[1,16,2,128]{3,1,2,0:T(8,128)S(1)}, f32[1,16,2,128]{3,1,2,0:T(8,128)S(1)}, u32[]{:S(2)}, u32[]{:S(2)}) collective-permute-start(f32[1,16,2,128]{3,1,2,0:T(8,128)S(1)} %slice.288), channel_id=1, source_target_pairs={{0,1},{1,2},{2,3},{3,0},{4,5},{5,6},{6,7},{7,4},{8,9},{9,10},{10,1... | collective-permute-start | bytes 49160 | tf_op jit(solution)/shard_map/ppermute | solution.py:33
  209.5 5.2 collective-permute-done.30
  278.6 5.2 collective-permute-done.41
  303.6 7.3 %collective-permute-start.45 = (f32[1,32,2,128]{3,1,2,0:T(8,128)S(1)}, f32[1,32,2,128]{3,1,2,0:T(8,128)S(1)}, u32[]{:S(2)}, u32[]{:S(2)}) collective-permute-start(f32[1,32,2,128]{3,1,2,0:T(8,128)S(1)} %get-tuple-element.60), channel_id=1, source_target_pairs={{0,3},{1,0},{2,1},{3,2},{4,7},{5,4},{6,5},{7,6},{8,11},{9,8},{10,9... | collective-permute-start | bytes 98312 | tf_op jit(solution)/shard_map/ppermute | solution.py:33
  313.3 7.3 %collective-permute-start.48 = (f32[1,16,2,128]{3,1,2,0:T(8,128)S(1)}, f32[1,16,2,128]{3,1,2,0:T(8,128)S(1)}, u32[]{:S(2)}, u32[]{:S(2)}) collective-permute-start(f32[1,16,2,128]{3,1,2,0:T(8,128)S(1)} %slice.301), channel_id=1, source_target_pairs={{0,3},{1,0},{2,1},{3,2},{4,7},{5,4},{6,5},{7,6},{8,11},{9,8},{10,9... | collective-permute-start | bytes 49160 | tf_op jit(solution)/shard_map/ppermute | solution.py:33
  323.1 7.2 %collective-permute-done.47 = f32[1,16,2,128]{3,1,2,0:T(8,128)S(1)} collective-permute-done((f32[1,16,2,128]{3,1,2,0:T(8,128)S(1)}, f32[1,16,2,128]{3,1,2,0:T(8,128)S(1)}, u32[]{:S(2)}, u32[]{:S(2)}) %collective-permute-start.47) | collective-permute-done | bytes 16416 | tf_op jit(solution)/shard_map/ppermute | solution.py:33
  375.8 7.8 %collective-permute-start.56 = (f32[1,32,2,128]{3,1,2,0:T(8,128)S(1)}, f32[1,32,2,128]{3,1,2,0:T(8,128)S(1)}, u32[]{:S(2)}, u32[]{:S(2)}) collective-permute-start(f32[1,32,2,128]{3,1,2,0:T(8,128)S(1)} %maximum_add_fusion.6), channel_id=1, source_target_pairs={{0,3},{1,0},{2,1},{3,2},{4,7},{5,4},{6,5},{7,6},{8,11},{9,8},{10,9... | collective-permute-start | bytes 98312 | tf_op jit(solution)/shard_map/ppermute | solution.py:33
  385.6 7.8 %collective-permute-start.59 = (f32[1,16,2,128]{3,1,2,0:T(8,128)S(1)}, f32[1,16,2,128]{3,1,2,0:T(8,128)S(1)}, u32[]{:S(2)}, u32[]{:S(2)}) collective-permute-start(f32[1,16,2,128]{3,1,2,0:T(8,128)S(1)} %slice.307), channel_id=1, source_target_pairs={{0,3},{1,0},{2,1},{3,2},{4,7},{5,4},{6,5},{7,6},{8,11},{9,8},{10,9... | collective-permute-start | bytes 49160 | tf_op jit(solution)/shard_map/ppermute | solution.py:33
  395.9 7.6 %collective-permute-done.58 = f32[1,16,2,128]{3,1,2,0:T(8,128)S(1)} collective-permute-done((f32[1,16,2,128]{3,1,2,0:T(8,128)S(1)}, f32[1,16,2,128]{3,1,2,0:T(8,128)S(1)}, u32[]{:S(2)}, u32[]{:S(2)}) %collective-permute-start.58) | collective-permute-done | bytes 16416 | tf_op jit(solution)/shard_map/ppermute | solution.py:33
  450.1 7.8 %collective-permute-start.68 = (f32[1,32,2,128]{3,1,2,0:T(8,128)S(1)}, f32[1,32,2,128]{3,1,2,0:T(8,128)S(1)}, u32[]{:S(2)}, u32[]{:S(2)}) collective-permute-start(f32[1,32,2,128]{3,1,2,0:T(8,128)S(1)} %get-tuple-element.58), channel_id=1, source_target_pairs={{0,1},{1,2},{2,3},{3,0},{4,5},{5,6},{6,7},{7,4},{8,9},{9,10},{10,1... | collective-permute-start | bytes 98312 | tf_op jit(solution)/shard_map/ppermute | solution.py:33
  460.9 7.5 %collective-permute-start.69 = (f32[1,16,2,128]{3,1,2,0:T(8,128)S(1)}, f32[1,16,2,128]{3,1,2,0:T(8,128)S(1)}, u32[]{:S(2)}, u32[]{:S(2)}) collective-permute-start(f32[1,16,2,128]{3,1,2,0:T(8,128)S(1)} %slice.312), channel_id=1, source_target_pairs={{0,1},{1,2},{2,3},{3,0},{4,5},{5,6},{6,7},{7,4},{8,9},{9,10},{10,1... | collective-permute-start | bytes 49160 | tf_op jit(solution)/shard_map/ppermute | solution.py:33
  503.1 5.6 %collective-permute-start.77 = (f32[2,4,1,32,2,128]{5,3,4,1,0,2:T(8,128)S(1)}, f32[2,4,1,32,2,128]{5,3,4,1,0,2:T(8,128)S(1)}, u32[]{:S(2)}, u32[]{:S(2)}) collective-permute-start(f32[2,4,1,32,2,128]{5,3,4,1,0,2:T(8,128)S(1)} %slice.315), channel_id=1, source_target_pairs={{0,48},{1,49},{2,50},{3,51},{4,52},{5,53},{6,54},{7,55},{8,56},{9,... | collective-permute-start | bytes 786440 | tf_op jit(solution)/shard_map/ppermute | solution.py:33
  512.6 5.6 %collective-permute-done.76 = f32[2,4,1,32,2,128]{5,3,4,1,0,2:T(8,128)S(1)} collective-permute-done((f32[2,4,1,32,2,128]{5,3,4,1,0,2:T(8,128)S(1)}, f32[2,4,1,32,2,128]{5,3,4,1,0,2:T(8,128)S(1)}, u32[]{:S(2)}, u32[]{:S(2)}) %collective-permute-start.76) | collective-permute-done | bytes 262176 | tf_op jit(solution)/shard_map/ppermute | solution.py:33
  (279 shorter events, 360.6 us)
Async XLA Ops:
  9.3 15.0 %collective-permute-start.1 = (f32[1,32,2,128]{3,1,2,0:T(8,128)S(1)}, f32[1,32,2,128]{3,1,2,0:T(8,128)S(1)}, u32[]{:S(2)}, u32[]{:S(2)}) collective-permute-start(f32[1,32,2,128]{3,1,2,0:T(8,128)S(1)} %get-tuple-element.64), channel_id=1, source_target_pairs={{0,3},{1,0},{2,1},{3,2},{4,7},{5,4},{6,5},{7,6},{8,11},{9,8},{10,9... | collective-permute-start | bytes 98312 | tf_op jit(solution)/shard_map/ppermute | solution.py:33
  21.2 11.4 %collective-permute-start.2 = (f32[1,32,2,128]{3,1,2,0:T(8,128)S(1)}, f32[1,32,2,128]{3,1,2,0:T(8,128)S(1)}, u32[]{:S(2)}, u32[]{:S(2)}) collective-permute-start(f32[1,32,2,128]{3,1,2,0:T(8,128)S(1)} %get-tuple-element.64), channel_id=1, source_target_pairs={{0,1},{1,2},{2,3},{3,0},{4,5},{5,6},{6,7},{7,4},{8,9},{9,10},{10,1... | collective-permute-start | bytes 98312 | tf_op jit(solution)/shard_map/ppermute | solution.py:33
  42.2 11.2 %collective-permute-start.7 = (f32[4,1,32,2,128]{4,2,3,1,0:T(8,128)S(1)}, f32[4,1,32,2,128]{4,2,3,1,0:T(8,128)S(1)}, u32[]{:S(2)}, u32[]{:S(2)}) collective-permute-start(f32[4,1,32,2,128]{4,2,3,1,0:T(8,128)S(1)} %get-tuple-element.56), channel_id=1, source_target_pairs={{0,4},{1,5},{2,6},{3,7},{4,8},{5,9},{6,10},{7,11},{8,12},{9,13},{1... | collective-permute-start | bytes 393224 | tf_op jit(solution)/shard_map/ppermute | solution.py:33
  58.0 13.3 %collective-permute-start.8 = (f32[4,4,1,32,2,128]{5,3,4,1,0,2:T(8,128)}, f32[4,4,1,32,2,128]{5,3,4,1,0,2:T(8,128)S(1)}, u32[]{:S(2)}, u32[]{:S(2)}) collective-permute-start(f32[4,4,1,32,2,128]{5,3,4,1,0,2:T(8,128)} %get-tuple-element.32), channel_id=1, source_target_pairs={{0,48},{1,49},{2,50},{3,51},{4,52},{5,53},{6,54},{7,55},{8,56},{9,... | collective-permute-start | bytes 1572872 | tf_op jit(solution)/shard_map/ppermute | solution.py:33
  63.0 13.9 %collective-permute-start.9 = (f32[4,4,1,32,2,128]{5,3,4,1,2,0:T(8,128)S(1)}, f32[4,4,1,32,2,128]{5,3,4,1,2,0:T(8,128)S(1)}, u32[]{:S(2)}, u32[]{:S(2)}) collective-permute-start(f32[4,4,1,32,2,128]{5,3,4,1,2,0:T(8,128)S(1)} %get-tuple-element.33), channel_id=1, source_target_pairs={{0,16},{1,17},{2,18},{3,19},{4,20},{5,21},{6,22},{7,23},{8,24},{9,... | collective-permute-start | bytes 1572872 | tf_op jit(solution)/shard_map/ppermute | solution.py:33
  100.3 10.8 %collective-permute-start.13 = (f32[1,32,2,128]{3,1,2,0:T(8,128)S(1)}, f32[1,32,2,128]{3,1,2,0:T(8,128)S(1)}, u32[]{:S(2)}, u32[]{:S(2)}) collective-permute-start(f32[1,32,2,128]{3,1,2,0:T(8,128)S(1)} %maximum_add_fusion.2), channel_id=1, source_target_pairs={{0,1},{1,2},{2,3},{3,0},{4,5},{5,6},{6,7},{7,4},{8,9},{9,10},{10,1... | collective-permute-start | bytes 98312 | tf_op jit(solution)/shard_map/ppermute | solution.py:33
  134.6 13.4 %collective-permute-start.19 = (f32[4,4,1,32,2,128]{5,3,4,1,0,2:T(8,128)S(1)}, f32[4,4,1,32,2,128]{5,3,4,1,0,2:T(8,128)S(1)}, u32[]{:S(2)}, u32[]{:S(2)}) collective-permute-start(f32[4,4,1,32,2,128]{5,3,4,1,0,2:T(8,128)S(1)} %get-tuple-element.27), channel_id=1, source_target_pairs={{0,48},{1,49},{2,50},{3,51},{4,52},{5,53},{6,54},{7,55},{8,56},{9,... | collective-permute-start | bytes 1572872 | tf_op jit(solution)/shard_map/ppermute | solution.py:33
  136.6 15.1 %collective-permute-start.20 = (f32[4,4,1,32,2,128]{5,3,4,1,2,0:T(8,128)S(1)}, f32[4,4,1,32,2,128]{5,3,4,1,2,0:T(8,128)S(1)}, u32[]{:S(2)}, u32[]{:S(2)}) collective-permute-start(f32[4,4,1,32,2,128]{5,3,4,1,2,0:T(8,128)S(1)} %get-tuple-element.28), channel_id=1, source_target_pairs={{0,16},{1,17},{2,18},{3,19},{4,20},{5,21},{6,22},{7,23},{8,24},{9,... | collective-permute-start | bytes 1572872 | tf_op jit(solution)/shard_map/ppermute | solution.py:33
  203.7 11.1 %collective-permute-start.30 = (f32[4,4,1,32,2,128]{5,3,4,1,0,2:T(8,128)S(1)}, f32[4,4,1,32,2,128]{5,3,4,1,0,2:T(8,128)S(1)}, u32[]{:S(2)}, u32[]{:S(2)}) collective-permute-start(f32[4,4,1,32,2,128]{5,3,4,1,0,2:T(8,128)S(1)} %get-tuple-element.24), channel_id=1, source_target_pairs={{0,48},{1,49},{2,50},{3,51},{4,52},{5,53},{6,54},{7,55},{8,56},{9,... | collective-permute-start | bytes 1572872 | tf_op jit(solution)/shard_map/ppermute | solution.py:33
  205.6 12.3 %collective-permute-start.31 = (f32[4,4,1,32,2,128]{5,3,4,1,2,0:T(8,128)S(1)}, f32[4,4,1,32,2,128]{5,3,4,1,2,0:T(8,128)S(1)}, u32[]{:S(2)}, u32[]{:S(2)}) collective-permute-start(f32[4,4,1,32,2,128]{5,3,4,1,2,0:T(8,128)S(1)} %get-tuple-element.25), channel_id=1, source_target_pairs={{0,16},{1,17},{2,18},{3,19},{4,20},{5,21},{6,22},{7,23},{8,24},{9,... | collective-permute-start | bytes 1572872 | tf_op jit(solution)/shard_map/ppermute | solution.py:33
  272.7 11.1 %collective-permute-start.41 = (f32[4,4,1,32,2,128]{5,3,4,1,0,2:T(8,128)S(1)}, f32[4,4,1,32,2,128]{5,3,4,1,0,2:T(8,128)S(1)}, u32[]{:S(2)}, u32[]{:S(2)}) collective-permute-start(f32[4,4,1,32,2,128]{5,3,4,1,0,2:T(8,128)S(1)} %get-tuple-element.21), channel_id=1, source_target_pairs={{0,48},{1,49},{2,50},{3,51},{4,52},{5,53},{6,54},{7,55},{8,56},{9,... | collective-permute-start | bytes 1572872 | tf_op jit(solution)/shard_map/ppermute | solution.py:33
  274.6 12.3 %collective-permute-start.42 = (f32[4,4,1,32,2,128]{5,3,4,1,2,0:T(8,128)S(1)}, f32[4,4,1,32,2,128]{5,3,4,1,2,0:T(8,128)S(1)}, u32[]{:S(2)}, u32[]{:S(2)}) collective-permute-start(f32[4,4,1,32,2,128]{5,3,4,1,2,0:T(8,128)S(1)} %get-tuple-element.22), channel_id=1, source_target_pairs={{0,16},{1,17},{2,18},{3,19},{4,20},{5,21},{6,22},{7,23},{8,24},{9,... | collective-permute-start | bytes 1572872 | tf_op jit(solution)/shard_map/ppermute | solution.py:33
  344.9 11.1 %collective-permute-start.52 = (f32[4,4,1,32,2,128]{5,3,4,1,0,2:T(8,128)S(1)}, f32[4,4,1,32,2,128]{5,3,4,1,0,2:T(8,128)S(1)}, u32[]{:S(2)}, u32[]{:S(2)}) collective-permute-start(f32[4,4,1,32,2,128]{5,3,4,1,0,2:T(8,128)S(1)} %get-tuple-element.18), channel_id=1, source_target_pairs={{0,48},{1,49},{2,50},{3,51},{4,52},{5,53},{6,54},{7,55},{8,56},{9,... | collective-permute-start | bytes 1572872 | tf_op jit(solution)/shard_map/ppermute | solution.py:33
  346.9 12.3 %collective-permute-start.53 = (f32[4,4,1,32,2,128]{5,3,4,1,2,0:T(8,128)S(1)}, f32[4,4,1,32,2,128]{5,3,4,1,2,0:T(8,128)S(1)}, u32[]{:S(2)}, u32[]{:S(2)}) collective-permute-start(f32[4,4,1,32,2,128]{5,3,4,1,2,0:T(8,128)S(1)} %get-tuple-element.19), channel_id=1, source_target_pairs={{0,16},{1,17},{2,18},{3,19},{4,20},{5,21},{6,22},{7,23},{8,24},{9,... | collective-permute-start | bytes 1572872 | tf_op jit(solution)/shard_map/ppermute | solution.py:33
  417.3 11.1 %collective-permute-start.63 = (f32[4,4,1,32,2,128]{5,3,4,1,0,2:T(8,128)S(1)}, f32[4,4,1,32,2,128]{5,3,4,1,0,2:T(8,128)S(1)}, u32[]{:S(2)}, u32[]{:S(2)}) collective-permute-start(f32[4,4,1,32,2,128]{5,3,4,1,0,2:T(8,128)S(1)} %get-tuple-element.15), channel_id=1, source_target_pairs={{0,48},{1,49},{2,50},{3,51},{4,52},{5,53},{6,54},{7,55},{8,56},{9,... | collective-permute-start | bytes 1572872 | tf_op jit(solution)/shard_map/ppermute | solution.py:33
  419.2 12.3 %collective-permute-start.64 = (f32[4,4,1,32,2,128]{5,3,4,1,2,0:T(8,128)S(1)}, f32[4,4,1,32,2,128]{5,3,4,1,2,0:T(8,128)S(1)}, u32[]{:S(2)}, u32[]{:S(2)}) collective-permute-start(f32[4,4,1,32,2,128]{5,3,4,1,2,0:T(8,128)S(1)} %get-tuple-element.16), channel_id=1, source_target_pairs={{0,16},{1,17},{2,18},{3,19},{4,20},{5,21},{6,22},{7,23},{8,24},{9,... | collective-permute-start | bytes 1572872 | tf_op jit(solution)/shard_map/ppermute | solution.py:33
  434.3 47.6 %collective-permute-start.78 = (f32[96,2,2048]{2,1,0:T(2,128)}, f32[96,2,2048]{2,1,0:T(2,128)}, u32[]{:S(2)}, u32[]{:S(2)}) collective-permute-start(f32[96,2,2048]{2,1,0:T(2,128)} %bitcast.178), channel_id=1, source_target_pairs={{0,64},{64,0},{128,192},{192,128},{256,320},{320,256},{384,448},{4... | collective-permute-start | bytes 4718600 | tf_op jit(solution)/shard_map/ppermute | solution.py:10
  450.1 10.8 %collective-permute-start.68 = (f32[1,32,2,128]{3,1,2,0:T(8,128)S(1)}, f32[1,32,2,128]{3,1,2,0:T(8,128)S(1)}, u32[]{:S(2)}, u32[]{:S(2)}) collective-permute-start(f32[1,32,2,128]{3,1,2,0:T(8,128)S(1)} %get-tuple-element.58), channel_id=1, source_target_pairs={{0,1},{1,2},{2,3},{3,0},{4,5},{5,6},{6,7},{7,4},{8,9},{9,10},{10,1... | collective-permute-start | bytes 98312 | tf_op jit(solution)/shard_map/ppermute | solution.py:33
  458.1 14.8 %collective-permute-start.70 = (f32[1,16,2,128]{3,1,2,0:T(8,128)S(1)}, f32[1,16,2,128]{3,1,2,0:T(8,128)S(1)}, u32[]{:S(2)}, u32[]{:S(2)}) collective-permute-start(f32[1,16,2,128]{3,1,2,0:T(8,128)S(1)} %slice.313), channel_id=1, source_target_pairs={{0,3},{1,0},{2,1},{3,2},{4,7},{5,4},{6,5},{7,6},{8,11},{9,8},{10,9... | collective-permute-start | bytes 49160 | tf_op jit(solution)/shard_map/ppermute | solution.py:33
  460.9 12.0 %collective-permute-start.69 = (f32[1,16,2,128]{3,1,2,0:T(8,128)S(1)}, f32[1,16,2,128]{3,1,2,0:T(8,128)S(1)}, u32[]{:S(2)}, u32[]{:S(2)}) collective-permute-start(f32[1,16,2,128]{3,1,2,0:T(8,128)S(1)} %slice.312), channel_id=1, source_target_pairs={{0,1},{1,2},{2,3},{3,0},{4,5},{5,6},{6,7},{7,4},{8,9},{9,10},{10,1... | collective-permute-start | bytes 49160 | tf_op jit(solution)/shard_map/ppermute | solution.py:33
  472.9 15.1 %collective-permute-start.72 = (f32[4,1,32,2,128]{4,2,3,0,1:T(8,128)S(1)}, f32[4,1,32,2,128]{4,2,3,0,1:T(8,128)S(1)}, u32[]{:S(2)}, u32[]{:S(2)}) collective-permute-start(f32[4,1,32,2,128]{4,2,3,0,1:T(8,128)S(1)} %get-tuple-element.37), channel_id=1, source_target_pairs={{0,8},{1,9},{2,10},{3,11},{4,12},{5,13},{6,14},{7,15},{8,0},{9,1},... | collective-permute-start | bytes 393224 | tf_op jit(solution)/shard_map/ppermute | solution.py:33
  475.8 12.2 %collective-permute-start.71 = (f32[4,1,32,2,128]{4,2,3,0,1:T(8,128)S(1)}, f32[4,1,32,2,128]{4,2,3,0,1:T(8,128)S(1)}, u32[]{:S(2)}, u32[]{:S(2)}) collective-permute-start(f32[4,1,32,2,128]{4,2,3,0,1:T(8,128)S(1)} %get-tuple-element.37), channel_id=1, source_target_pairs={{0,12},{1,13},{2,14},{3,15},{4,0},{5,1},{6,2},{7,3},{8,4},{9,5},{1... | collective-permute-start | bytes 393224 | tf_op jit(solution)/shard_map/ppermute | solution.py:33
  488.2 20.5 %collective-permute-start.75 = (f32[4,4,1,32,2,128]{5,3,4,1,2,0:T(8,128)S(1)}, f32[4,4,1,32,2,128]{5,3,4,1,2,0:T(8,128)S(1)}, u32[]{:S(2)}, u32[]{:S(2)}) collective-permute-start(f32[4,4,1,32,2,128]{5,3,4,1,2,0:T(8,128)S(1)} %get-tuple-element.13), channel_id=1, source_target_pairs={{0,16},{1,17},{2,18},{3,19},{4,20},{5,21},{6,22},{7,23},{8,24},{9,... | collective-permute-start | bytes 1572872 | tf_op jit(solution)/shard_map/ppermute | solution.py:33
  490.1 13.0 %collective-permute-start.74 = (f32[4,4,1,32,2,128]{5,3,4,1,0,2:T(8,128)S(1)}, f32[4,4,1,32,2,128]{5,3,4,1,0,2:T(8,128)S(1)}, u32[]{:S(2)}, u32[]{:S(2)}) collective-permute-start(f32[4,4,1,32,2,128]{5,3,4,1,0,2:T(8,128)S(1)} %get-tuple-element.12), channel_id=1, source_target_pairs={{0,48},{1,49},{2,50},{3,51},{4,52},{5,53},{6,54},{7,55},{8,56},{9,... | collective-permute-start | bytes 1572872 | tf_op jit(solution)/shard_map/ppermute | solution.py:33
  (60 other events, 581.4 us)

commit v6 on v4

--- a/solution.py
+++ b/solution.py
@@ -11,7 +11,7 @@
 
 
 def complex_product(left_factor, operand):
-    highest = lax.Precision.HIGHEST
+    highest = lax.Precision.HIGH
     real_part = jnp.dot(
         left_factor[:, 0], operand[:, 0], precision=highest, preferred_element_type=jnp.float32
     ) - jnp.dot(

time: 519 us -> 501 us (0.965); the launches traced: 509 us -> 499 us
  matrix products: 31 us -> 18.7 us
  transfers between devices with their start and end apart: 72 -> 72, of which waited for: 44 -> 45; matrix products, arithmetic and copies ran while one was open for 5% -> 4% of each run, Pallas kernels for 0% -> 0%
where the time goes in v6:
time: 501 us; the launch traced here: 499 us
  starting transfers between devices  282 us (56%)
  waiting for transfers between devices  150 us (30%)
  local copies, waits for them, and re-layouts  41.1 us (8%)
  matrix products  18.7 us (4%)
  other arithmetic  5.35 us (1%)
    ppermute x70, starting transfers between devices, shifted_along(): return lax.ppermute(piece, 'panel', pairs)  278 us
    ppermute x70, waiting for transfers between devices, shifted_along(): return lax.ppermute(piece, 'panel', pairs)  150 us
    gather x14, local copies, waits for them, and re-layouts, panel_gather(): out = jnp.take(blocks, slot, axis=0, mode='clip')  26.3 us
  transfers between devices with their start and end apart: 72, of which 45 were waited for; matrix products, arithmetic and copies ran while one was open for 4% of the time, Pallas kernels for 0%

profile of v6, /device:TPU:6, one launch (start us, length us, event | category | flops | bytes accessed | tf_op | source)
XLA Modules:
  0.0 498.8 jit_solution(8709773879128331965)
XLA Ops:
  8.4 9.1 %collective-permute-start.3 = (f32[1,32,2,128]{3,1,2,0:T(8,128)S(1)}, f32[1,32,2,128]{3,1,2,0:T(8,128)S(1)}, u32[]{:S(2)}, u32[]{:S(2)}) collective-permute-start(f32[1,32,2,128]{3,1,2,0:T(8,128)S(1)} %get-tuple-element.64), channel_id=1, source_target_pairs={{0,1},{1,2},{2,3},{3,0},{4,5},{5,6},{6,7},{7,4},{8,9},{9,10},{10,1... | collective-permute-start | bytes 98312 | tf_op jit(solution)/shard_map/ppermute | solution.py:33
  17.5 10.9 %collective-permute-start.2 = (f32[1,32,2,128]{3,1,2,0:T(8,128)S(1)}, f32[1,32,2,128]{3,1,2,0:T(8,128)S(1)}, u32[]{:S(2)}, u32[]{:S(2)}) collective-permute-start(f32[1,32,2,128]{3,1,2,0:T(8,128)S(1)} %get-tuple-element.64), channel_id=1, source_target_pairs={{0,2},{1,3},{2,0},{3,1},{4,6},{5,7},{6,4},{7,5},{8,10},{9,11},{10,... | collective-permute-start | bytes 98312 | tf_op jit(solution)/shard_map/ppermute | solution.py:33
  28.5 5.5 %collective-permute-start.1 = (f32[1,32,2,128]{3,1,2,0:T(8,128)S(1)}, f32[1,32,2,128]{3,1,2,0:T(8,128)S(1)}, u32[]{:S(2)}, u32[]{:S(2)}) collective-permute-start(f32[1,32,2,128]{3,1,2,0:T(8,128)S(1)} %get-tuple-element.64), channel_id=1, source_target_pairs={{0,3},{1,0},{2,1},{3,2},{4,7},{5,4},{6,5},{7,6},{8,11},{9,8},{10,9... | collective-permute-start | bytes 98312 | tf_op jit(solution)/shard_map/ppermute | solution.py:33
  62.4 6.4 %collective-permute-done.7 = f32[4,4,1,32,2,128]{5,3,4,1,0,2:T(8,128)S(1)} collective-permute-done((f32[4,4,1,32,2,128]{5,3,4,1,0,2:T(8,128)}, f32[4,4,1,32,2,128]{5,3,4,1,0,2:T(8,128)S(1)}, u32[]{:S(2)}, u32[]{:S(2)}) %collective-permute-start.7) | collective-permute-done | bytes 524320 | tf_op jit(solution)/shard_map/ppermute | solution.py:33
  68.8 5.5 %collective-permute-start.10 = (f32[2,4,1,32,2,128]{5,3,4,1,0,2:T(8,128)S(1)}, f32[2,4,1,32,2,128]{5,3,4,1,0,2:T(8,128)S(1)}, u32[]{:S(2)}, u32[]{:S(2)}) collective-permute-start(f32[2,4,1,32,2,128]{5,3,4,1,0,2:T(8,128)S(1)} %slice.219), channel_id=1, source_target_pairs={{0,48},{1,49},{2,50},{3,51},{4,52},{5,53},{6,54},{7,55},{8,56},{9,... | collective-permute-start | bytes 786440 | tf_op jit(solution)/shard_map/ppermute | solution.py:33
  78.2 5.7 %collective-permute-done.9 = f32[2,4,1,32,2,128]{5,3,4,1,0,2:T(8,128)S(1)} collective-permute-done((f32[2,4,1,32,2,128]{5,3,4,1,0,2:T(8,128)S(1)}, f32[2,4,1,32,2,128]{5,3,4,1,0,2:T(8,128)S(1)}, u32[]{:S(2)}, u32[]{:S(2)}) %collective-permute-start.9) | collective-permute-done | bytes 262176 | tf_op jit(solution)/shard_map/ppermute | solution.py:33
  94.3 9.3 %collective-permute-start.12 = (f32[1,32,2,128]{3,1,2,0:T(8,128)S(1)}, f32[1,32,2,128]{3,1,2,0:T(8,128)S(1)}, u32[]{:S(2)}, u32[]{:S(2)}) collective-permute-start(f32[1,32,2,128]{3,1,2,0:T(8,128)S(1)} %maximum_add_fusion.2), channel_id=1, source_target_pairs={{0,2},{1,3},{2,0},{3,1},{4,6},{5,7},{6,4},{7,5},{8,10},{9,11},{10,... | collective-permute-start | bytes 98312 | tf_op jit(solution)/shard_map/ppermute | solution.py:33
  132.8 8.0 %collective-permute-done.17 = f32[4,4,1,32,2,128]{5,3,4,1,0,2:T(8,128)S(1)} collective-permute-done((f32[4,4,1,32,2,128]{5,3,4,1,0,2:T(8,128)S(1)}, f32[4,4,1,32,2,128]{5,3,4,1,0,2:T(8,128)S(1)}, u32[]{:S(2)}, u32[]{:S(2)}) %collective-permute-start.17) | collective-permute-done | bytes 524320 | tf_op jit(solution)/shard_map/ppermute | solution.py:33
  164.1 7.6 %collective-permute-start.22 = (f32[1,32,2,128]{3,1,2,0:T(8,128)S(1)}, f32[1,32,2,128]{3,1,2,0:T(8,128)S(1)}, u32[]{:S(2)}, u32[]{:S(2)}) collective-permute-start(f32[1,32,2,128]{3,1,2,0:T(8,128)S(1)} %get-tuple-element.62), channel_id=1, source_target_pairs={{0,2},{1,3},{2,0},{3,1},{4,6},{5,7},{6,4},{7,5},{8,10},{9,11},{10,... | collective-permute-start | bytes 98312 | tf_op jit(solution)/shard_map/ppermute | solution.py:33
  201.9 5.2 %collective-permute-done.27 = f32[4,4,1,32,2,128]{5,3,4,1,0,2:T(8,128)S(1)} collective-permute-done((f32[4,4,1,32,2,128]{5,3,4,1,0,2:T(8,128)S(1)}, f32[4,4,1,32,2,128]{5,3,4,1,0,2:T(8,128)S(1)}, u32[]{:S(2)}, u32[]{:S(2)}) %collective-permute-start.27) | collective-permute-done | bytes 524320 | tf_op jit(solution)/shard_map/ppermute | solution.py:33
  230.3 6.2 %collective-permute-start.32 = (f32[1,32,2,128]{3,1,2,0:T(8,128)S(1)}, f32[1,32,2,128]{3,1,2,0:T(8,128)S(1)}, u32[]{:S(2)}, u32[]{:S(2)}) collective-permute-start(f32[1,32,2,128]{3,1,2,0:T(8,128)S(1)} %maximum_add_fusion.4), channel_id=1, source_target_pairs={{0,2},{1,3},{2,0},{3,1},{4,6},{5,7},{6,4},{7,5},{8,10},{9,11},{10,... | collective-permute-start | bytes 98312 | tf_op jit(solution)/shard_map/ppermute | solution.py:33
  236.6 5.5 %collective-permute-start.31 = (f32[1,32,2,128]{3,1,2,0:T(8,128)S(1)}, f32[1,32,2,128]{3,1,2,0:T(8,128)S(1)}, u32[]{:S(2)}, u32[]{:S(2)}) collective-permute-start(f32[1,32,2,128]{3,1,2,0:T(8,128)S(1)} %maximum_add_fusion.4), channel_id=1, source_target_pairs={{0,3},{1,0},{2,1},{3,2},{4,7},{5,4},{6,5},{7,6},{8,11},{9,8},{10,9... | collective-permute-start | bytes 98312 | tf_op jit(solution)/shard_map/ppermute | solution.py:33
  266.2 5.2 %collective-permute-done.37 = f32[4,4,1,32,2,128]{5,3,4,1,0,2:T(8,128)S(1)} collective-permute-done((f32[4,4,1,32,2,128]{5,3,4,1,0,2:T(8,128)S(1)}, f32[4,4,1,32,2,128]{5,3,4,1,0,2:T(8,128)S(1)}, u32[]{:S(2)}, u32[]{:S(2)}) %collective-permute-start.37) | collective-permute-done | bytes 524320 | tf_op jit(solution)/shard_map/ppermute | solution.py:33
  290.0 7.1 %collective-permute-start.43 = (f32[1,32,2,128]{3,1,2,0:T(8,128)S(1)}, f32[1,32,2,128]{3,1,2,0:T(8,128)S(1)}, u32[]{:S(2)}, u32[]{:S(2)}) collective-permute-start(f32[1,32,2,128]{3,1,2,0:T(8,128)S(1)} %get-tuple-element.60), channel_id=1, source_target_pairs={{0,1},{1,2},{2,3},{3,0},{4,5},{5,6},{6,7},{7,4},{8,9},{9,10},{10,1... | collective-permute-start | bytes 98312 | tf_op jit(solution)/shard_map/ppermute | solution.py:33
  297.1 5.9 %collective-permute-start.42 = (f32[1,32,2,128]{3,1,2,0:T(8,128)S(1)}, f32[1,32,2,128]{3,1,2,0:T(8,128)S(1)}, u32[]{:S(2)}, u32[]{:S(2)}) collective-permute-start(f32[1,32,2,128]{3,1,2,0:T(8,128)S(1)} %get-tuple-element.60), channel_id=1, source_target_pairs={{0,2},{1,3},{2,0},{3,1},{4,6},{5,7},{6,4},{7,5},{8,10},{9,11},{10,... | collective-permute-start | bytes 98312 | tf_op jit(solution)/shard_map/ppermute | solution.py:33
  333.0 5.2 %collective-permute-done.47 = f32[4,4,1,32,2,128]{5,3,4,1,0,2:T(8,128)S(1)} collective-permute-done((f32[4,4,1,32,2,128]{5,3,4,1,0,2:T(8,128)S(1)}, f32[4,4,1,32,2,128]{5,3,4,1,0,2:T(8,128)S(1)}, u32[]{:S(2)}, u32[]{:S(2)}) %collective-permute-start.47) | collective-permute-done | bytes 524320 | tf_op jit(solution)/shard_map/ppermute | solution.py:33
  360.7 8.2 %collective-permute-start.52 = (f32[1,32,2,128]{3,1,2,0:T(8,128)S(1)}, f32[1,32,2,128]{3,1,2,0:T(8,128)S(1)}, u32[]{:S(2)}, u32[]{:S(2)}) collective-permute-start(f32[1,32,2,128]{3,1,2,0:T(8,128)S(1)} %maximum_add_fusion.6), channel_id=1, source_target_pairs={{0,2},{1,3},{2,0},{3,1},{4,6},{5,7},{6,4},{7,5},{8,10},{9,11},{10,... | collective-permute-start | bytes 98312 | tf_op jit(solution)/shard_map/ppermute | solution.py:33
  368.9 6.2 %collective-permute-start.51 = (f32[1,32,2,128]{3,1,2,0:T(8,128)S(1)}, f32[1,32,2,128]{3,1,2,0:T(8,128)S(1)}, u32[]{:S(2)}, u32[]{:S(2)}) collective-permute-start(f32[1,32,2,128]{3,1,2,0:T(8,128)S(1)} %maximum_add_fusion.6), channel_id=1, source_target_pairs={{0,3},{1,0},{2,1},{3,2},{4,7},{5,4},{6,5},{7,6},{8,11},{9,8},{10,9... | collective-permute-start | bytes 98312 | tf_op jit(solution)/shard_map/ppermute | solution.py:33
  398.3 5.2 %collective-permute-done.57 = f32[4,4,1,32,2,128]{5,3,4,1,0,2:T(8,128)S(1)} collective-permute-done((f32[4,4,1,32,2,128]{5,3,4,1,0,2:T(8,128)S(1)}, f32[4,4,1,32,2,128]{5,3,4,1,0,2:T(8,128)S(1)}, u32[]{:S(2)}, u32[]{:S(2)}) %collective-permute-start.57) | collective-permute-done | bytes 524320 | tf_op jit(solution)/shard_map/ppermute | solution.py:33
  422.0 5.4 %collective-permute-start.63 = (f32[1,32,2,128]{3,1,2,0:T(8,128)S(1)}, f32[1,32,2,128]{3,1,2,0:T(8,128)S(1)}, u32[]{:S(2)}, u32[]{:S(2)}) collective-permute-start(f32[1,32,2,128]{3,1,2,0:T(8,128)S(1)} %get-tuple-element.58), channel_id=1, source_target_pairs={{0,1},{1,2},{2,3},{3,0},{4,5},{5,6},{6,7},{7,4},{8,9},{9,10},{10,1... | collective-permute-start | bytes 98312 | tf_op jit(solution)/shard_map/ppermute | solution.py:33
  427.4 8.3 %collective-permute-start.62 = (f32[1,32,2,128]{3,1,2,0:T(8,128)S(1)}, f32[1,32,2,128]{3,1,2,0:T(8,128)S(1)}, u32[]{:S(2)}, u32[]{:S(2)}) collective-permute-start(f32[1,32,2,128]{3,1,2,0:T(8,128)S(1)} %get-tuple-element.58), channel_id=1, source_target_pairs={{0,2},{1,3},{2,0},{3,1},{4,6},{5,7},{6,4},{7,5},{8,10},{9,11},{10,... | collective-permute-start | bytes 98312 | tf_op jit(solution)/shard_map/ppermute | solution.py:33
  469.2 6.5 %collective-permute-done.67 = f32[4,4,1,32,2,128]{5,3,4,1,0,2:T(8,128)S(1)} collective-permute-done((f32[4,4,1,32,2,128]{5,3,4,1,0,2:T(8,128)S(1)}, f32[4,4,1,32,2,128]{5,3,4,1,0,2:T(8,128)S(1)}, u32[]{:S(2)}, u32[]{:S(2)}) %collective-permute-start.67) | collective-permute-done | bytes 524320 | tf_op jit(solution)/shard_map/ppermute | solution.py:33
  475.7 5.6 %collective-permute-start.70 = (f32[2,4,1,32,2,128]{5,3,4,1,0,2:T(8,128)S(1)}, f32[2,4,1,32,2,128]{5,3,4,1,0,2:T(8,128)S(1)}, u32[]{:S(2)}, u32[]{:S(2)}) collective-permute-start(f32[2,4,1,32,2,128]{5,3,4,1,0,2:T(8,128)S(1)} %slice.245), channel_id=1, source_target_pairs={{0,48},{1,49},{2,50},{3,51},{4,52},{5,53},{6,54},{7,55},{8,56},{9,... | collective-permute-start | bytes 786440 | tf_op jit(solution)/shard_map/ppermute | solution.py:33
  485.2 5.6 %collective-permute-done.69 = f32[2,4,1,32,2,128]{5,3,4,1,0,2:T(8,128)S(1)} collective-permute-done((f32[2,4,1,32,2,128]{5,3,4,1,0,2:T(8,128)S(1)}, f32[2,4,1,32,2,128]{5,3,4,1,0,2:T(8,128)S(1)}, u32[]{:S(2)}, u32[]{:S(2)}) %collective-permute-start.69) | collective-permute-done | bytes 262176 | tf_op jit(solution)/shard_map/ppermute | solution.py:33
  (244 shorter events, 337.7 us)
Async XLA Ops:
  8.4 25.5 %collective-permute-start.3 = (f32[1,32,2,128]{3,1,2,0:T(8,128)S(1)}, f32[1,32,2,128]{3,1,2,0:T(8,128)S(1)}, u32[]{:S(2)}, u32[]{:S(2)}) collective-permute-start(f32[1,32,2,128]{3,1,2,0:T(8,128)S(1)} %get-tuple-element.64), channel_id=1, source_target_pairs={{0,1},{1,2},{2,3},{3,0},{4,5},{5,6},{6,7},{7,4},{8,9},{9,10},{10,1... | collective-permute-start | bytes 98312 | tf_op jit(solution)/shard_map/ppermute | solution.py:33
  17.5 16.4 %collective-permute-start.2 = (f32[1,32,2,128]{3,1,2,0:T(8,128)S(1)}, f32[1,32,2,128]{3,1,2,0:T(8,128)S(1)}, u32[]{:S(2)}, u32[]{:S(2)}) collective-permute-start(f32[1,32,2,128]{3,1,2,0:T(8,128)S(1)} %get-tuple-element.64), channel_id=1, source_target_pairs={{0,2},{1,3},{2,0},{3,1},{4,6},{5,7},{6,4},{7,5},{8,10},{9,11},{10,... | collective-permute-start | bytes 98312 | tf_op jit(solution)/shard_map/ppermute | solution.py:33
  55.1 13.7 %collective-permute-start.7 = (f32[4,4,1,32,2,128]{5,3,4,1,0,2:T(8,128)}, f32[4,4,1,32,2,128]{5,3,4,1,0,2:T(8,128)S(1)}, u32[]{:S(2)}, u32[]{:S(2)}) collective-permute-start(f32[4,4,1,32,2,128]{5,3,4,1,0,2:T(8,128)} %get-tuple-element.32), channel_id=1, source_target_pairs={{0,48},{1,49},{2,50},{3,51},{4,52},{5,53},{6,54},{7,55},{8,56},{9,... | collective-permute-start | bytes 1572872 | tf_op jit(solution)/shard_map/ppermute | solution.py:33
  60.0 14.4 %collective-permute-start.8 = (f32[4,4,1,32,2,128]{5,3,4,1,2,0:T(8,128)S(1)}, f32[4,4,1,32,2,128]{5,3,4,1,2,0:T(8,128)S(1)}, u32[]{:S(2)}, u32[]{:S(2)}) collective-permute-start(f32[4,4,1,32,2,128]{5,3,4,1,2,0:T(8,128)S(1)} %get-tuple-element.33), channel_id=1, source_target_pairs={{0,16},{1,17},{2,18},{3,19},{4,20},{5,21},{6,22},{7,23},{8,24},{9,... | collective-permute-start | bytes 1572872 | tf_op jit(solution)/shard_map/ppermute | solution.py:33
  91.1 16.8 %collective-permute-start.13 = (f32[1,32,2,128]{3,1,2,0:T(8,128)S(1)}, f32[1,32,2,128]{3,1,2,0:T(8,128)S(1)}, u32[]{:S(2)}, u32[]{:S(2)}) collective-permute-start(f32[1,32,2,128]{3,1,2,0:T(8,128)S(1)} %maximum_add_fusion.2), channel_id=1, source_target_pairs={{0,1},{1,2},{2,3},{3,0},{4,5},{5,6},{6,7},{7,4},{8,9},{9,10},{10,1... | collective-permute-start | bytes 98312 | tf_op jit(solution)/shard_map/ppermute | solution.py:33
  94.3 14.7 %collective-permute-start.12 = (f32[1,32,2,128]{3,1,2,0:T(8,128)S(1)}, f32[1,32,2,128]{3,1,2,0:T(8,128)S(1)}, u32[]{:S(2)}, u32[]{:S(2)}) collective-permute-start(f32[1,32,2,128]{3,1,2,0:T(8,128)S(1)} %maximum_add_fusion.2), channel_id=1, source_target_pairs={{0,2},{1,3},{2,0},{3,1},{4,6},{5,7},{6,4},{7,5},{8,10},{9,11},{10,... | collective-permute-start | bytes 98312 | tf_op jit(solution)/shard_map/ppermute | solution.py:33
  127.0 13.9 %collective-permute-start.17 = (f32[4,4,1,32,2,128]{5,3,4,1,0,2:T(8,128)S(1)}, f32[4,4,1,32,2,128]{5,3,4,1,0,2:T(8,128)S(1)}, u32[]{:S(2)}, u32[]{:S(2)}) collective-permute-start(f32[4,4,1,32,2,128]{5,3,4,1,0,2:T(8,128)S(1)} %get-tuple-element.27), channel_id=1, source_target_pairs={{0,48},{1,49},{2,50},{3,51},{4,52},{5,53},{6,54},{7,55},{8,56},{9,... | collective-permute-start | bytes 1572872 | tf_op jit(solution)/shard_map/ppermute | solution.py:33
  128.9 15.1 %collective-permute-start.18 = (f32[4,4,1,32,2,128]{5,3,4,1,2,0:T(8,128)S(1)}, f32[4,4,1,32,2,128]{5,3,4,1,2,0:T(8,128)S(1)}, u32[]{:S(2)}, u32[]{:S(2)}) collective-permute-start(f32[4,4,1,32,2,128]{5,3,4,1,2,0:T(8,128)S(1)} %get-tuple-element.28), channel_id=1, source_target_pairs={{0,16},{1,17},{2,18},{3,19},{4,20},{5,21},{6,22},{7,23},{8,24},{9,... | collective-permute-start | bytes 1572872 | tf_op jit(solution)/shard_map/ppermute | solution.py:33
  159.4 15.8 %collective-permute-start.23 = (f32[1,32,2,128]{3,1,2,0:T(8,128)S(1)}, f32[1,32,2,128]{3,1,2,0:T(8,128)S(1)}, u32[]{:S(2)}, u32[]{:S(2)}) collective-permute-start(f32[1,32,2,128]{3,1,2,0:T(8,128)S(1)} %get-tuple-element.62), channel_id=1, source_target_pairs={{0,1},{1,2},{2,3},{3,0},{4,5},{5,6},{6,7},{7,4},{8,9},{9,10},{10,1... | collective-permute-start | bytes 98312 | tf_op jit(solution)/shard_map/ppermute | solution.py:33
  164.1 14.6 %collective-permute-start.22 = (f32[1,32,2,128]{3,1,2,0:T(8,128)S(1)}, f32[1,32,2,128]{3,1,2,0:T(8,128)S(1)}, u32[]{:S(2)}, u32[]{:S(2)}) collective-permute-start(f32[1,32,2,128]{3,1,2,0:T(8,128)S(1)} %get-tuple-element.62), channel_id=1, source_target_pairs={{0,2},{1,3},{2,0},{3,1},{4,6},{5,7},{6,4},{7,5},{8,10},{9,11},{10,... | collective-permute-start | bytes 98312 | tf_op jit(solution)/shard_map/ppermute | solution.py:33
  197.9 12.3 %collective-permute-start.28 = (f32[4,4,1,32,2,128]{5,3,4,1,2,0:T(8,128)S(1)}, f32[4,4,1,32,2,128]{5,3,4,1,2,0:T(8,128)S(1)}, u32[]{:S(2)}, u32[]{:S(2)}) collective-permute-start(f32[4,4,1,32,2,128]{5,3,4,1,2,0:T(8,128)S(1)} %get-tuple-element.25), channel_id=1, source_target_pairs={{0,16},{1,17},{2,18},{3,19},{4,20},{5,21},{6,22},{7,23},{8,24},{9,... | collective-permute-start | bytes 1572872 | tf_op jit(solution)/shard_map/ppermute | solution.py:33
  225.6 16.4 %collective-permute-start.33 = (f32[1,32,2,128]{3,1,2,0:T(8,128)S(1)}, f32[1,32,2,128]{3,1,2,0:T(8,128)S(1)}, u32[]{:S(2)}, u32[]{:S(2)}) collective-permute-start(f32[1,32,2,128]{3,1,2,0:T(8,128)S(1)} %maximum_add_fusion.4), channel_id=1, source_target_pairs={{0,1},{1,2},{2,3},{3,0},{4,5},{5,6},{6,7},{7,4},{8,9},{9,10},{10,1... | collective-permute-start | bytes 98312 | tf_op jit(solution)/shard_map/ppermute | solution.py:33
  230.3 14.5 %collective-permute-start.32 = (f32[1,32,2,128]{3,1,2,0:T(8,128)S(1)}, f32[1,32,2,128]{3,1,2,0:T(8,128)S(1)}, u32[]{:S(2)}, u32[]{:S(2)}) collective-permute-start(f32[1,32,2,128]{3,1,2,0:T(8,128)S(1)} %maximum_add_fusion.4), channel_id=1, source_target_pairs={{0,2},{1,3},{2,0},{3,1},{4,6},{5,7},{6,4},{7,5},{8,10},{9,11},{10,... | collective-permute-start | bytes 98312 | tf_op jit(solution)/shard_map/ppermute | solution.py:33
  262.3 12.3 %collective-permute-start.38 = (f32[4,4,1,32,2,128]{5,3,4,1,2,0:T(8,128)S(1)}, f32[4,4,1,32,2,128]{5,3,4,1,2,0:T(8,128)S(1)}, u32[]{:S(2)}, u32[]{:S(2)}) collective-permute-start(f32[4,4,1,32,2,128]{5,3,4,1,2,0:T(8,128)S(1)} %get-tuple-element.22), channel_id=1, source_target_pairs={{0,16},{1,17},{2,18},{3,19},{4,20},{5,21},{6,22},{7,23},{8,24},{9,... | collective-permute-start | bytes 1572872 | tf_op jit(solution)/shard_map/ppermute | solution.py:33
  290.0 18.0 %collective-permute-start.43 = (f32[1,32,2,128]{3,1,2,0:T(8,128)S(1)}, f32[1,32,2,128]{3,1,2,0:T(8,128)S(1)}, u32[]{:S(2)}, u32[]{:S(2)}) collective-permute-start(f32[1,32,2,128]{3,1,2,0:T(8,128)S(1)} %get-tuple-element.60), channel_id=1, source_target_pairs={{0,1},{1,2},{2,3},{3,0},{4,5},{5,6},{6,7},{7,4},{8,9},{9,10},{10,1... | collective-permute-start | bytes 98312 | tf_op jit(solution)/shard_map/ppermute | solution.py:33
  297.1 15.2 %collective-permute-start.42 = (f32[1,32,2,128]{3,1,2,0:T(8,128)S(1)}, f32[1,32,2,128]{3,1,2,0:T(8,128)S(1)}, u32[]{:S(2)}, u32[]{:S(2)}) collective-permute-start(f32[1,32,2,128]{3,1,2,0:T(8,128)S(1)} %get-tuple-element.60), channel_id=1, source_target_pairs={{0,2},{1,3},{2,0},{3,1},{4,6},{5,7},{6,4},{7,5},{8,10},{9,11},{10,... | collective-permute-start | bytes 98312 | tf_op jit(solution)/shard_map/ppermute | solution.py:33
  356.7 18.5 %collective-permute-start.53 = (f32[1,32,2,128]{3,1,2,0:T(8,128)S(1)}, f32[1,32,2,128]{3,1,2,0:T(8,128)S(1)}, u32[]{:S(2)}, u32[]{:S(2)}) collective-permute-start(f32[1,32,2,128]{3,1,2,0:T(8,128)S(1)} %maximum_add_fusion.6), channel_id=1, source_target_pairs={{0,1},{1,2},{2,3},{3,0},{4,5},{5,6},{6,7},{7,4},{8,9},{9,10},{10,1... | collective-permute-start | bytes 98312 | tf_op jit(solution)/shard_map/ppermute | solution.py:33
  360.7 14.6 %collective-permute-start.52 = (f32[1,32,2,128]{3,1,2,0:T(8,128)S(1)}, f32[1,32,2,128]{3,1,2,0:T(8,128)S(1)}, u32[]{:S(2)}, u32[]{:S(2)}) collective-permute-start(f32[1,32,2,128]{3,1,2,0:T(8,128)S(1)} %maximum_add_fusion.6), channel_id=1, source_target_pairs={{0,2},{1,3},{2,0},{3,1},{4,6},{5,7},{6,4},{7,5},{8,10},{9,11},{10,... | collective-permute-start | bytes 98312 | tf_op jit(solution)/shard_map/ppermute | solution.py:33
  409.4 46.8 %collective-permute-start.71 = (f32[96,2,2048]{2,1,0:T(2,128)}, f32[96,2,2048]{2,1,0:T(2,128)}, u32[]{:S(2)}, u32[]{:S(2)}) collective-permute-start(f32[96,2,2048]{2,1,0:T(2,128)} %bitcast.178), channel_id=1, source_target_pairs={{0,64},{64,0},{128,192},{192,128},{256,320},{320,256},{384,448},{4... | collective-permute-start | bytes 4718600 | tf_op jit(solution)/shard_map/ppermute | solution.py:10
  422.0 21.4 %collective-permute-start.63 = (f32[1,32,2,128]{3,1,2,0:T(8,128)S(1)}, f32[1,32,2,128]{3,1,2,0:T(8,128)S(1)}, u32[]{:S(2)}, u32[]{:S(2)}) collective-permute-start(f32[1,32,2,128]{3,1,2,0:T(8,128)S(1)} %get-tuple-element.58), channel_id=1, source_target_pairs={{0,1},{1,2},{2,3},{3,0},{4,5},{5,6},{6,7},{7,4},{8,9},{9,10},{10,1... | collective-permute-start | bytes 98312 | tf_op jit(solution)/shard_map/ppermute | solution.py:33
  427.4 16.0 %collective-permute-start.62 = (f32[1,32,2,128]{3,1,2,0:T(8,128)S(1)}, f32[1,32,2,128]{3,1,2,0:T(8,128)S(1)}, u32[]{:S(2)}, u32[]{:S(2)}) collective-permute-start(f32[1,32,2,128]{3,1,2,0:T(8,128)S(1)} %get-tuple-element.58), channel_id=1, source_target_pairs={{0,2},{1,3},{2,0},{3,1},{4,6},{5,7},{6,4},{7,5},{8,10},{9,11},{10,... | collective-permute-start | bytes 98312 | tf_op jit(solution)/shard_map/ppermute | solution.py:33
  445.9 13.8 %collective-permute-start.65 = (f32[4,1,32,2,128]{4,2,3,0,1:T(8,128)S(1)}, f32[4,1,32,2,128]{4,2,3,0,1:T(8,128)S(1)}, u32[]{:S(2)}, u32[]{:S(2)}) collective-permute-start(f32[4,1,32,2,128]{4,2,3,0,1:T(8,128)S(1)} %get-tuple-element.37), channel_id=1, source_target_pairs={{0,8},{1,9},{2,10},{3,11},{4,12},{5,13},{6,14},{7,15},{8,0},{9,1},... | collective-permute-start | bytes 393224 | tf_op jit(solution)/shard_map/ppermute | solution.py:33
  459.9 21.4 %collective-permute-start.68 = (f32[4,4,1,32,2,128]{5,3,4,1,2,0:T(8,128)S(1)}, f32[4,4,1,32,2,128]{5,3,4,1,2,0:T(8,128)S(1)}, u32[]{:S(2)}, u32[]{:S(2)}) collective-permute-start(f32[4,4,1,32,2,128]{5,3,4,1,2,0:T(8,128)S(1)} %get-tuple-element.13), channel_id=1, source_target_pairs={{0,16},{1,17},{2,18},{3,19},{4,20},{5,21},{6,22},{7,23},{8,24},{9,... | collective-permute-start | bytes 1572872 | tf_op jit(solution)/shard_map/ppermute | solution.py:33
  461.8 13.8 %collective-permute-start.67 = (f32[4,4,1,32,2,128]{5,3,4,1,0,2:T(8,128)S(1)}, f32[4,4,1,32,2,128]{5,3,4,1,0,2:T(8,128)S(1)}, u32[]{:S(2)}, u32[]{:S(2)}) collective-permute-start(f32[4,4,1,32,2,128]{5,3,4,1,0,2:T(8,128)S(1)} %get-tuple-element.12), channel_id=1, source_target_pairs={{0,48},{1,49},{2,50},{3,51},{4,52},{5,53},{6,54},{7,55},{8,56},{9,... | collective-permute-start | bytes 1572872 | tf_op jit(solution)/shard_map/ppermute | solution.py:33
  (53 other events, 524.5 us)

commit v7 on v6

--- a/solution.py
+++ b/solution.py
@@ -78,19 +78,16 @@
     other_form = swapped(own_shared, "box", 0)
     other_crossing = swapped(own_crossing, "box", 0)
 
-    def through_own(gathered_piece):
-        return slice_product(own_shared, gathered_piece)
+    blocks_by_parity = jnp.stack([own_shared, other_form], 0)
 
-    def own_step(image_now):
-        return own_rows + through_own(panel_gather(image_now))
+    def step(index, vector):
+        parity = index % 2
+        matrix = lax.dynamic_index_in_dim(blocks_by_parity, parity, 0, keepdims=False)
+        addend = own_rows * (1 - parity).astype(own_rows.dtype)
+        return addend + slice_product(matrix, panel_gather(vector))
 
     image_panel = complex_product(other_form, start_rows)
-    rows_panel = own_step(image_panel)
-    for iteration in range(1, ITERS):
-        image_panel = slice_product(
-            other_form, panel_gather(rows_panel)
-        )
-        rows_panel = own_step(image_panel)
+    rows_panel = lax.fori_loop(0, 2 * ITERS - 1, step, image_panel)
     gathered_piece = panel_gather(rows_panel)
     image_final = slice_product(other_form, gathered_piece)
     other_terms = slice_product(other_crossing, gathered_piece)

time: 501 us -> 511 us (1.020)
  local copies, waits for them, and re-layouts: 41.1 us -> 48.2 us
  other arithmetic: 5.35 us -> 12.3 us
  waiting for transfers between devices: 150 us -> 144 us
    ppermute x70, waiting for transfers between devices: 150 us -> 144 us  [shifted_along(): return lax.ppermute(piece, 'panel', pairs)]
    squeeze x0 -> x5, local copies, waits for them, and re-layouts: none -> 5.4 us  [step(): lax.dynamic_index_in_dim(blocks_by_parity, parity, 0, keepdims=False)]
    another operation x21, other arithmetic: 4.98 us -> 10.3 us  [relay_stage(): return jnp.stack([blocks, from_above, opposite, from_below], 0)]
  transfers between devices with their start and end apart: 72 -> 72, of which waited for: 45 -> 45; matrix products, arithmetic and copies ran while one was open for 4% -> 6% of each run, Pallas kernels for 0% -> 0%
where the time goes in v7:
time: 511 us; the launch traced here: 508 us
  starting transfers between devices  282 us (55%)
  waiting for transfers between devices  144 us (28%)
  local copies, waits for them, and re-layouts  48.2 us (9%)
  matrix products  20.4 us (4%)
  other arithmetic  12.3 us (2%)
    ppermute x70, starting transfers between devices, shifted_along(): return lax.ppermute(piece, 'panel', pairs)  278 us
    ppermute x70, waiting for transfers between devices, shifted_along(): return lax.ppermute(piece, 'panel', pairs)  144 us
    gather x14, local copies, waits for them, and re-layouts, panel_gather(): out = jnp.take(blocks, slot, axis=0, mode='clip')  26.6 us
    another operation x21, other arithmetic, relay_stage(): return jnp.stack([blocks, from_above, opposite, from_below], 0)  10.3 us
  transfers between devices with their start and end apart: 72, of which 45 were waited for; matrix products, arithmetic and copies ran while one was open for 6% of the time, Pallas kernels for 0%

profile of v7, /device:TPU:6, one launch (start us, length us, event | category | flops | bytes accessed | tf_op | source)
XLA Modules:
  0.0 508.4 jit_solution(12256237731682436399)
XLA Ops:
  10.7 354.0 %while.16 = (s32[]{:T(128)}, f32[32,2,128]{2,0,1:T(8,128)S(1)}, f32[32,2,128]{2,0,1:T(8,128)S(1)}, f32[2,32,2,2048]{3,2,1,0:T(2,128)}, s32[]{:T(128)}, /*index=5...) while((s32[]{:T(128)}, f32[32,2,128]{2,0,1:T(8,128)S(1)}, ...), condition=%wide.region_1.2_spmd, body=%wide.region_0.1_spmd.sunk | while | flops 203561024 | bytes 37296056 | solution.py:90
  10.7 9.1 %collective-permute-start = (f32[1,32,2,128]{3,1,2,0:T(8,128)S(1)}, f32[1,32,2,128]{3,1,2,0:T(8,128)S(1)}, u32[]{:S(2)}, u32[]{:S(2)}) collective-permute-start(f32[1,32,2,128]{3,1,2,0:T(8,128)S(1)} %bitcast.290), channel_id=1, source_target_pairs={{0,1},{1,2},{2,3},{3,0},{4,5},{5,6},{6,7},{7,4},{8,9},{9,10},{10,1... | collective-permute-start | bytes 98312 | tf_op jit(solution)/shard_map/while/body/eval_jaxpr/ppermute | solution.py:33
  19.8 10.9 %collective-permute-start.1 = (f32[1,32,2,128]{3,1,2,0:T(8,128)S(1)}, f32[1,32,2,128]{3,1,2,0:T(8,128)S(1)}, u32[]{:S(2)}, u32[]{:S(2)}) collective-permute-start(f32[1,32,2,128]{3,1,2,0:T(8,128)S(1)} %bitcast.291), channel_id=1, source_target_pairs={{0,2},{1,3},{2,0},{3,1},{4,6},{5,7},{6,4},{7,5},{8,10},{9,11},{10,... | collective-permute-start | bytes 98312 | tf_op jit(solution)/shard_map/while/body/eval_jaxpr/ppermute | solution.py:33
  30.7 5.5 %collective-permute-start.2 = (f32[1,32,2,128]{3,1,2,0:T(8,128)S(1)}, f32[1,32,2,128]{3,1,2,0:T(8,128)S(1)}, u32[]{:S(2)}, u32[]{:S(2)}) collective-permute-start(f32[1,32,2,128]{3,1,2,0:T(8,128)S(1)} %bitcast.292), channel_id=1, source_target_pairs={{0,3},{1,0},{2,1},{3,2},{4,7},{5,4},{6,5},{7,6},{8,11},{9,8},{10,9... | collective-permute-start | bytes 98312 | tf_op jit(solution)/shard_map/while/body/eval_jaxpr/ppermute | solution.py:33
  36.2 5.1 %collective-permute-done.2 = f32[1,32,2,128]{3,1,2,0:T(8,128)S(1)} collective-permute-done((f32[1,32,2,128]{3,1,2,0:T(8,128)S(1)}, f32[1,32,2,128]{3,1,2,0:T(8,128)S(1)}, u32[]{:S(2)}, u32[]{:S(2)}) %collective-permute-start.2) | collective-permute-done | bytes 32800 | tf_op jit(solution)/shard_map/while/body/eval_jaxpr/ppermute | solution.py:33
  64.3 5.5 %collective-permute-done.7 = f32[4,4,1,32,2,128]{5,3,4,1,0,2:T(8,128)S(1)} collective-permute-done((f32[4,4,1,32,2,128]{5,3,4,1,0,2:T(8,128)S(1)}, f32[4,4,1,32,2,128]{5,3,4,1,0,2:T(8,128)S(1)}, u32[]{:S(2)}, u32[]{:S(2)}) %collective-permute-start.7) | collective-permute-done | bytes 524320 | tf_op jit(solution)/shard_map/while/body/eval_jaxpr/ppermute | solution.py:33
  69.8 5.6 %collective-permute-start.8 = (f32[2,4,1,32,2,128]{5,3,4,1,0,2:T(8,128)S(1)}, f32[2,4,1,32,2,128]{5,3,4,1,0,2:T(8,128)S(1)}, u32[]{:S(2)}, u32[]{:S(2)}) collective-permute-start(f32[2,4,1,32,2,128]{5,3,4,1,0,2:T(8,128)S(1)} %slice.230), channel_id=1, source_target_pairs={{0,48},{1,49},{2,50},{3,51},{4,52},{5,53},{6,54},{7,55},{8,56},{9,... | collective-permute-start | bytes 786440 | tf_op jit(solution)/shard_map/while/body/eval_jaxpr/ppermute | solution.py:33
  79.3 5.7 %collective-permute-done.9 = f32[2,4,1,32,2,128]{5,3,4,1,0,2:T(8,128)S(1)} collective-permute-done((f32[2,4,1,32,2,128]{5,3,4,1,0,2:T(8,128)S(1)}, f32[2,4,1,32,2,128]{5,3,4,1,0,2:T(8,128)S(1)}, u32[]{:S(2)}, u32[]{:S(2)}) %collective-permute-start.9) | collective-permute-done | bytes 262176 | tf_op jit(solution)/shard_map/while/body/eval_jaxpr/ppermute | solution.py:33
  95.7 9.3 %collective-permute-start.1 = (f32[1,32,2,128]{3,1,2,0:T(8,128)S(1)}, f32[1,32,2,128]{3,1,2,0:T(8,128)S(1)}, u32[]{:S(2)}, u32[]{:S(2)}) collective-permute-start(f32[1,32,2,128]{3,1,2,0:T(8,128)S(1)} %bitcast.291), channel_id=1, source_target_pairs={{0,2},{1,3},{2,0},{3,1},{4,6},{5,7},{6,4},{7,5},{8,10},{9,11},{10,... | collective-permute-start | bytes 98312 | tf_op jit(solution)/shard_map/while/body/eval_jaxpr/ppermute | solution.py:33
  135.3 6.9 %collective-permute-done.7 = f32[4,4,1,32,2,128]{5,3,4,1,0,2:T(8,128)S(1)} collective-permute-done((f32[4,4,1,32,2,128]{5,3,4,1,0,2:T(8,128)S(1)}, f32[4,4,1,32,2,128]{5,3,4,1,0,2:T(8,128)S(1)}, u32[]{:S(2)}, u32[]{:S(2)}) %collective-permute-start.7) | collective-permute-done | bytes 524320 | tf_op jit(solution)/shard_map/while/body/eval_jaxpr/ppermute | solution.py:33
  167.2 7.6 %collective-permute-start.1 = (f32[1,32,2,128]{3,1,2,0:T(8,128)S(1)}, f32[1,32,2,128]{3,1,2,0:T(8,128)S(1)}, u32[]{:S(2)}, u32[]{:S(2)}) collective-permute-start(f32[1,32,2,128]{3,1,2,0:T(8,128)S(1)} %bitcast.291), channel_id=1, source_target_pairs={{0,2},{1,3},{2,0},{3,1},{4,6},{5,7},{6,4},{7,5},{8,10},{9,11},{10,... | collective-permute-start | bytes 98312 | tf_op jit(solution)/shard_map/while/body/eval_jaxpr/ppermute | solution.py:33
  235.0 6.2 %collective-permute-start.1 = (f32[1,32,2,128]{3,1,2,0:T(8,128)S(1)}, f32[1,32,2,128]{3,1,2,0:T(8,128)S(1)}, u32[]{:S(2)}, u32[]{:S(2)}) collective-permute-start(f32[1,32,2,128]{3,1,2,0:T(8,128)S(1)} %bitcast.291), channel_id=1, source_target_pairs={{0,2},{1,3},{2,0},{3,1},{4,6},{5,7},{6,4},{7,5},{8,10},{9,11},{10,... | collective-permute-start | bytes 98312 | tf_op jit(solution)/shard_map/while/body/eval_jaxpr/ppermute | solution.py:33
  241.3 5.5 %collective-permute-start.2 = (f32[1,32,2,128]{3,1,2,0:T(8,128)S(1)}, f32[1,32,2,128]{3,1,2,0:T(8,128)S(1)}, u32[]{:S(2)}, u32[]{:S(2)}) collective-permute-start(f32[1,32,2,128]{3,1,2,0:T(8,128)S(1)} %bitcast.292), channel_id=1, source_target_pairs={{0,3},{1,0},{2,1},{3,2},{4,7},{5,4},{6,5},{7,6},{8,11},{9,8},{10,9... | collective-permute-start | bytes 98312 | tf_op jit(solution)/shard_map/while/body/eval_jaxpr/ppermute | solution.py:33
  296.3 7.1 %collective-permute-start = (f32[1,32,2,128]{3,1,2,0:T(8,128)S(1)}, f32[1,32,2,128]{3,1,2,0:T(8,128)S(1)}, u32[]{:S(2)}, u32[]{:S(2)}) collective-permute-start(f32[1,32,2,128]{3,1,2,0:T(8,128)S(1)} %bitcast.290), channel_id=1, source_target_pairs={{0,1},{1,2},{2,3},{3,0},{4,5},{5,6},{6,7},{7,4},{8,9},{9,10},{10,1... | collective-permute-start | bytes 98312 | tf_op jit(solution)/shard_map/while/body/eval_jaxpr/ppermute | solution.py:33
  303.4 6.0 %collective-permute-start.1 = (f32[1,32,2,128]{3,1,2,0:T(8,128)S(1)}, f32[1,32,2,128]{3,1,2,0:T(8,128)S(1)}, u32[]{:S(2)}, u32[]{:S(2)}) collective-permute-start(f32[1,32,2,128]{3,1,2,0:T(8,128)S(1)} %bitcast.291), channel_id=1, source_target_pairs={{0,2},{1,3},{2,0},{3,1},{4,6},{5,7},{6,4},{7,5},{8,10},{9,11},{10,... | collective-permute-start | bytes 98312 | tf_op jit(solution)/shard_map/while/body/eval_jaxpr/ppermute | solution.py:33
  368.7 8.2 %collective-permute-start.12 = (f32[1,32,2,128]{3,1,2,0:T(8,128)S(1)}, f32[1,32,2,128]{3,1,2,0:T(8,128)S(1)}, u32[]{:S(2)}, u32[]{:S(2)}) collective-permute-start(f32[1,32,2,128]{3,1,2,0:T(8,128)S(1)} %bitcast.295), channel_id=1, source_target_pairs={{0,2},{1,3},{2,0},{3,1},{4,6},{5,7},{6,4},{7,5},{8,10},{9,11},{10,... | collective-permute-start | bytes 98312 | tf_op jit(solution)/shard_map/ppermute | solution.py:33
  376.9 6.2 %collective-permute-start.11 = (f32[1,32,2,128]{3,1,2,0:T(8,128)S(1)}, f32[1,32,2,128]{3,1,2,0:T(8,128)S(1)}, u32[]{:S(2)}, u32[]{:S(2)}) collective-permute-start(f32[1,32,2,128]{3,1,2,0:T(8,128)S(1)} %bitcast.296), channel_id=1, source_target_pairs={{0,3},{1,0},{2,1},{3,2},{4,7},{5,4},{6,5},{7,6},{8,11},{9,8},{10,9... | collective-permute-start | bytes 98312 | tf_op jit(solution)/shard_map/ppermute | solution.py:33
  406.4 5.2 %collective-permute-done.17 = f32[4,4,1,32,2,128]{5,3,4,1,0,2:T(8,128)S(1)} collective-permute-done((f32[4,4,1,32,2,128]{5,3,4,1,0,2:T(8,128)S(1)}, f32[4,4,1,32,2,128]{5,3,4,1,0,2:T(8,128)S(1)}, u32[]{:S(2)}, u32[]{:S(2)}) %collective-permute-start.17) | collective-permute-done | bytes 524320 | tf_op jit(solution)/shard_map/ppermute | solution.py:33
  431.5 5.4 %collective-permute-start.23 = (f32[1,32,2,128]{3,1,2,0:T(8,128)S(1)}, f32[1,32,2,128]{3,1,2,0:T(8,128)S(1)}, u32[]{:S(2)}, u32[]{:S(2)}) collective-permute-start(f32[1,32,2,128]{3,1,2,0:T(8,128)S(1)} %get-tuple-element.194), channel_id=1, source_target_pairs={{0,1},{1,2},{2,3},{3,0},{4,5},{5,6},{6,7},{7,4},{8,9},{9,10},{10,1... | collective-permute-start | bytes 98312 | tf_op jit(solution)/shard_map/ppermute | solution.py:33
  436.9 8.3 %collective-permute-start.22 = (f32[1,32,2,128]{3,1,2,0:T(8,128)S(1)}, f32[1,32,2,128]{3,1,2,0:T(8,128)S(1)}, u32[]{:S(2)}, u32[]{:S(2)}) collective-permute-start(f32[1,32,2,128]{3,1,2,0:T(8,128)S(1)} %get-tuple-element.194), channel_id=1, source_target_pairs={{0,2},{1,3},{2,0},{3,1},{4,6},{5,7},{6,4},{7,5},{8,10},{9,11},{10,... | collective-permute-start | bytes 98312 | tf_op jit(solution)/shard_map/ppermute | solution.py:33
  471.2 5.1 %collective-permute-start.27 = (f32[4,4,1,32,2,128]{5,3,4,1,0,2:T(8,128)S(1)}, f32[4,4,1,32,2,128]{5,3,4,1,0,2:T(8,128)S(1)}, u32[]{:S(2)}, u32[]{:S(2)}) collective-permute-start(f32[4,4,1,32,2,128]{5,3,4,1,0,2:T(8,128)S(1)} %get-tuple-element.180), channel_id=1, source_target_pairs={{0,48},{1,49},{2,50},{3,51},{4,52},{5,53},{6,54},{7,55},{8,56},{9,... | collective-permute-start | bytes 1572872 | tf_op jit(solution)/shard_map/ppermute | solution.py:33
  478.6 6.7 %collective-permute-done.27 = f32[4,4,1,32,2,128]{5,3,4,1,0,2:T(8,128)S(1)} collective-permute-done((f32[4,4,1,32,2,128]{5,3,4,1,0,2:T(8,128)S(1)}, f32[4,4,1,32,2,128]{5,3,4,1,0,2:T(8,128)S(1)}, u32[]{:S(2)}, u32[]{:S(2)}) %collective-permute-start.27) | collective-permute-done | bytes 524320 | tf_op jit(solution)/shard_map/ppermute | solution.py:33
  485.3 5.6 %collective-permute-start.30 = (f32[2,4,1,32,2,128]{5,3,4,1,0,2:T(8,128)S(1)}, f32[2,4,1,32,2,128]{5,3,4,1,0,2:T(8,128)S(1)}, u32[]{:S(2)}, u32[]{:S(2)}) collective-permute-start(f32[2,4,1,32,2,128]{5,3,4,1,0,2:T(8,128)S(1)} %slice.175), channel_id=1, source_target_pairs={{0,48},{1,49},{2,50},{3,51},{4,52},{5,53},{6,54},{7,55},{8,56},{9,... | collective-permute-start | bytes 786440 | tf_op jit(solution)/shard_map/ppermute | solution.py:33
  494.7 5.6 %collective-permute-done.29 = f32[2,4,1,32,2,128]{5,3,4,1,0,2:T(8,128)S(1)} collective-permute-done((f32[2,4,1,32,2,128]{5,3,4,1,0,2:T(8,128)S(1)}, f32[2,4,1,32,2,128]{5,3,4,1,0,2:T(8,128)S(1)}, u32[]{:S(2)}, u32[]{:S(2)}) %collective-permute-start.29) | collective-permute-done | bytes 262176 | tf_op jit(solution)/shard_map/ppermute | solution.py:33
  (287 shorter events, 354.0 us)
Async XLA Ops:
  10.7 25.5 %collective-permute-start = (f32[1,32,2,128]{3,1,2,0:T(8,128)S(1)}, f32[1,32,2,128]{3,1,2,0:T(8,128)S(1)}, u32[]{:S(2)}, u32[]{:S(2)}) collective-permute-start(f32[1,32,2,128]{3,1,2,0:T(8,128)S(1)} %bitcast.290), channel_id=1, source_target_pairs={{0,1},{1,2},{2,3},{3,0},{4,5},{5,6},{6,7},{7,4},{8,9},{9,10},{10,1... | collective-permute-start | bytes 98312 | tf_op jit(solution)/shard_map/while/body/eval_jaxpr/ppermute | solution.py:33
  19.8 16.4 %collective-permute-start.1 = (f32[1,32,2,128]{3,1,2,0:T(8,128)S(1)}, f32[1,32,2,128]{3,1,2,0:T(8,128)S(1)}, u32[]{:S(2)}, u32[]{:S(2)}) collective-permute-start(f32[1,32,2,128]{3,1,2,0:T(8,128)S(1)} %bitcast.291), channel_id=1, source_target_pairs={{0,2},{1,3},{2,0},{3,1},{4,6},{5,7},{6,4},{7,5},{8,10},{9,11},{10,... | collective-permute-start | bytes 98312 | tf_op jit(solution)/shard_map/while/body/eval_jaxpr/ppermute | solution.py:33
  56.4 13.4 %collective-permute-start.7 = (f32[4,4,1,32,2,128]{5,3,4,1,0,2:T(8,128)S(1)}, f32[4,4,1,32,2,128]{5,3,4,1,0,2:T(8,128)S(1)}, u32[]{:S(2)}, u32[]{:S(2)}) collective-permute-start(f32[4,4,1,32,2,128]{5,3,4,1,0,2:T(8,128)S(1)} %get-tuple-element.232), channel_id=1, source_target_pairs={{0,48},{1,49},{2,50},{3,51},{4,52},{5,53},{6,54},{7,55},{8,56},{9,... | collective-permute-start | bytes 1572872 | tf_op jit(solution)/shard_map/while/body/eval_jaxpr/ppermute | solution.py:33
  61.3 14.1 %collective-permute-start.6 = (f32[4,4,1,32,2,128]{5,3,4,1,2,0:T(8,128)S(1)}, f32[4,4,1,32,2,128]{5,3,4,1,2,0:T(8,128)S(1)}, u32[]{:S(2)}, u32[]{:S(2)}) collective-permute-start(f32[4,4,1,32,2,128]{5,3,4,1,2,0:T(8,128)S(1)} %get-tuple-element.231), channel_id=1, source_target_pairs={{0,16},{1,17},{2,18},{3,19},{4,20},{5,21},{6,22},{7,23},{8,24},{9,... | collective-permute-start | bytes 1572872 | tf_op jit(solution)/shard_map/while/body/eval_jaxpr/ppermute | solution.py:33
  92.4 17.0 %collective-permute-start = (f32[1,32,2,128]{3,1,2,0:T(8,128)S(1)}, f32[1,32,2,128]{3,1,2,0:T(8,128)S(1)}, u32[]{:S(2)}, u32[]{:S(2)}) collective-permute-start(f32[1,32,2,128]{3,1,2,0:T(8,128)S(1)} %bitcast.290), channel_id=1, source_target_pairs={{0,1},{1,2},{2,3},{3,0},{4,5},{5,6},{6,7},{7,4},{8,9},{9,10},{10,1... | collective-permute-start | bytes 98312 | tf_op jit(solution)/shard_map/while/body/eval_jaxpr/ppermute | solution.py:33
  95.7 14.7 %collective-permute-start.1 = (f32[1,32,2,128]{3,1,2,0:T(8,128)S(1)}, f32[1,32,2,128]{3,1,2,0:T(8,128)S(1)}, u32[]{:S(2)}, u32[]{:S(2)}) collective-permute-start(f32[1,32,2,128]{3,1,2,0:T(8,128)S(1)} %bitcast.291), channel_id=1, source_target_pairs={{0,2},{1,3},{2,0},{3,1},{4,6},{5,7},{6,4},{7,5},{8,10},{9,11},{10,... | collective-permute-start | bytes 98312 | tf_op jit(solution)/shard_map/while/body/eval_jaxpr/ppermute | solution.py:33
  128.3 13.9 %collective-permute-start.7 = (f32[4,4,1,32,2,128]{5,3,4,1,0,2:T(8,128)S(1)}, f32[4,4,1,32,2,128]{5,3,4,1,0,2:T(8,128)S(1)}, u32[]{:S(2)}, u32[]{:S(2)}) collective-permute-start(f32[4,4,1,32,2,128]{5,3,4,1,0,2:T(8,128)S(1)} %get-tuple-element.232), channel_id=1, source_target_pairs={{0,48},{1,49},{2,50},{3,51},{4,52},{5,53},{6,54},{7,55},{8,56},{9,... | collective-permute-start | bytes 1572872 | tf_op jit(solution)/shard_map/while/body/eval_jaxpr/ppermute | solution.py:33
  130.3 15.1 %collective-permute-start.6 = (f32[4,4,1,32,2,128]{5,3,4,1,2,0:T(8,128)S(1)}, f32[4,4,1,32,2,128]{5,3,4,1,2,0:T(8,128)S(1)}, u32[]{:S(2)}, u32[]{:S(2)}) collective-permute-start(f32[4,4,1,32,2,128]{5,3,4,1,2,0:T(8,128)S(1)} %get-tuple-element.231), channel_id=1, source_target_pairs={{0,16},{1,17},{2,18},{3,19},{4,20},{5,21},{6,22},{7,23},{8,24},{9,... | collective-permute-start | bytes 1572872 | tf_op jit(solution)/shard_map/while/body/eval_jaxpr/ppermute | solution.py:33
  162.4 15.8 %collective-permute-start = (f32[1,32,2,128]{3,1,2,0:T(8,128)S(1)}, f32[1,32,2,128]{3,1,2,0:T(8,128)S(1)}, u32[]{:S(2)}, u32[]{:S(2)}) collective-permute-start(f32[1,32,2,128]{3,1,2,0:T(8,128)S(1)} %bitcast.290), channel_id=1, source_target_pairs={{0,1},{1,2},{2,3},{3,0},{4,5},{5,6},{6,7},{7,4},{8,9},{9,10},{10,1... | collective-permute-start | bytes 98312 | tf_op jit(solution)/shard_map/while/body/eval_jaxpr/ppermute | solution.py:33
  167.2 14.6 %collective-permute-start.1 = (f32[1,32,2,128]{3,1,2,0:T(8,128)S(1)}, f32[1,32,2,128]{3,1,2,0:T(8,128)S(1)}, u32[]{:S(2)}, u32[]{:S(2)}) collective-permute-start(f32[1,32,2,128]{3,1,2,0:T(8,128)S(1)} %bitcast.291), channel_id=1, source_target_pairs={{0,2},{1,3},{2,0},{3,1},{4,6},{5,7},{6,4},{7,5},{8,10},{9,11},{10,... | collective-permute-start | bytes 98312 | tf_op jit(solution)/shard_map/while/body/eval_jaxpr/ppermute | solution.py:33
  201.0 12.3 %collective-permute-start.6 = (f32[4,4,1,32,2,128]{5,3,4,1,2,0:T(8,128)S(1)}, f32[4,4,1,32,2,128]{5,3,4,1,2,0:T(8,128)S(1)}, u32[]{:S(2)}, u32[]{:S(2)}) collective-permute-start(f32[4,4,1,32,2,128]{5,3,4,1,2,0:T(8,128)S(1)} %get-tuple-element.231), channel_id=1, source_target_pairs={{0,16},{1,17},{2,18},{3,19},{4,20},{5,21},{6,22},{7,23},{8,24},{9,... | collective-permute-start | bytes 1572872 | tf_op jit(solution)/shard_map/while/body/eval_jaxpr/ppermute | solution.py:33
  230.3 16.4 %collective-permute-start = (f32[1,32,2,128]{3,1,2,0:T(8,128)S(1)}, f32[1,32,2,128]{3,1,2,0:T(8,128)S(1)}, u32[]{:S(2)}, u32[]{:S(2)}) collective-permute-start(f32[1,32,2,128]{3,1,2,0:T(8,128)S(1)} %bitcast.290), channel_id=1, source_target_pairs={{0,1},{1,2},{2,3},{3,0},{4,5},{5,6},{6,7},{7,4},{8,9},{9,10},{10,1... | collective-permute-start | bytes 98312 | tf_op jit(solution)/shard_map/while/body/eval_jaxpr/ppermute | solution.py:33
  235.0 14.5 %collective-permute-start.1 = (f32[1,32,2,128]{3,1,2,0:T(8,128)S(1)}, f32[1,32,2,128]{3,1,2,0:T(8,128)S(1)}, u32[]{:S(2)}, u32[]{:S(2)}) collective-permute-start(f32[1,32,2,128]{3,1,2,0:T(8,128)S(1)} %bitcast.291), channel_id=1, source_target_pairs={{0,2},{1,3},{2,0},{3,1},{4,6},{5,7},{6,4},{7,5},{8,10},{9,11},{10,... | collective-permute-start | bytes 98312 | tf_op jit(solution)/shard_map/while/body/eval_jaxpr/ppermute | solution.py:33
  267.0 12.3 %collective-permute-start.6 = (f32[4,4,1,32,2,128]{5,3,4,1,2,0:T(8,128)S(1)}, f32[4,4,1,32,2,128]{5,3,4,1,2,0:T(8,128)S(1)}, u32[]{:S(2)}, u32[]{:S(2)}) collective-permute-start(f32[4,4,1,32,2,128]{5,3,4,1,2,0:T(8,128)S(1)} %get-tuple-element.231), channel_id=1, source_target_pairs={{0,16},{1,17},{2,18},{3,19},{4,20},{5,21},{6,22},{7,23},{8,24},{9,... | collective-permute-start | bytes 1572872 | tf_op jit(solution)/shard_map/while/body/eval_jaxpr/ppermute | solution.py:33
  296.3 18.0 %collective-permute-start = (f32[1,32,2,128]{3,1,2,0:T(8,128)S(1)}, f32[1,32,2,128]{3,1,2,0:T(8,128)S(1)}, u32[]{:S(2)}, u32[]{:S(2)}) collective-permute-start(f32[1,32,2,128]{3,1,2,0:T(8,128)S(1)} %bitcast.290), channel_id=1, source_target_pairs={{0,1},{1,2},{2,3},{3,0},{4,5},{5,6},{6,7},{7,4},{8,9},{9,10},{10,1... | collective-permute-start | bytes 98312 | tf_op jit(solution)/shard_map/while/body/eval_jaxpr/ppermute | solution.py:33
  303.4 15.2 %collective-permute-start.1 = (f32[1,32,2,128]{3,1,2,0:T(8,128)S(1)}, f32[1,32,2,128]{3,1,2,0:T(8,128)S(1)}, u32[]{:S(2)}, u32[]{:S(2)}) collective-permute-start(f32[1,32,2,128]{3,1,2,0:T(8,128)S(1)} %bitcast.291), channel_id=1, source_target_pairs={{0,2},{1,3},{2,0},{3,1},{4,6},{5,7},{6,4},{7,5},{8,10},{9,11},{10,... | collective-permute-start | bytes 98312 | tf_op jit(solution)/shard_map/while/body/eval_jaxpr/ppermute | solution.py:33
  364.7 18.4 %collective-permute-start.13 = (f32[1,32,2,128]{3,1,2,0:T(8,128)S(1)}, f32[1,32,2,128]{3,1,2,0:T(8,128)S(1)}, u32[]{:S(2)}, u32[]{:S(2)}) collective-permute-start(f32[1,32,2,128]{3,1,2,0:T(8,128)S(1)} %bitcast.294), channel_id=1, source_target_pairs={{0,1},{1,2},{2,3},{3,0},{4,5},{5,6},{6,7},{7,4},{8,9},{9,10},{10,1... | collective-permute-start | bytes 98312 | tf_op jit(solution)/shard_map/ppermute | solution.py:33
  368.7 14.6 %collective-permute-start.12 = (f32[1,32,2,128]{3,1,2,0:T(8,128)S(1)}, f32[1,32,2,128]{3,1,2,0:T(8,128)S(1)}, u32[]{:S(2)}, u32[]{:S(2)}) collective-permute-start(f32[1,32,2,128]{3,1,2,0:T(8,128)S(1)} %bitcast.295), channel_id=1, source_target_pairs={{0,2},{1,3},{2,0},{3,1},{4,6},{5,7},{6,4},{7,5},{8,10},{9,11},{10,... | collective-permute-start | bytes 98312 | tf_op jit(solution)/shard_map/ppermute | solution.py:33
  417.5 48.0 %collective-permute-start.31 = (f32[96,2,2048]{2,1,0:T(2,128)}, f32[96,2,2048]{2,1,0:T(2,128)}, u32[]{:S(2)}, u32[]{:S(2)}) collective-permute-start(f32[96,2,2048]{2,1,0:T(2,128)} %bitcast.79), channel_id=1, source_target_pairs={{0,64},{64,0},{128,192},{192,128},{256,320},{320,256},{384,448},{4... | collective-permute-start | bytes 4718600 | tf_op jit(solution)/shard_map/ppermute | solution.py:10
  431.5 21.4 %collective-permute-start.23 = (f32[1,32,2,128]{3,1,2,0:T(8,128)S(1)}, f32[1,32,2,128]{3,1,2,0:T(8,128)S(1)}, u32[]{:S(2)}, u32[]{:S(2)}) collective-permute-start(f32[1,32,2,128]{3,1,2,0:T(8,128)S(1)} %get-tuple-element.194), channel_id=1, source_target_pairs={{0,1},{1,2},{2,3},{3,0},{4,5},{5,6},{6,7},{7,4},{8,9},{9,10},{10,1... | collective-permute-start | bytes 98312 | tf_op jit(solution)/shard_map/ppermute | solution.py:33
  436.9 16.0 %collective-permute-start.22 = (f32[1,32,2,128]{3,1,2,0:T(8,128)S(1)}, f32[1,32,2,128]{3,1,2,0:T(8,128)S(1)}, u32[]{:S(2)}, u32[]{:S(2)}) collective-permute-start(f32[1,32,2,128]{3,1,2,0:T(8,128)S(1)} %get-tuple-element.194), channel_id=1, source_target_pairs={{0,2},{1,3},{2,0},{3,1},{4,6},{5,7},{6,4},{7,5},{8,10},{9,11},{10,... | collective-permute-start | bytes 98312 | tf_op jit(solution)/shard_map/ppermute | solution.py:33
  455.3 13.8 %collective-permute-start.25 = (f32[4,1,32,2,128]{4,2,3,0,1:T(8,128)S(1)}, f32[4,1,32,2,128]{4,2,3,0,1:T(8,128)S(1)}, u32[]{:S(2)}, u32[]{:S(2)}) collective-permute-start(f32[4,1,32,2,128]{4,2,3,0,1:T(8,128)S(1)} %get-tuple-element.188), channel_id=1, source_target_pairs={{0,8},{1,9},{2,10},{3,11},{4,12},{5,13},{6,14},{7,15},{8,0},{9,1},... | collective-permute-start | bytes 393224 | tf_op jit(solution)/shard_map/ppermute | solution.py:33
  469.3 21.6 %collective-permute-start.28 = (f32[4,4,1,32,2,128]{5,3,4,1,2,0:T(8,128)S(1)}, f32[4,4,1,32,2,128]{5,3,4,1,2,0:T(8,128)S(1)}, u32[]{:S(2)}, u32[]{:S(2)}) collective-permute-start(f32[4,4,1,32,2,128]{5,3,4,1,2,0:T(8,128)S(1)} %get-tuple-element.181), channel_id=1, source_target_pairs={{0,16},{1,17},{2,18},{3,19},{4,20},{5,21},{6,22},{7,23},{8,24},{9,... | collective-permute-start | bytes 1572872 | tf_op jit(solution)/shard_map/ppermute | solution.py:33
  471.2 14.0 %collective-permute-start.27 = (f32[4,4,1,32,2,128]{5,3,4,1,0,2:T(8,128)S(1)}, f32[4,4,1,32,2,128]{5,3,4,1,0,2:T(8,128)S(1)}, u32[]{:S(2)}, u32[]{:S(2)}) collective-permute-start(f32[4,4,1,32,2,128]{5,3,4,1,0,2:T(8,128)S(1)} %get-tuple-element.180), channel_id=1, source_target_pairs={{0,48},{1,49},{2,50},{3,51},{4,52},{5,53},{6,54},{7,55},{8,56},{9,... | collective-permute-start | bytes 1572872 | tf_op jit(solution)/shard_map/ppermute | solution.py:33
  (65 other events, 588.3 us)

commit v8 on v6

--- a/solution.py
+++ b/solution.py
@@ -49,22 +49,34 @@
 
 
 def panel_gather(piece):
-    blocks = direct_stage(piece[None], 1)
+    planar = jnp.swapaxes(piece, 0, 1)
+    blocks = direct_stage(planar[None], 1)
     blocks = direct_stage(blocks, 4)
     blocks = relay_stage(blocks, 16)
-    blocks = blocks.reshape((64,) + piece.shape)
+    blocks = jnp.swapaxes(blocks.reshape((64,) + planar.shape), 0, 1)
     me = lax.axis_index("panel")
     target = jnp.arange(64)
     slot = jnp.zeros((64,), jnp.int32)
     for stride in (16, 4, 1):
         offset = (target // stride % 4 - me // stride % 4) % 4
         slot = slot + offset * stride
-    out = jnp.take(blocks, slot, axis=0, mode="clip")
-    return out.reshape((64 * piece.shape[0],) + piece.shape[1:])
+    out = jnp.take(blocks, slot, axis=1, mode="clip")
+    return out.reshape((2, 64 * piece.shape[0], piece.shape[2]))
 
 
 def slice_product(matrix, gathered_piece):
-    return complex_product(matrix, gathered_piece)
+    highest = lax.Precision.HIGH
+    real_part = jnp.dot(
+        matrix[:, 0], gathered_piece[0], precision=highest, preferred_element_type=jnp.float32
+    ) - jnp.dot(
+        matrix[:, 1], gathered_piece[1], precision=highest, preferred_element_type=jnp.float32
+    )
+    imag_part = jnp.dot(
+        matrix[:, 0], gathered_piece[1], precision=highest, preferred_element_type=jnp.float32
+    ) + jnp.dot(
+        matrix[:, 1], gathered_piece[0], precision=highest, preferred_element_type=jnp.float32
+    )
+    return jnp.stack([real_part, imag_part], axis=1)
 
 
 def local(exterior_rows, exterior_block, shared_block, crossing_block):

time: 501 us -> 501 us (level)
    dot_general x0 -> x32, matrix products: none -> 16.8 us  [the longest x8 4.22 us: slice_product(): jnp.dot(matrix[:, 1], gathered_piece[0], precision=highest, preferred_ele...]
    slice x4 -> x11, local copies, waits for them, and re-layouts: 8.83 us -> 21.2 us  [the longest x4 6.97 us: slice_product(): gathered_piece[0]]
    gather x14 -> x7, local copies, waits for them, and re-layouts: 26.3 us -> 14.1 us  [panel_gather(): out = jnp.take(blocks, slot, axis=1, mode='clip')]
  transfers between devices with their start and end apart: 72 -> 72, of which waited for: 45 -> 45; matrix products, arithmetic and copies ran while one was open for 4% -> 5% of each run, Pallas kernels for 0% -> 0%
where the time goes in v8:
time: 501 us; the launch traced here: 499 us
  starting transfers between devices  282 us (56%)
  waiting for transfers between devices  150 us (30%)
  local copies, waits for them, and re-layouts  41.2 us (8%)
  matrix products  18.7 us (4%)
  other arithmetic  5.33 us (1%)
    ppermute x70, starting transfers between devices, shifted_along(): return lax.ppermute(piece, 'panel', pairs)  278 us
    ppermute x70, waiting for transfers between devices, shifted_along(): return lax.ppermute(piece, 'panel', pairs)  150 us
    gather x7, local copies, waits for them, and re-layouts, panel_gather(): out = jnp.take(blocks, slot, axis=1, mode='clip')  14.1 us
  transfers between devices with their start and end apart: 72, of which 45 were waited for; matrix products, arithmetic and copies ran while one was open for 5% of the time, Pallas kernels for 0%

profile of v8, /device:TPU:6, one launch (start us, length us, event | category | flops | bytes accessed | tf_op | source)
XLA Modules:
  0.0 498.6 jit_solution(4481195182411960006)
XLA Ops:
  8.4 9.1 %collective-permute-start.3 = (f32[1,2,32,128]{3,2,1,0:T(8,128)S(1)}, f32[1,2,32,128]{3,2,1,0:T(8,128)S(1)}, u32[]{:S(2)}, u32[]{:S(2)}) collective-permute-start(f32[1,2,32,128]{3,2,1,0:T(8,128)S(1)} %get-tuple-element.84), channel_id=1, source_target_pairs={{0,1},{1,2},{2,3},{3,0},{4,5},{5,6},{6,7},{7,4},{8,9},{9,10},{10,1... | collective-permute-start | bytes 98312 | tf_op jit(solution)/shard_map/ppermute | solution.py:33
  17.5 10.9 %collective-permute-start.2 = (f32[1,2,32,128]{3,2,1,0:T(8,128)S(1)}, f32[1,2,32,128]{3,2,1,0:T(8,128)S(1)}, u32[]{:S(2)}, u32[]{:S(2)}) collective-permute-start(f32[1,2,32,128]{3,2,1,0:T(8,128)S(1)} %get-tuple-element.84), channel_id=1, source_target_pairs={{0,2},{1,3},{2,0},{3,1},{4,6},{5,7},{6,4},{7,5},{8,10},{9,11},{10,... | collective-permute-start | bytes 98312 | tf_op jit(solution)/shard_map/ppermute | solution.py:33
  28.5 5.5 %collective-permute-start.1 = (f32[1,2,32,128]{3,2,1,0:T(8,128)S(1)}, f32[1,2,32,128]{3,2,1,0:T(8,128)S(1)}, u32[]{:S(2)}, u32[]{:S(2)}) collective-permute-start(f32[1,2,32,128]{3,2,1,0:T(8,128)S(1)} %get-tuple-element.84), channel_id=1, source_target_pairs={{0,3},{1,0},{2,1},{3,2},{4,7},{5,4},{6,5},{7,6},{8,11},{9,8},{10,9... | collective-permute-start | bytes 98312 | tf_op jit(solution)/shard_map/ppermute | solution.py:33
  62.4 6.4 %collective-permute-done.7 = f32[4,4,1,2,32,128]{5,4,3,1,0,2:T(8,128)S(1)} collective-permute-done((f32[4,4,1,2,32,128]{5,4,3,1,0,2:T(8,128)}, f32[4,4,1,2,32,128]{5,4,3,1,0,2:T(8,128)S(1)}, u32[]{:S(2)}, u32[]{:S(2)}) %collective-permute-start.7) | collective-permute-done | bytes 524320 | tf_op jit(solution)/shard_map/ppermute | solution.py:33
  68.8 5.5 %collective-permute-start.10 = (f32[2,4,1,2,32,128]{5,4,3,1,0,2:T(8,128)S(1)}, f32[2,4,1,2,32,128]{5,4,3,1,0,2:T(8,128)S(1)}, u32[]{:S(2)}, u32[]{:S(2)}) collective-permute-start(f32[2,4,1,2,32,128]{5,4,3,1,0,2:T(8,128)S(1)} %slice.233), channel_id=1, source_target_pairs={{0,48},{1,49},{2,50},{3,51},{4,52},{5,53},{6,54},{7,55},{8,56},{9,... | collective-permute-start | bytes 786440 | tf_op jit(solution)/shard_map/ppermute | solution.py:33
  78.2 5.7 %collective-permute-done.9 = f32[2,4,1,2,32,128]{5,4,3,1,0,2:T(8,128)S(1)} collective-permute-done((f32[2,4,1,2,32,128]{5,4,3,1,0,2:T(8,128)S(1)}, f32[2,4,1,2,32,128]{5,4,3,1,0,2:T(8,128)S(1)}, u32[]{:S(2)}, u32[]{:S(2)}) %collective-permute-start.9) | collective-permute-done | bytes 262176 | tf_op jit(solution)/shard_map/ppermute | solution.py:33
  94.3 9.3 %collective-permute-start.12 = (f32[1,2,32,128]{3,2,1,0:T(8,128)S(1)}, f32[1,2,32,128]{3,2,1,0:T(8,128)S(1)}, u32[]{:S(2)}, u32[]{:S(2)}) collective-permute-start(f32[1,2,32,128]{3,2,1,0:T(8,128)S(1)} %get-tuple-element.76), channel_id=1, source_target_pairs={{0,2},{1,3},{2,0},{3,1},{4,6},{5,7},{6,4},{7,5},{8,10},{9,11},{10,... | collective-permute-start | bytes 98312 | tf_op jit(solution)/shard_map/ppermute | solution.py:33
  132.8 8.0 %collective-permute-done.17 = f32[4,4,1,2,32,128]{5,4,3,1,0,2:T(8,128)S(1)} collective-permute-done((f32[4,4,1,2,32,128]{5,4,3,1,0,2:T(8,128)S(1)}, f32[4,4,1,2,32,128]{5,4,3,1,0,2:T(8,128)S(1)}, u32[]{:S(2)}, u32[]{:S(2)}) %collective-permute-start.17) | collective-permute-done | bytes 524320 | tf_op jit(solution)/shard_map/ppermute | solution.py:33
  164.1 7.6 %collective-permute-start.22 = (f32[1,2,32,128]{3,2,1,0:T(8,128)S(1)}, f32[1,2,32,128]{3,2,1,0:T(8,128)S(1)}, u32[]{:S(2)}, u32[]{:S(2)}) collective-permute-start(f32[1,2,32,128]{3,2,1,0:T(8,128)S(1)} %get-tuple-element.82), channel_id=1, source_target_pairs={{0,2},{1,3},{2,0},{3,1},{4,6},{5,7},{6,4},{7,5},{8,10},{9,11},{10,... | collective-permute-start | bytes 98312 | tf_op jit(solution)/shard_map/ppermute | solution.py:33
  201.8 5.2 %collective-permute-done.27 = f32[4,4,1,2,32,128]{5,4,3,1,0,2:T(8,128)S(1)} collective-permute-done((f32[4,4,1,2,32,128]{5,4,3,1,0,2:T(8,128)S(1)}, f32[4,4,1,2,32,128]{5,4,3,1,0,2:T(8,128)S(1)}, u32[]{:S(2)}, u32[]{:S(2)}) %collective-permute-start.27) | collective-permute-done | bytes 524320 | tf_op jit(solution)/shard_map/ppermute | solution.py:33
  230.2 6.2 %collective-permute-start.32 = (f32[1,2,32,128]{3,2,1,0:T(8,128)S(1)}, f32[1,2,32,128]{3,2,1,0:T(8,128)S(1)}, u32[]{:S(2)}, u32[]{:S(2)}) collective-permute-start(f32[1,2,32,128]{3,2,1,0:T(8,128)S(1)} %get-tuple-element.74), channel_id=1, source_target_pairs={{0,2},{1,3},{2,0},{3,1},{4,6},{5,7},{6,4},{7,5},{8,10},{9,11},{10,... | collective-permute-start | bytes 98312 | tf_op jit(solution)/shard_map/ppermute | solution.py:33
  236.4 5.5 %collective-permute-start.31 = (f32[1,2,32,128]{3,2,1,0:T(8,128)S(1)}, f32[1,2,32,128]{3,2,1,0:T(8,128)S(1)}, u32[]{:S(2)}, u32[]{:S(2)}) collective-permute-start(f32[1,2,32,128]{3,2,1,0:T(8,128)S(1)} %get-tuple-element.74), channel_id=1, source_target_pairs={{0,3},{1,0},{2,1},{3,2},{4,7},{5,4},{6,5},{7,6},{8,11},{9,8},{10,9... | collective-permute-start | bytes 98312 | tf_op jit(solution)/shard_map/ppermute | solution.py:33
  266.1 5.2 %collective-permute-done.37 = f32[4,4,1,2,32,128]{5,4,3,1,0,2:T(8,128)S(1)} collective-permute-done((f32[4,4,1,2,32,128]{5,4,3,1,0,2:T(8,128)S(1)}, f32[4,4,1,2,32,128]{5,4,3,1,0,2:T(8,128)S(1)}, u32[]{:S(2)}, u32[]{:S(2)}) %collective-permute-start.37) | collective-permute-done | bytes 524320 | tf_op jit(solution)/shard_map/ppermute | solution.py:33
  289.8 7.1 %collective-permute-start.43 = (f32[1,2,32,128]{3,2,1,0:T(8,128)S(1)}, f32[1,2,32,128]{3,2,1,0:T(8,128)S(1)}, u32[]{:S(2)}, u32[]{:S(2)}) collective-permute-start(f32[1,2,32,128]{3,2,1,0:T(8,128)S(1)} %get-tuple-element.80), channel_id=1, source_target_pairs={{0,1},{1,2},{2,3},{3,0},{4,5},{5,6},{6,7},{7,4},{8,9},{9,10},{10,1... | collective-permute-start | bytes 98312 | tf_op jit(solution)/shard_map/ppermute | solution.py:33
  296.9 5.9 %collective-permute-start.42 = (f32[1,2,32,128]{3,2,1,0:T(8,128)S(1)}, f32[1,2,32,128]{3,2,1,0:T(8,128)S(1)}, u32[]{:S(2)}, u32[]{:S(2)}) collective-permute-start(f32[1,2,32,128]{3,2,1,0:T(8,128)S(1)} %get-tuple-element.80), channel_id=1, source_target_pairs={{0,2},{1,3},{2,0},{3,1},{4,6},{5,7},{6,4},{7,5},{8,10},{9,11},{10,... | collective-permute-start | bytes 98312 | tf_op jit(solution)/shard_map/ppermute | solution.py:33
  332.8 5.2 %collective-permute-done.47 = f32[4,4,1,2,32,128]{5,4,3,1,0,2:T(8,128)S(1)} collective-permute-done((f32[4,4,1,2,32,128]{5,4,3,1,0,2:T(8,128)S(1)}, f32[4,4,1,2,32,128]{5,4,3,1,0,2:T(8,128)S(1)}, u32[]{:S(2)}, u32[]{:S(2)}) %collective-permute-start.47) | collective-permute-done | bytes 524320 | tf_op jit(solution)/shard_map/ppermute | solution.py:33
  360.5 8.2 %collective-permute-start.52 = (f32[1,2,32,128]{3,2,1,0:T(8,128)S(1)}, f32[1,2,32,128]{3,2,1,0:T(8,128)S(1)}, u32[]{:S(2)}, u32[]{:S(2)}) collective-permute-start(f32[1,2,32,128]{3,2,1,0:T(8,128)S(1)} %get-tuple-element.72), channel_id=1, source_target_pairs={{0,2},{1,3},{2,0},{3,1},{4,6},{5,7},{6,4},{7,5},{8,10},{9,11},{10,... | collective-permute-start | bytes 98312 | tf_op jit(solution)/shard_map/ppermute | solution.py:33
  368.7 6.2 %collective-permute-start.51 = (f32[1,2,32,128]{3,2,1,0:T(8,128)S(1)}, f32[1,2,32,128]{3,2,1,0:T(8,128)S(1)}, u32[]{:S(2)}, u32[]{:S(2)}) collective-permute-start(f32[1,2,32,128]{3,2,1,0:T(8,128)S(1)} %get-tuple-element.72), channel_id=1, source_target_pairs={{0,3},{1,0},{2,1},{3,2},{4,7},{5,4},{6,5},{7,6},{8,11},{9,8},{10,9... | collective-permute-start | bytes 98312 | tf_op jit(solution)/shard_map/ppermute | solution.py:33
  398.1 5.2 %collective-permute-done.57 = f32[4,4,1,2,32,128]{5,4,3,1,0,2:T(8,128)S(1)} collective-permute-done((f32[4,4,1,2,32,128]{5,4,3,1,0,2:T(8,128)S(1)}, f32[4,4,1,2,32,128]{5,4,3,1,0,2:T(8,128)S(1)}, u32[]{:S(2)}, u32[]{:S(2)}) %collective-permute-start.57) | collective-permute-done | bytes 524320 | tf_op jit(solution)/shard_map/ppermute | solution.py:33
  421.8 5.4 %collective-permute-start.63 = (f32[1,2,32,128]{3,2,1,0:T(8,128)S(1)}, f32[1,2,32,128]{3,2,1,0:T(8,128)S(1)}, u32[]{:S(2)}, u32[]{:S(2)}) collective-permute-start(f32[1,2,32,128]{3,2,1,0:T(8,128)S(1)} %get-tuple-element.78), channel_id=1, source_target_pairs={{0,1},{1,2},{2,3},{3,0},{4,5},{5,6},{6,7},{7,4},{8,9},{9,10},{10,1... | collective-permute-start | bytes 98312 | tf_op jit(solution)/shard_map/ppermute | solution.py:33
  427.2 8.3 %collective-permute-start.62 = (f32[1,2,32,128]{3,2,1,0:T(8,128)S(1)}, f32[1,2,32,128]{3,2,1,0:T(8,128)S(1)}, u32[]{:S(2)}, u32[]{:S(2)}) collective-permute-start(f32[1,2,32,128]{3,2,1,0:T(8,128)S(1)} %get-tuple-element.78), channel_id=1, source_target_pairs={{0,2},{1,3},{2,0},{3,1},{4,6},{5,7},{6,4},{7,5},{8,10},{9,11},{10,... | collective-permute-start | bytes 98312 | tf_op jit(solution)/shard_map/ppermute | solution.py:33
  469.0 6.4 %collective-permute-done.67 = f32[4,4,1,2,32,128]{5,4,3,1,0,2:T(8,128)S(1)} collective-permute-done((f32[4,4,1,2,32,128]{5,4,3,1,0,2:T(8,128)S(1)}, f32[4,4,1,2,32,128]{5,4,3,1,0,2:T(8,128)S(1)}, u32[]{:S(2)}, u32[]{:S(2)}) %collective-permute-start.67) | collective-permute-done | bytes 524320 | tf_op jit(solution)/shard_map/ppermute | solution.py:33
  475.5 5.6 %collective-permute-start.70 = (f32[2,4,1,2,32,128]{5,4,3,1,0,2:T(8,128)S(1)}, f32[2,4,1,2,32,128]{5,4,3,1,0,2:T(8,128)S(1)}, u32[]{:S(2)}, u32[]{:S(2)}) collective-permute-start(f32[2,4,1,2,32,128]{5,4,3,1,0,2:T(8,128)S(1)} %slice.259), channel_id=1, source_target_pairs={{0,48},{1,49},{2,50},{3,51},{4,52},{5,53},{6,54},{7,55},{8,56},{9,... | collective-permute-start | bytes 786440 | tf_op jit(solution)/shard_map/ppermute | solution.py:33
  484.9 5.6 %collective-permute-done.69 = f32[2,4,1,2,32,128]{5,4,3,1,0,2:T(8,128)S(1)} collective-permute-done((f32[2,4,1,2,32,128]{5,4,3,1,0,2:T(8,128)S(1)}, f32[2,4,1,2,32,128]{5,4,3,1,0,2:T(8,128)S(1)}, u32[]{:S(2)}, u32[]{:S(2)}) %collective-permute-start.69) | collective-permute-done | bytes 262176 | tf_op jit(solution)/shard_map/ppermute | solution.py:33
  (243 shorter events, 337.6 us)
Async XLA Ops:
  8.4 25.5 %collective-permute-start.3 = (f32[1,2,32,128]{3,2,1,0:T(8,128)S(1)}, f32[1,2,32,128]{3,2,1,0:T(8,128)S(1)}, u32[]{:S(2)}, u32[]{:S(2)}) collective-permute-start(f32[1,2,32,128]{3,2,1,0:T(8,128)S(1)} %get-tuple-element.84), channel_id=1, source_target_pairs={{0,1},{1,2},{2,3},{3,0},{4,5},{5,6},{6,7},{7,4},{8,9},{9,10},{10,1... | collective-permute-start | bytes 98312 | tf_op jit(solution)/shard_map/ppermute | solution.py:33
  17.5 16.4 %collective-permute-start.2 = (f32[1,2,32,128]{3,2,1,0:T(8,128)S(1)}, f32[1,2,32,128]{3,2,1,0:T(8,128)S(1)}, u32[]{:S(2)}, u32[]{:S(2)}) collective-permute-start(f32[1,2,32,128]{3,2,1,0:T(8,128)S(1)} %get-tuple-element.84), channel_id=1, source_target_pairs={{0,2},{1,3},{2,0},{3,1},{4,6},{5,7},{6,4},{7,5},{8,10},{9,11},{10,... | collective-permute-start | bytes 98312 | tf_op jit(solution)/shard_map/ppermute | solution.py:33
  55.1 13.7 %collective-permute-start.7 = (f32[4,4,1,2,32,128]{5,4,3,1,0,2:T(8,128)}, f32[4,4,1,2,32,128]{5,4,3,1,0,2:T(8,128)S(1)}, u32[]{:S(2)}, u32[]{:S(2)}) collective-permute-start(f32[4,4,1,2,32,128]{5,4,3,1,0,2:T(8,128)} %get-tuple-element.46), channel_id=1, source_target_pairs={{0,48},{1,49},{2,50},{3,51},{4,52},{5,53},{6,54},{7,55},{8,56},{9,... | collective-permute-start | bytes 1572872 | tf_op jit(solution)/shard_map/ppermute | solution.py:33
  60.0 14.4 %collective-permute-start.8 = (f32[4,4,1,2,32,128]{5,4,3,1,2,0:T(8,128)S(1)}, f32[4,4,1,2,32,128]{5,4,3,1,2,0:T(8,128)S(1)}, u32[]{:S(2)}, u32[]{:S(2)}) collective-permute-start(f32[4,4,1,2,32,128]{5,4,3,1,2,0:T(8,128)S(1)} %get-tuple-element.47), channel_id=1, source_target_pairs={{0,16},{1,17},{2,18},{3,19},{4,20},{5,21},{6,22},{7,23},{8,24},{9,... | collective-permute-start | bytes 1572872 | tf_op jit(solution)/shard_map/ppermute | solution.py:33
  91.1 16.8 %collective-permute-start.13 = (f32[1,2,32,128]{3,2,1,0:T(8,128)S(1)}, f32[1,2,32,128]{3,2,1,0:T(8,128)S(1)}, u32[]{:S(2)}, u32[]{:S(2)}) collective-permute-start(f32[1,2,32,128]{3,2,1,0:T(8,128)S(1)} %get-tuple-element.76), channel_id=1, source_target_pairs={{0,1},{1,2},{2,3},{3,0},{4,5},{5,6},{6,7},{7,4},{8,9},{9,10},{10,1... | collective-permute-start | bytes 98312 | tf_op jit(solution)/shard_map/ppermute | solution.py:33
  94.3 14.7 %collective-permute-start.12 = (f32[1,2,32,128]{3,2,1,0:T(8,128)S(1)}, f32[1,2,32,128]{3,2,1,0:T(8,128)S(1)}, u32[]{:S(2)}, u32[]{:S(2)}) collective-permute-start(f32[1,2,32,128]{3,2,1,0:T(8,128)S(1)} %get-tuple-element.76), channel_id=1, source_target_pairs={{0,2},{1,3},{2,0},{3,1},{4,6},{5,7},{6,4},{7,5},{8,10},{9,11},{10,... | collective-permute-start | bytes 98312 | tf_op jit(solution)/shard_map/ppermute | solution.py:33
  126.9 13.9 %collective-permute-start.17 = (f32[4,4,1,2,32,128]{5,4,3,1,0,2:T(8,128)S(1)}, f32[4,4,1,2,32,128]{5,4,3,1,0,2:T(8,128)S(1)}, u32[]{:S(2)}, u32[]{:S(2)}) collective-permute-start(f32[4,4,1,2,32,128]{5,4,3,1,0,2:T(8,128)S(1)} %get-tuple-element.41), channel_id=1, source_target_pairs={{0,48},{1,49},{2,50},{3,51},{4,52},{5,53},{6,54},{7,55},{8,56},{9,... | collective-permute-start | bytes 1572872 | tf_op jit(solution)/shard_map/ppermute | solution.py:33
  128.9 15.1 %collective-permute-start.18 = (f32[4,4,1,2,32,128]{5,4,3,1,2,0:T(8,128)S(1)}, f32[4,4,1,2,32,128]{5,4,3,1,2,0:T(8,128)S(1)}, u32[]{:S(2)}, u32[]{:S(2)}) collective-permute-start(f32[4,4,1,2,32,128]{5,4,3,1,2,0:T(8,128)S(1)} %get-tuple-element.42), channel_id=1, source_target_pairs={{0,16},{1,17},{2,18},{3,19},{4,20},{5,21},{6,22},{7,23},{8,24},{9,... | collective-permute-start | bytes 1572872 | tf_op jit(solution)/shard_map/ppermute | solution.py:33
  159.3 15.8 %collective-permute-start.23 = (f32[1,2,32,128]{3,2,1,0:T(8,128)S(1)}, f32[1,2,32,128]{3,2,1,0:T(8,128)S(1)}, u32[]{:S(2)}, u32[]{:S(2)}) collective-permute-start(f32[1,2,32,128]{3,2,1,0:T(8,128)S(1)} %get-tuple-element.82), channel_id=1, source_target_pairs={{0,1},{1,2},{2,3},{3,0},{4,5},{5,6},{6,7},{7,4},{8,9},{9,10},{10,1... | collective-permute-start | bytes 98312 | tf_op jit(solution)/shard_map/ppermute | solution.py:33
  164.1 14.6 %collective-permute-start.22 = (f32[1,2,32,128]{3,2,1,0:T(8,128)S(1)}, f32[1,2,32,128]{3,2,1,0:T(8,128)S(1)}, u32[]{:S(2)}, u32[]{:S(2)}) collective-permute-start(f32[1,2,32,128]{3,2,1,0:T(8,128)S(1)} %get-tuple-element.82), channel_id=1, source_target_pairs={{0,2},{1,3},{2,0},{3,1},{4,6},{5,7},{6,4},{7,5},{8,10},{9,11},{10,... | collective-permute-start | bytes 98312 | tf_op jit(solution)/shard_map/ppermute | solution.py:33
  197.9 12.3 %collective-permute-start.28 = (f32[4,4,1,2,32,128]{5,4,3,1,2,0:T(8,128)S(1)}, f32[4,4,1,2,32,128]{5,4,3,1,2,0:T(8,128)S(1)}, u32[]{:S(2)}, u32[]{:S(2)}) collective-permute-start(f32[4,4,1,2,32,128]{5,4,3,1,2,0:T(8,128)S(1)} %get-tuple-element.39), channel_id=1, source_target_pairs={{0,16},{1,17},{2,18},{3,19},{4,20},{5,21},{6,22},{7,23},{8,24},{9,... | collective-permute-start | bytes 1572872 | tf_op jit(solution)/shard_map/ppermute | solution.py:33
  225.5 16.4 %collective-permute-start.33 = (f32[1,2,32,128]{3,2,1,0:T(8,128)S(1)}, f32[1,2,32,128]{3,2,1,0:T(8,128)S(1)}, u32[]{:S(2)}, u32[]{:S(2)}) collective-permute-start(f32[1,2,32,128]{3,2,1,0:T(8,128)S(1)} %get-tuple-element.74), channel_id=1, source_target_pairs={{0,1},{1,2},{2,3},{3,0},{4,5},{5,6},{6,7},{7,4},{8,9},{9,10},{10,1... | collective-permute-start | bytes 98312 | tf_op jit(solution)/shard_map/ppermute | solution.py:33
  230.2 14.5 %collective-permute-start.32 = (f32[1,2,32,128]{3,2,1,0:T(8,128)S(1)}, f32[1,2,32,128]{3,2,1,0:T(8,128)S(1)}, u32[]{:S(2)}, u32[]{:S(2)}) collective-permute-start(f32[1,2,32,128]{3,2,1,0:T(8,128)S(1)} %get-tuple-element.74), channel_id=1, source_target_pairs={{0,2},{1,3},{2,0},{3,1},{4,6},{5,7},{6,4},{7,5},{8,10},{9,11},{10,... | collective-permute-start | bytes 98312 | tf_op jit(solution)/shard_map/ppermute | solution.py:33
  289.8 18.0 %collective-permute-start.43 = (f32[1,2,32,128]{3,2,1,0:T(8,128)S(1)}, f32[1,2,32,128]{3,2,1,0:T(8,128)S(1)}, u32[]{:S(2)}, u32[]{:S(2)}) collective-permute-start(f32[1,2,32,128]{3,2,1,0:T(8,128)S(1)} %get-tuple-element.80), channel_id=1, source_target_pairs={{0,1},{1,2},{2,3},{3,0},{4,5},{5,6},{6,7},{7,4},{8,9},{9,10},{10,1... | collective-permute-start | bytes 98312 | tf_op jit(solution)/shard_map/ppermute | solution.py:33
  296.9 15.2 %collective-permute-start.42 = (f32[1,2,32,128]{3,2,1,0:T(8,128)S(1)}, f32[1,2,32,128]{3,2,1,0:T(8,128)S(1)}, u32[]{:S(2)}, u32[]{:S(2)}) collective-permute-start(f32[1,2,32,128]{3,2,1,0:T(8,128)S(1)} %get-tuple-element.80), channel_id=1, source_target_pairs={{0,2},{1,3},{2,0},{3,1},{4,6},{5,7},{6,4},{7,5},{8,10},{9,11},{10,... | collective-permute-start | bytes 98312 | tf_op jit(solution)/shard_map/ppermute | solution.py:33
  356.5 18.5 %collective-permute-start.53 = (f32[1,2,32,128]{3,2,1,0:T(8,128)S(1)}, f32[1,2,32,128]{3,2,1,0:T(8,128)S(1)}, u32[]{:S(2)}, u32[]{:S(2)}) collective-permute-start(f32[1,2,32,128]{3,2,1,0:T(8,128)S(1)} %get-tuple-element.72), channel_id=1, source_target_pairs={{0,1},{1,2},{2,3},{3,0},{4,5},{5,6},{6,7},{7,4},{8,9},{9,10},{10,1... | collective-permute-start | bytes 98312 | tf_op jit(solution)/shard_map/ppermute | solution.py:33
  360.5 14.6 %collective-permute-start.52 = (f32[1,2,32,128]{3,2,1,0:T(8,128)S(1)}, f32[1,2,32,128]{3,2,1,0:T(8,128)S(1)}, u32[]{:S(2)}, u32[]{:S(2)}) collective-permute-start(f32[1,2,32,128]{3,2,1,0:T(8,128)S(1)} %get-tuple-element.72), channel_id=1, source_target_pairs={{0,2},{1,3},{2,0},{3,1},{4,6},{5,7},{6,4},{7,5},{8,10},{9,11},{10,... | collective-permute-start | bytes 98312 | tf_op jit(solution)/shard_map/ppermute | solution.py:33
  394.2 12.3 %collective-permute-start.58 = (f32[4,4,1,2,32,128]{5,4,3,1,2,0:T(8,128)S(1)}, f32[4,4,1,2,32,128]{5,4,3,1,2,0:T(8,128)S(1)}, u32[]{:S(2)}, u32[]{:S(2)}) collective-permute-start(f32[4,4,1,2,32,128]{5,4,3,1,2,0:T(8,128)S(1)} %get-tuple-element.30), channel_id=1, source_target_pairs={{0,16},{1,17},{2,18},{3,19},{4,20},{5,21},{6,22},{7,23},{8,24},{9,... | collective-permute-start | bytes 1572872 | tf_op jit(solution)/shard_map/ppermute | solution.py:33
  409.2 46.7 %collective-permute-start.71 = (f32[96,2,2048]{2,1,0:T(2,128)}, f32[96,2,2048]{2,1,0:T(2,128)}, u32[]{:S(2)}, u32[]{:S(2)}) collective-permute-start(f32[96,2,2048]{2,1,0:T(2,128)} %bitcast.199), channel_id=1, source_target_pairs={{0,64},{64,0},{128,192},{192,128},{256,320},{320,256},{384,448},{4... | collective-permute-start | bytes 4718600 | tf_op jit(solution)/shard_map/ppermute | solution.py:10
  421.8 21.6 %collective-permute-start.63 = (f32[1,2,32,128]{3,2,1,0:T(8,128)S(1)}, f32[1,2,32,128]{3,2,1,0:T(8,128)S(1)}, u32[]{:S(2)}, u32[]{:S(2)}) collective-permute-start(f32[1,2,32,128]{3,2,1,0:T(8,128)S(1)} %get-tuple-element.78), channel_id=1, source_target_pairs={{0,1},{1,2},{2,3},{3,0},{4,5},{5,6},{6,7},{7,4},{8,9},{9,10},{10,1... | collective-permute-start | bytes 98312 | tf_op jit(solution)/shard_map/ppermute | solution.py:33
  427.2 16.2 %collective-permute-start.62 = (f32[1,2,32,128]{3,2,1,0:T(8,128)S(1)}, f32[1,2,32,128]{3,2,1,0:T(8,128)S(1)}, u32[]{:S(2)}, u32[]{:S(2)}) collective-permute-start(f32[1,2,32,128]{3,2,1,0:T(8,128)S(1)} %get-tuple-element.78), channel_id=1, source_target_pairs={{0,2},{1,3},{2,0},{3,1},{4,6},{5,7},{6,4},{7,5},{8,10},{9,11},{10,... | collective-permute-start | bytes 98312 | tf_op jit(solution)/shard_map/ppermute | solution.py:33
  445.7 13.8 %collective-permute-start.65 = (f32[4,1,2,32,128]{4,3,2,0,1:T(8,128)S(1)}, f32[4,1,2,32,128]{4,3,2,0,1:T(8,128)S(1)}, u32[]{:S(2)}, u32[]{:S(2)}) collective-permute-start(f32[4,1,2,32,128]{4,3,2,0,1:T(8,128)S(1)} %get-tuple-element.51), channel_id=1, source_target_pairs={{0,8},{1,9},{2,10},{3,11},{4,12},{5,13},{6,14},{7,15},{8,0},{9,1},... | collective-permute-start | bytes 393224 | tf_op jit(solution)/shard_map/ppermute | solution.py:33
  459.7 21.4 %collective-permute-start.68 = (f32[4,4,1,2,32,128]{5,4,3,1,2,0:T(8,128)S(1)}, f32[4,4,1,2,32,128]{5,4,3,1,2,0:T(8,128)S(1)}, u32[]{:S(2)}, u32[]{:S(2)}) collective-permute-start(f32[4,4,1,2,32,128]{5,4,3,1,2,0:T(8,128)S(1)} %get-tuple-element.27), channel_id=1, source_target_pairs={{0,16},{1,17},{2,18},{3,19},{4,20},{5,21},{6,22},{7,23},{8,24},{9,... | collective-permute-start | bytes 1572872 | tf_op jit(solution)/shard_map/ppermute | solution.py:33
  461.6 13.8 %collective-permute-start.67 = (f32[4,4,1,2,32,128]{5,4,3,1,0,2:T(8,128)S(1)}, f32[4,4,1,2,32,128]{5,4,3,1,0,2:T(8,128)S(1)}, u32[]{:S(2)}, u32[]{:S(2)}) collective-permute-start(f32[4,4,1,2,32,128]{5,4,3,1,0,2:T(8,128)S(1)} %get-tuple-element.26), channel_id=1, source_target_pairs={{0,48},{1,49},{2,50},{3,51},{4,52},{5,53},{6,54},{7,55},{8,56},{9,... | collective-permute-start | bytes 1572872 | tf_op jit(solution)/shard_map/ppermute | solution.py:33
  (54 other events, 526.3 us)

commit v9 on v8

--- a/solution.py
+++ b/solution.py
@@ -51,15 +51,15 @@
 def panel_gather(piece):
     planar = jnp.swapaxes(piece, 0, 1)
     blocks = direct_stage(planar[None], 1)
-    blocks = direct_stage(blocks, 4)
-    blocks = relay_stage(blocks, 16)
+    blocks = direct_stage(blocks, 16)
+    blocks = relay_stage(blocks, 4)
     blocks = jnp.swapaxes(blocks.reshape((64,) + planar.shape), 0, 1)
     me = lax.axis_index("panel")
     target = jnp.arange(64)
     slot = jnp.zeros((64,), jnp.int32)
-    for stride in (16, 4, 1):
+    for stride, place in ((4, 16), (16, 4), (1, 1)):
         offset = (target // stride % 4 - me // stride % 4) % 4
-        slot = slot + offset * stride
+        slot = slot + offset * place
     out = jnp.take(blocks, slot, axis=1, mode="clip")
     return out.reshape((2, 64 * piece.shape[0], piece.shape[2]))
 

time: 501 us -> 501 us (level)
  waiting for transfers between devices: 150 us -> 129 us
  starting transfers between devices: 282 us -> 301 us
    ppermute x70, waiting for transfers between devices: 150 us -> 129 us  [shifted_along(): return lax.ppermute(piece, 'panel', pairs)]
    ppermute x70, starting transfers between devices: 278 us -> 297 us  [shifted_along(): return lax.ppermute(piece, 'panel', pairs)]
  transfers between devices with their start and end apart: 72 -> 72, of which waited for: 45 -> 46; matrix products, arithmetic and copies ran while one was open for 5% -> 5% of each run, Pallas kernels for 0% -> 0%
where the time goes in v9:
time: 501 us; the launch traced here: 497 us
  starting transfers between devices  301 us (60%)
  waiting for transfers between devices  129 us (26%)
  local copies, waits for them, and re-layouts  41.2 us (8%)
  matrix products  18.7 us (4%)
  other arithmetic  5.33 us (1%)
    ppermute x70, starting transfers between devices, shifted_along(): return lax.ppermute(piece, 'panel', pairs)  297 us
    ppermute x70, waiting for transfers between devices, shifted_along(): return lax.ppermute(piece, 'panel', pairs)  129 us
    gather x7, local copies, waits for them, and re-layouts, panel_gather(): out = jnp.take(blocks, slot, axis=1, mode='clip')  14.1 us
  transfers between devices with their start and end apart: 72, of which 46 were waited for; matrix products, arithmetic and copies ran while one was open for 5% of the time, Pallas kernels for 0%

profile of v9, /device:TPU:6, one launch (start us, length us, event | category | flops | bytes accessed | tf_op | source)
XLA Modules:
  0.0 496.7 jit_solution(10710833128864280667)
XLA Ops:
  8.4 9.1 %collective-permute-start.3 = (f32[1,2,32,128]{3,2,1,0:T(8,128)S(1)}, f32[1,2,32,128]{3,2,1,0:T(8,128)S(1)}, u32[]{:S(2)}, u32[]{:S(2)}) collective-permute-start(f32[1,2,32,128]{3,2,1,0:T(8,128)S(1)} %get-tuple-element.84), channel_id=1, source_target_pairs={{0,1},{1,2},{2,3},{3,0},{4,5},{5,6},{6,7},{7,4},{8,9},{9,10},{10,1... | collective-permute-start | bytes 98312 | tf_op jit(solution)/shard_map/ppermute | solution.py:33
  17.5 10.9 %collective-permute-start.2 = (f32[1,2,32,128]{3,2,1,0:T(8,128)S(1)}, f32[1,2,32,128]{3,2,1,0:T(8,128)S(1)}, u32[]{:S(2)}, u32[]{:S(2)}) collective-permute-start(f32[1,2,32,128]{3,2,1,0:T(8,128)S(1)} %get-tuple-element.84), channel_id=1, source_target_pairs={{0,2},{1,3},{2,0},{3,1},{4,6},{5,7},{6,4},{7,5},{8,10},{9,11},{10,... | collective-permute-start | bytes 98312 | tf_op jit(solution)/shard_map/ppermute | solution.py:33
  28.5 5.5 %collective-permute-start.1 = (f32[1,2,32,128]{3,2,1,0:T(8,128)S(1)}, f32[1,2,32,128]{3,2,1,0:T(8,128)S(1)}, u32[]{:S(2)}, u32[]{:S(2)}) collective-permute-start(f32[1,2,32,128]{3,2,1,0:T(8,128)S(1)} %get-tuple-element.84), channel_id=1, source_target_pairs={{0,3},{1,0},{2,1},{3,2},{4,7},{5,4},{6,5},{7,6},{8,11},{9,8},{10,9... | collective-permute-start | bytes 98312 | tf_op jit(solution)/shard_map/ppermute | solution.py:33
  63.0 6.5 %collective-permute-done.7 = f32[4,4,1,2,32,128]{5,4,3,1,0,2:T(8,128)S(1)} collective-permute-done((f32[4,4,1,2,32,128]{5,4,3,1,0,2:T(8,128)}, f32[4,4,1,2,32,128]{5,4,3,1,0,2:T(8,128)S(1)}, u32[]{:S(2)}, u32[]{:S(2)}) %collective-permute-start.7) | collective-permute-done | bytes 524320 | tf_op jit(solution)/shard_map/ppermute | solution.py:33
  90.9 9.3 %collective-permute-start.12 = (f32[1,2,32,128]{3,2,1,0:T(8,128)S(1)}, f32[1,2,32,128]{3,2,1,0:T(8,128)S(1)}, u32[]{:S(2)}, u32[]{:S(2)}) collective-permute-start(f32[1,2,32,128]{3,2,1,0:T(8,128)S(1)} %get-tuple-element.76), channel_id=1, source_target_pairs={{0,2},{1,3},{2,0},{3,1},{4,6},{5,7},{6,4},{7,5},{8,10},{9,11},{10,... | collective-permute-start | bytes 98312 | tf_op jit(solution)/shard_map/ppermute | solution.py:33
  111.9 6.0 %collective-permute-start.15 = (f32[4,1,2,32,128]{4,3,2,0,1:T(8,128)S(1)}, f32[4,1,2,32,128]{4,3,2,0,1:T(8,128)S(1)}, u32[]{:S(2)}, u32[]{:S(2)}) collective-permute-start(f32[4,1,2,32,128]{4,3,2,0,1:T(8,128)S(1)} %get-tuple-element.66), channel_id=1, source_target_pairs={{0,32},{1,33},{2,34},{3,35},{4,36},{5,37},{6,38},{7,39},{8,40},{9,... | collective-permute-start | bytes 393224 | tf_op jit(solution)/shard_map/ppermute | solution.py:33
  126.9 5.6 %collective-permute-start.18 = (f32[4,4,1,2,32,128]{5,4,3,1,2,0:T(8,128)S(1)}, f32[4,4,1,2,32,128]{5,4,3,1,2,0:T(8,128)S(1)}, u32[]{:S(2)}, u32[]{:S(2)}) collective-permute-start(f32[4,4,1,2,32,128]{5,4,3,1,2,0:T(8,128)S(1)} %get-tuple-element.42), channel_id=1, source_target_pairs={{0,4},{1,5},{2,6},{3,7},{4,8},{5,9},{6,10},{7,11},{8,12},{9,13},{1... | collective-permute-start | bytes 1572872 | tf_op jit(solution)/shard_map/ppermute | solution.py:33
  132.5 8.0 %collective-permute-done.17 = f32[4,4,1,2,32,128]{5,4,3,1,0,2:T(8,128)S(1)} collective-permute-done((f32[4,4,1,2,32,128]{5,4,3,1,0,2:T(8,128)S(1)}, f32[4,4,1,2,32,128]{5,4,3,1,0,2:T(8,128)S(1)}, u32[]{:S(2)}, u32[]{:S(2)}) %collective-permute-start.17) | collective-permute-done | bytes 524320 | tf_op jit(solution)/shard_map/ppermute | solution.py:33
  162.1 7.1 %collective-permute-start.22 = (f32[1,2,32,128]{3,2,1,0:T(8,128)S(1)}, f32[1,2,32,128]{3,2,1,0:T(8,128)S(1)}, u32[]{:S(2)}, u32[]{:S(2)}) collective-permute-start(f32[1,2,32,128]{3,2,1,0:T(8,128)S(1)} %get-tuple-element.82), channel_id=1, source_target_pairs={{0,2},{1,3},{2,0},{3,1},{4,6},{5,7},{6,4},{7,5},{8,10},{9,11},{10,... | collective-permute-start | bytes 98312 | tf_op jit(solution)/shard_map/ppermute | solution.py:33
  195.2 5.6 %collective-permute-start.28 = (f32[4,4,1,2,32,128]{5,4,3,1,2,0:T(8,128)S(1)}, f32[4,4,1,2,32,128]{5,4,3,1,2,0:T(8,128)S(1)}, u32[]{:S(2)}, u32[]{:S(2)}) collective-permute-start(f32[4,4,1,2,32,128]{5,4,3,1,2,0:T(8,128)S(1)} %get-tuple-element.39), channel_id=1, source_target_pairs={{0,4},{1,5},{2,6},{3,7},{4,8},{5,9},{6,10},{7,11},{8,12},{9,13},{1... | collective-permute-start | bytes 1572872 | tf_op jit(solution)/shard_map/ppermute | solution.py:33
  200.9 5.2 %collective-permute-done.27 = f32[4,4,1,2,32,128]{5,4,3,1,0,2:T(8,128)S(1)} collective-permute-done((f32[4,4,1,2,32,128]{5,4,3,1,0,2:T(8,128)S(1)}, f32[4,4,1,2,32,128]{5,4,3,1,0,2:T(8,128)S(1)}, u32[]{:S(2)}, u32[]{:S(2)}) %collective-permute-start.27) | collective-permute-done | bytes 524320 | tf_op jit(solution)/shard_map/ppermute | solution.py:33
  208.1 5.3 %collective-permute-start.29 = (f32[2,4,1,2,32,128]{5,4,3,1,0,2:T(8,128)S(1)}, f32[2,4,1,2,32,128]{5,4,3,1,0,2:T(8,128)S(1)}, u32[]{:S(2)}, u32[]{:S(2)}) collective-permute-start(f32[2,4,1,2,32,128]{5,4,3,1,0,2:T(8,128)S(1)} %slice.242), channel_id=1, source_target_pairs={{0,4},{1,5},{2,6},{3,7},{4,8},{5,9},{6,10},{7,11},{8,12},{9,13},{1... | collective-permute-start | bytes 786440 | tf_op jit(solution)/shard_map/ppermute | solution.py:33
  227.7 5.4 %collective-permute-start.32 = (f32[1,2,32,128]{3,2,1,0:T(8,128)S(1)}, f32[1,2,32,128]{3,2,1,0:T(8,128)S(1)}, u32[]{:S(2)}, u32[]{:S(2)}) collective-permute-start(f32[1,2,32,128]{3,2,1,0:T(8,128)S(1)} %get-tuple-element.74), channel_id=1, source_target_pairs={{0,2},{1,3},{2,0},{3,1},{4,6},{5,7},{6,4},{7,5},{8,10},{9,11},{10,... | collective-permute-start | bytes 98312 | tf_op jit(solution)/shard_map/ppermute | solution.py:33
  233.1 6.6 %collective-permute-start.31 = (f32[1,2,32,128]{3,2,1,0:T(8,128)S(1)}, f32[1,2,32,128]{3,2,1,0:T(8,128)S(1)}, u32[]{:S(2)}, u32[]{:S(2)}) collective-permute-start(f32[1,2,32,128]{3,2,1,0:T(8,128)S(1)} %get-tuple-element.74), channel_id=1, source_target_pairs={{0,3},{1,0},{2,1},{3,2},{4,7},{5,4},{6,5},{7,6},{8,11},{9,8},{10,9... | collective-permute-start | bytes 98312 | tf_op jit(solution)/shard_map/ppermute | solution.py:33
  259.5 5.6 %collective-permute-start.38 = (f32[4,4,1,2,32,128]{5,4,3,1,2,0:T(8,128)S(1)}, f32[4,4,1,2,32,128]{5,4,3,1,2,0:T(8,128)S(1)}, u32[]{:S(2)}, u32[]{:S(2)}) collective-permute-start(f32[4,4,1,2,32,128]{5,4,3,1,2,0:T(8,128)S(1)} %get-tuple-element.36), channel_id=1, source_target_pairs={{0,4},{1,5},{2,6},{3,7},{4,8},{5,9},{6,10},{7,11},{8,12},{9,13},{1... | collective-permute-start | bytes 1572872 | tf_op jit(solution)/shard_map/ppermute | solution.py:33
  265.1 5.2 %collective-permute-done.37 = f32[4,4,1,2,32,128]{5,4,3,1,0,2:T(8,128)S(1)} collective-permute-done((f32[4,4,1,2,32,128]{5,4,3,1,0,2:T(8,128)S(1)}, f32[4,4,1,2,32,128]{5,4,3,1,0,2:T(8,128)S(1)}, u32[]{:S(2)}, u32[]{:S(2)}) %collective-permute-start.37) | collective-permute-done | bytes 524320 | tf_op jit(solution)/shard_map/ppermute | solution.py:33
  287.1 7.4 %collective-permute-start.43 = (f32[1,2,32,128]{3,2,1,0:T(8,128)S(1)}, f32[1,2,32,128]{3,2,1,0:T(8,128)S(1)}, u32[]{:S(2)}, u32[]{:S(2)}) collective-permute-start(f32[1,2,32,128]{3,2,1,0:T(8,128)S(1)} %get-tuple-element.80), channel_id=1, source_target_pairs={{0,1},{1,2},{2,3},{3,0},{4,5},{5,6},{6,7},{7,4},{8,9},{9,10},{10,1... | collective-permute-start | bytes 98312 | tf_op jit(solution)/shard_map/ppermute | solution.py:33
  294.5 5.6 %collective-permute-start.42 = (f32[1,2,32,128]{3,2,1,0:T(8,128)S(1)}, f32[1,2,32,128]{3,2,1,0:T(8,128)S(1)}, u32[]{:S(2)}, u32[]{:S(2)}) collective-permute-start(f32[1,2,32,128]{3,2,1,0:T(8,128)S(1)} %get-tuple-element.80), channel_id=1, source_target_pairs={{0,2},{1,3},{2,0},{3,1},{4,6},{5,7},{6,4},{7,5},{8,10},{9,11},{10,... | collective-permute-start | bytes 98312 | tf_op jit(solution)/shard_map/ppermute | solution.py:33
  300.1 6.1 %collective-permute-start.41 = (f32[1,2,32,128]{3,2,1,0:T(8,128)S(1)}, f32[1,2,32,128]{3,2,1,0:T(8,128)S(1)}, u32[]{:S(2)}, u32[]{:S(2)}) collective-permute-start(f32[1,2,32,128]{3,2,1,0:T(8,128)S(1)} %get-tuple-element.80), channel_id=1, source_target_pairs={{0,3},{1,0},{2,1},{3,2},{4,7},{5,4},{6,5},{7,6},{8,11},{9,8},{10,9... | collective-permute-start | bytes 98312 | tf_op jit(solution)/shard_map/ppermute | solution.py:33
  331.9 5.2 %collective-permute-done.47 = f32[4,4,1,2,32,128]{5,4,3,1,0,2:T(8,128)S(1)} collective-permute-done((f32[4,4,1,2,32,128]{5,4,3,1,0,2:T(8,128)S(1)}, f32[4,4,1,2,32,128]{5,4,3,1,0,2:T(8,128)S(1)}, u32[]{:S(2)}, u32[]{:S(2)}) %collective-permute-start.47) | collective-permute-done | bytes 524320 | tf_op jit(solution)/shard_map/ppermute | solution.py:33
  357.8 9.3 %collective-permute-start.52 = (f32[1,2,32,128]{3,2,1,0:T(8,128)S(1)}, f32[1,2,32,128]{3,2,1,0:T(8,128)S(1)}, u32[]{:S(2)}, u32[]{:S(2)}) collective-permute-start(f32[1,2,32,128]{3,2,1,0:T(8,128)S(1)} %get-tuple-element.72), channel_id=1, source_target_pairs={{0,2},{1,3},{2,0},{3,1},{4,6},{5,7},{6,4},{7,5},{8,10},{9,11},{10,... | collective-permute-start | bytes 98312 | tf_op jit(solution)/shard_map/ppermute | solution.py:33
  424.7 8.3 %collective-permute-start.62 = (f32[1,2,32,128]{3,2,1,0:T(8,128)S(1)}, f32[1,2,32,128]{3,2,1,0:T(8,128)S(1)}, u32[]{:S(2)}, u32[]{:S(2)}) collective-permute-start(f32[1,2,32,128]{3,2,1,0:T(8,128)S(1)} %get-tuple-element.78), channel_id=1, source_target_pairs={{0,2},{1,3},{2,0},{3,1},{4,6},{5,7},{6,4},{7,5},{8,10},{9,11},{10,... | collective-permute-start | bytes 98312 | tf_op jit(solution)/shard_map/ppermute | solution.py:33
  468.2 9.4 %collective-permute-done.67 = f32[4,4,1,2,32,128]{5,4,3,1,0,2:T(8,128)S(1)} collective-permute-done((f32[4,4,1,2,32,128]{5,4,3,1,0,2:T(8,128)S(1)}, f32[4,4,1,2,32,128]{5,4,3,1,0,2:T(8,128)S(1)}, u32[]{:S(2)}, u32[]{:S(2)}) %collective-permute-start.67) | collective-permute-done | bytes 524320 | tf_op jit(solution)/shard_map/ppermute | solution.py:33
  479.7 5.4 %collective-permute-start.69 = (f32[2,4,1,2,32,128]{5,4,3,1,0,2:T(8,128)S(1)}, f32[2,4,1,2,32,128]{5,4,3,1,0,2:T(8,128)S(1)}, u32[]{:S(2)}, u32[]{:S(2)}) collective-permute-start(f32[2,4,1,2,32,128]{5,4,3,1,0,2:T(8,128)S(1)} %slice.258), channel_id=1, source_target_pairs={{0,4},{1,5},{2,6},{3,7},{4,8},{5,9},{6,10},{7,11},{8,12},{9,13},{1... | collective-permute-start | bytes 786440 | tf_op jit(solution)/shard_map/ppermute | solution.py:33
  (243 shorter events, 331.5 us)
Async XLA Ops:
  8.4 25.5 %collective-permute-start.3 = (f32[1,2,32,128]{3,2,1,0:T(8,128)S(1)}, f32[1,2,32,128]{3,2,1,0:T(8,128)S(1)}, u32[]{:S(2)}, u32[]{:S(2)}) collective-permute-start(f32[1,2,32,128]{3,2,1,0:T(8,128)S(1)} %get-tuple-element.84), channel_id=1, source_target_pairs={{0,1},{1,2},{2,3},{3,0},{4,5},{5,6},{6,7},{7,4},{8,9},{9,10},{10,1... | collective-permute-start | bytes 98312 | tf_op jit(solution)/shard_map/ppermute | solution.py:33
  17.5 16.4 %collective-permute-start.2 = (f32[1,2,32,128]{3,2,1,0:T(8,128)S(1)}, f32[1,2,32,128]{3,2,1,0:T(8,128)S(1)}, u32[]{:S(2)}, u32[]{:S(2)}) collective-permute-start(f32[1,2,32,128]{3,2,1,0:T(8,128)S(1)} %get-tuple-element.84), channel_id=1, source_target_pairs={{0,2},{1,3},{2,0},{3,1},{4,6},{5,7},{6,4},{7,5},{8,10},{9,11},{10,... | collective-permute-start | bytes 98312 | tf_op jit(solution)/shard_map/ppermute | solution.py:33
  55.4 14.0 %collective-permute-start.7 = (f32[4,4,1,2,32,128]{5,4,3,1,0,2:T(8,128)}, f32[4,4,1,2,32,128]{5,4,3,1,0,2:T(8,128)S(1)}, u32[]{:S(2)}, u32[]{:S(2)}) collective-permute-start(f32[4,4,1,2,32,128]{5,4,3,1,0,2:T(8,128)} %get-tuple-element.46), channel_id=1, source_target_pairs={{0,12},{1,13},{2,14},{3,15},{4,0},{5,1},{6,2},{7,3},{8,4},{9,5},{1... | collective-permute-start | bytes 1572872 | tf_op jit(solution)/shard_map/ppermute | solution.py:33
  58.2 13.3 %collective-permute-start.8 = (f32[4,4,1,2,32,128]{5,4,3,1,2,0:T(8,128)S(1)}, f32[4,4,1,2,32,128]{5,4,3,1,2,0:T(8,128)S(1)}, u32[]{:S(2)}, u32[]{:S(2)}) collective-permute-start(f32[4,4,1,2,32,128]{5,4,3,1,2,0:T(8,128)S(1)} %get-tuple-element.47), channel_id=1, source_target_pairs={{0,4},{1,5},{2,6},{3,7},{4,8},{5,9},{6,10},{7,11},{8,12},{9,13},{1... | collective-permute-start | bytes 1572872 | tf_op jit(solution)/shard_map/ppermute | solution.py:33
  87.7 17.0 %collective-permute-start.13 = (f32[1,2,32,128]{3,2,1,0:T(8,128)S(1)}, f32[1,2,32,128]{3,2,1,0:T(8,128)S(1)}, u32[]{:S(2)}, u32[]{:S(2)}) collective-permute-start(f32[1,2,32,128]{3,2,1,0:T(8,128)S(1)} %get-tuple-element.76), channel_id=1, source_target_pairs={{0,1},{1,2},{2,3},{3,0},{4,5},{5,6},{6,7},{7,4},{8,9},{9,10},{10,1... | collective-permute-start | bytes 98312 | tf_op jit(solution)/shard_map/ppermute | solution.py:33
  90.9 14.8 %collective-permute-start.12 = (f32[1,2,32,128]{3,2,1,0:T(8,128)S(1)}, f32[1,2,32,128]{3,2,1,0:T(8,128)S(1)}, u32[]{:S(2)}, u32[]{:S(2)}) collective-permute-start(f32[1,2,32,128]{3,2,1,0:T(8,128)S(1)} %get-tuple-element.76), channel_id=1, source_target_pairs={{0,2},{1,3},{2,0},{3,1},{4,6},{5,7},{6,4},{7,5},{8,10},{9,11},{10,... | collective-permute-start | bytes 98312 | tf_op jit(solution)/shard_map/ppermute | solution.py:33
  125.0 15.6 %collective-permute-start.17 = (f32[4,4,1,2,32,128]{5,4,3,1,0,2:T(8,128)S(1)}, f32[4,4,1,2,32,128]{5,4,3,1,0,2:T(8,128)S(1)}, u32[]{:S(2)}, u32[]{:S(2)}) collective-permute-start(f32[4,4,1,2,32,128]{5,4,3,1,0,2:T(8,128)S(1)} %get-tuple-element.41), channel_id=1, source_target_pairs={{0,12},{1,13},{2,14},{3,15},{4,0},{5,1},{6,2},{7,3},{8,4},{9,5},{1... | collective-permute-start | bytes 1572872 | tf_op jit(solution)/shard_map/ppermute | solution.py:33
  126.9 15.6 %collective-permute-start.18 = (f32[4,4,1,2,32,128]{5,4,3,1,2,0:T(8,128)S(1)}, f32[4,4,1,2,32,128]{5,4,3,1,2,0:T(8,128)S(1)}, u32[]{:S(2)}, u32[]{:S(2)}) collective-permute-start(f32[4,4,1,2,32,128]{5,4,3,1,2,0:T(8,128)S(1)} %get-tuple-element.42), channel_id=1, source_target_pairs={{0,4},{1,5},{2,6},{3,7},{4,8},{5,9},{6,10},{7,11},{8,12},{9,13},{1... | collective-permute-start | bytes 1572872 | tf_op jit(solution)/shard_map/ppermute | solution.py:33
  157.4 15.3 %collective-permute-start.23 = (f32[1,2,32,128]{3,2,1,0:T(8,128)S(1)}, f32[1,2,32,128]{3,2,1,0:T(8,128)S(1)}, u32[]{:S(2)}, u32[]{:S(2)}) collective-permute-start(f32[1,2,32,128]{3,2,1,0:T(8,128)S(1)} %get-tuple-element.82), channel_id=1, source_target_pairs={{0,1},{1,2},{2,3},{3,0},{4,5},{5,6},{6,7},{7,4},{8,9},{9,10},{10,1... | collective-permute-start | bytes 98312 | tf_op jit(solution)/shard_map/ppermute | solution.py:33
  162.1 14.5 %collective-permute-start.22 = (f32[1,2,32,128]{3,2,1,0:T(8,128)S(1)}, f32[1,2,32,128]{3,2,1,0:T(8,128)S(1)}, u32[]{:S(2)}, u32[]{:S(2)}) collective-permute-start(f32[1,2,32,128]{3,2,1,0:T(8,128)S(1)} %get-tuple-element.82), channel_id=1, source_target_pairs={{0,2},{1,3},{2,0},{3,1},{4,6},{5,7},{6,4},{7,5},{8,10},{9,11},{10,... | collective-permute-start | bytes 98312 | tf_op jit(solution)/shard_map/ppermute | solution.py:33
  195.2 12.8 %collective-permute-start.28 = (f32[4,4,1,2,32,128]{5,4,3,1,2,0:T(8,128)S(1)}, f32[4,4,1,2,32,128]{5,4,3,1,2,0:T(8,128)S(1)}, u32[]{:S(2)}, u32[]{:S(2)}) collective-permute-start(f32[4,4,1,2,32,128]{5,4,3,1,2,0:T(8,128)S(1)} %get-tuple-element.39), channel_id=1, source_target_pairs={{0,4},{1,5},{2,6},{3,7},{4,8},{5,9},{6,10},{7,11},{8,12},{9,13},{1... | collective-permute-start | bytes 1572872 | tf_op jit(solution)/shard_map/ppermute | solution.py:33
  222.9 16.9 %collective-permute-start.33 = (f32[1,2,32,128]{3,2,1,0:T(8,128)S(1)}, f32[1,2,32,128]{3,2,1,0:T(8,128)S(1)}, u32[]{:S(2)}, u32[]{:S(2)}) collective-permute-start(f32[1,2,32,128]{3,2,1,0:T(8,128)S(1)} %get-tuple-element.74), channel_id=1, source_target_pairs={{0,1},{1,2},{2,3},{3,0},{4,5},{5,6},{6,7},{7,4},{8,9},{9,10},{10,1... | collective-permute-start | bytes 98312 | tf_op jit(solution)/shard_map/ppermute | solution.py:33
  227.7 14.8 %collective-permute-start.32 = (f32[1,2,32,128]{3,2,1,0:T(8,128)S(1)}, f32[1,2,32,128]{3,2,1,0:T(8,128)S(1)}, u32[]{:S(2)}, u32[]{:S(2)}) collective-permute-start(f32[1,2,32,128]{3,2,1,0:T(8,128)S(1)} %get-tuple-element.74), channel_id=1, source_target_pairs={{0,2},{1,3},{2,0},{3,1},{4,6},{5,7},{6,4},{7,5},{8,10},{9,11},{10,... | collective-permute-start | bytes 98312 | tf_op jit(solution)/shard_map/ppermute | solution.py:33
  259.5 12.8 %collective-permute-start.38 = (f32[4,4,1,2,32,128]{5,4,3,1,2,0:T(8,128)S(1)}, f32[4,4,1,2,32,128]{5,4,3,1,2,0:T(8,128)S(1)}, u32[]{:S(2)}, u32[]{:S(2)}) collective-permute-start(f32[4,4,1,2,32,128]{5,4,3,1,2,0:T(8,128)S(1)} %get-tuple-element.36), channel_id=1, source_target_pairs={{0,4},{1,5},{2,6},{3,7},{4,8},{5,9},{6,10},{7,11},{8,12},{9,13},{1... | collective-permute-start | bytes 1572872 | tf_op jit(solution)/shard_map/ppermute | solution.py:33
  287.1 19.1 %collective-permute-start.43 = (f32[1,2,32,128]{3,2,1,0:T(8,128)S(1)}, f32[1,2,32,128]{3,2,1,0:T(8,128)S(1)}, u32[]{:S(2)}, u32[]{:S(2)}) collective-permute-start(f32[1,2,32,128]{3,2,1,0:T(8,128)S(1)} %get-tuple-element.80), channel_id=1, source_target_pairs={{0,1},{1,2},{2,3},{3,0},{4,5},{5,6},{6,7},{7,4},{8,9},{9,10},{10,1... | collective-permute-start | bytes 98312 | tf_op jit(solution)/shard_map/ppermute | solution.py:33
  294.5 15.1 %collective-permute-start.42 = (f32[1,2,32,128]{3,2,1,0:T(8,128)S(1)}, f32[1,2,32,128]{3,2,1,0:T(8,128)S(1)}, u32[]{:S(2)}, u32[]{:S(2)}) collective-permute-start(f32[1,2,32,128]{3,2,1,0:T(8,128)S(1)} %get-tuple-element.80), channel_id=1, source_target_pairs={{0,2},{1,3},{2,0},{3,1},{4,6},{5,7},{6,4},{7,5},{8,10},{9,11},{10,... | collective-permute-start | bytes 98312 | tf_op jit(solution)/shard_map/ppermute | solution.py:33
  353.9 18.0 %collective-permute-start.53 = (f32[1,2,32,128]{3,2,1,0:T(8,128)S(1)}, f32[1,2,32,128]{3,2,1,0:T(8,128)S(1)}, u32[]{:S(2)}, u32[]{:S(2)}) collective-permute-start(f32[1,2,32,128]{3,2,1,0:T(8,128)S(1)} %get-tuple-element.72), channel_id=1, source_target_pairs={{0,1},{1,2},{2,3},{3,0},{4,5},{5,6},{6,7},{7,4},{8,9},{9,10},{10,1... | collective-permute-start | bytes 98312 | tf_op jit(solution)/shard_map/ppermute | solution.py:33
  357.8 14.6 %collective-permute-start.52 = (f32[1,2,32,128]{3,2,1,0:T(8,128)S(1)}, f32[1,2,32,128]{3,2,1,0:T(8,128)S(1)}, u32[]{:S(2)}, u32[]{:S(2)}) collective-permute-start(f32[1,2,32,128]{3,2,1,0:T(8,128)S(1)} %get-tuple-element.72), channel_id=1, source_target_pairs={{0,2},{1,3},{2,0},{3,1},{4,6},{5,7},{6,4},{7,5},{8,10},{9,11},{10,... | collective-permute-start | bytes 98312 | tf_op jit(solution)/shard_map/ppermute | solution.py:33
  411.2 41.5 %collective-permute-start.71 = (f32[96,2,2048]{2,1,0:T(2,128)}, f32[96,2,2048]{2,1,0:T(2,128)}, u32[]{:S(2)}, u32[]{:S(2)}) collective-permute-start(f32[96,2,2048]{2,1,0:T(2,128)} %bitcast.199), channel_id=1, source_target_pairs={{0,64},{64,0},{128,192},{192,128},{256,320},{320,256},{384,448},{4... | collective-permute-start | bytes 4718600 | tf_op jit(solution)/shard_map/ppermute | solution.py:10
  420.9 19.1 %collective-permute-start.63 = (f32[1,2,32,128]{3,2,1,0:T(8,128)S(1)}, f32[1,2,32,128]{3,2,1,0:T(8,128)S(1)}, u32[]{:S(2)}, u32[]{:S(2)}) collective-permute-start(f32[1,2,32,128]{3,2,1,0:T(8,128)S(1)} %get-tuple-element.78), channel_id=1, source_target_pairs={{0,1},{1,2},{2,3},{3,0},{4,5},{5,6},{6,7},{7,4},{8,9},{9,10},{10,1... | collective-permute-start | bytes 98312 | tf_op jit(solution)/shard_map/ppermute | solution.py:33
  424.7 15.3 %collective-permute-start.62 = (f32[1,2,32,128]{3,2,1,0:T(8,128)S(1)}, f32[1,2,32,128]{3,2,1,0:T(8,128)S(1)}, u32[]{:S(2)}, u32[]{:S(2)}) collective-permute-start(f32[1,2,32,128]{3,2,1,0:T(8,128)S(1)} %get-tuple-element.78), channel_id=1, source_target_pairs={{0,2},{1,3},{2,0},{3,1},{4,6},{5,7},{6,4},{7,5},{8,10},{9,11},{10,... | collective-permute-start | bytes 98312 | tf_op jit(solution)/shard_map/ppermute | solution.py:33
  443.4 15.3 %collective-permute-start.65 = (f32[4,1,2,32,128]{4,3,2,0,1:T(8,128)S(1)}, f32[4,1,2,32,128]{4,3,2,0,1:T(8,128)S(1)}, u32[]{:S(2)}, u32[]{:S(2)}) collective-permute-start(f32[4,1,2,32,128]{4,3,2,0,1:T(8,128)S(1)} %get-tuple-element.51), channel_id=1, source_target_pairs={{0,32},{1,33},{2,34},{3,35},{4,36},{5,37},{6,38},{7,39},{8,40},{9,... | collective-permute-start | bytes 393224 | tf_op jit(solution)/shard_map/ppermute | solution.py:33
  458.9 20.8 %collective-permute-start.68 = (f32[4,4,1,2,32,128]{5,4,3,1,2,0:T(8,128)S(1)}, f32[4,4,1,2,32,128]{5,4,3,1,2,0:T(8,128)S(1)}, u32[]{:S(2)}, u32[]{:S(2)}) collective-permute-start(f32[4,4,1,2,32,128]{5,4,3,1,2,0:T(8,128)S(1)} %get-tuple-element.27), channel_id=1, source_target_pairs={{0,4},{1,5},{2,6},{3,7},{4,8},{5,9},{6,10},{7,11},{8,12},{9,13},{1... | collective-permute-start | bytes 1572872 | tf_op jit(solution)/shard_map/ppermute | solution.py:33
  464.1 13.6 %collective-permute-start.67 = (f32[4,4,1,2,32,128]{5,4,3,1,0,2:T(8,128)S(1)}, f32[4,4,1,2,32,128]{5,4,3,1,0,2:T(8,128)S(1)}, u32[]{:S(2)}, u32[]{:S(2)}) collective-permute-start(f32[4,4,1,2,32,128]{5,4,3,1,0,2:T(8,128)S(1)} %get-tuple-element.26), channel_id=1, source_target_pairs={{0,12},{1,13},{2,14},{3,15},{4,0},{5,1},{6,2},{7,3},{8,4},{9,5},{1... | collective-permute-start | bytes 1572872 | tf_op jit(solution)/shard_map/ppermute | solution.py:33
  (54 other events, 532.9 us)
